TPU v7x, 512 devices: a whole 4x8x8 slice. The times are simulated.
512 devices in a mesh: exc: 8 (over y_lo, core), line: 64 (over z, x, y_hi).
Axes of the slice: x: 4, y: 8 (y_hi: 2, y_lo: 4; y = y_hi * 4 + y_lo), z: 8, core: 2. Of those that a mesh axis runs over, the one named last changes fastest.
Arguments:
- adj_e: float32 [3, 8, 1024, 1024], P(None, 'exc', 'line'), parts along dimension 1, may hold values from -6 to 6
- adj_h: float32 [3, 8, 1024, 1024], P(None, 'exc', 'line'), parts along dimension 1, may hold values from -6 to 6
- fwd_e: bfloat16 [2, 3, 8, 1024, 1024], P(None, None, 'exc', 'line'), parts along dimension 2, may hold values from -6 to 6
- permittivity: float32 [1, 1024, 1024], P(None, 'line'), may hold values from 1 to 6
- design_mask: int32 [1, 1024, 1024], P(None, 'line'), may hold values 0 or 1
- inverse: bfloat16 [1024, 1024], replicated, may hold values from -0.03125 to 0.6875
- omega: float32 [8], P('exc'), parts along dimension 0, may hold values from 0.3 to 2.5
- port_mode: float32 [8192], P('exc'), parts along dimension 0, may hold values from -6 to 6
- port_plane: int32 [8], P('exc'), parts along dimension 0, may hold values from 0 to 1023
Outputs:
- adj_e_out: float32 [3, 8, 1024, 1024], P(None, 'exc', 'line'), parts along dimension 1
- adj_h_out: float32 [3, 8, 1024, 1024], P(None, 'exc', 'line'), parts along dimension 1
- gradient: float32 [8, 1024, 1024], P('exc', 'line'), parts along dimension 0
There are 8 independent parts, one for each index of `exc`. A program takes and returns all parts, laid end to end along the dimension named above; an argument that names none is the same for every part. Nothing has to cross between parts.
All inputs are finite; a program needn't handle non-finite values. No bound on the sum of `design_mask` on one device may be relied on, other than what follows from the above.
Results may differ from a plain program's by a relative error of at most 0.005.
Values may be sent and summed in bfloat16 or wider, within the bound.
No kernel may reach another device: no remote copies, remote signals or barrier semaphores. Data moves between devices by JAX's collectives and lax.ppermute only.
A program may use at most 64 MiB of HBM per device.

v0:
```python
import jax
import jax.numpy as jnp
from jax import lax
from jax.sharding import PartitionSpec as P

COURANT = 0.4


def extended(array, sides, width):
    for axis, dim in sides:
        devices, length = (lax.axis_size(axis), array.shape[dim])
        up = [(i, (i + 1) % devices) for i in range(devices - 1)]
        down = [(j, i) for i, j in up]
        last = lax.slice_in_dim(array, length - width, length, axis=dim)
        first = lax.slice_in_dim(array, 0, width, axis=dim)
        before = lax.ppermute(last, axis, up)
        after = lax.ppermute(first, axis, down)
        array = jnp.concatenate([before, array, after], axis=dim)
    return array


def lower_diff(padded, along):
    inner = padded.shape[along] - 2
    middle = lax.slice_in_dim(padded, 1, inner + 1, axis=along)
    return middle - lax.slice_in_dim(padded, 0, inner, axis=along)


def upper_diff(padded, along):
    inner = padded.shape[along] - 2
    middle = lax.slice_in_dim(padded, 1, inner + 1, axis=along)
    return lax.slice_in_dim(padded, 2, inner + 2, axis=along) - middle


def zero_rim(stacked, along):
    widths = [(0, 0)] * stacked.ndim
    widths[along] = (1, 1)
    return jnp.pad(stacked, widths)


def row_rim(stacked, along):
    return extended(stacked, (("line", 2),), 1)


def column_rim(stacked, along):
    return extended(stacked, (("line", 2),), 1)


def curl_along_y(fields, inverse_eps, extend, along):
    electric_x, electric_y, electric_z = (fields[0], fields[1], fields[2])
    magnetic_x, magnetic_y, magnetic_z = (fields[3], fields[4], fields[5])
    scaled = COURANT * inverse_eps
    lower_terms = lower_diff(extend(jnp.stack([magnetic_x, magnetic_z]), along), along)
    electric_x = electric_x + scaled * lower_terms[1]
    electric_z = electric_z - scaled * lower_terms[0]
    upper_terms = upper_diff(extend(jnp.stack([electric_x, electric_z]), along), along)
    magnetic_x = magnetic_x - COURANT * upper_terms[1]
    magnetic_z = magnetic_z + COURANT * upper_terms[0]
    return jnp.stack([electric_x, electric_y, electric_z, magnetic_x, magnetic_y, magnetic_z])


def curl_along_xz(fields, inverse_eps, extend, along):
    electric_x, electric_y, electric_z = (fields[0], fields[1], fields[2])
    magnetic_x, magnetic_y, magnetic_z = (fields[3], fields[4], fields[5])
    scaled = COURANT * inverse_eps
    depth_terms = lower_diff(zero_rim(jnp.stack([magnetic_x, magnetic_y]), 1), 1)
    across = lower_diff(extend(jnp.stack([magnetic_y, magnetic_z]), along), along)
    electric_x = electric_x - scaled * depth_terms[1]
    electric_y = electric_y + scaled * (depth_terms[0] - across[1])
    electric_z = electric_z + scaled * across[0]
    depth_upper = upper_diff(zero_rim(jnp.stack([electric_x, electric_y]), 1), 1)
    across_upper = upper_diff(extend(jnp.stack([electric_y, electric_z]), along), along)
    magnetic_x = magnetic_x + COURANT * depth_upper[1]
    magnetic_y = magnetic_y + COURANT * (across_upper[1] - depth_upper[0])
    magnetic_z = magnetic_z - COURANT * across_upper[0]
    return jnp.stack([electric_x, electric_y, electric_z, magnetic_x, magnetic_y, magnetic_z])


def line_solve(rounded, inverse):
    flattened = rounded.reshape(-1, rounded.shape[-1])
    solved = lax.dot_general(
        flattened, inverse, (((1,), (1,)), ((), ())), preferred_element_type=jnp.float32
    )
    return solved.reshape(rounded.shape)


def fold_lines(field, line_count):
    strip_width = field.shape[-2]
    block = field.shape[-1] // line_count
    regrouped = field.reshape(field.shape[:-2] + (strip_width, line_count, block))
    regrouped = jnp.moveaxis(regrouped, -3, -1)
    return regrouped.reshape(field.shape[:-2] + (line_count, block * strip_width))


def unfold(received, block):
    line_count = received.shape[-2]
    strip_width = received.shape[-1] // block
    regrouped = received.reshape(received.shape[:-2] + (line_count, block, strip_width))
    regrouped = jnp.moveaxis(regrouped, -3, -2)
    return regrouped.reshape(received.shape[:-2] + (block, line_count * strip_width))


def accumulate(gradient, fields, snapshot, mask_weight, inverse_cols):
    forward = snapshot.astype(jnp.float32)
    intersection = fields[0] * forward[0] + fields[1] * forward[1] + fields[2] * forward[2]
    return gradient + mask_weight * intersection * (inverse_cols * inverse_cols)


def per_device(
    adj_e, adj_h, fwd_e, permittivity, design_mask, inverse, omega, port_mode, port_plane
):
    line_cells = inverse.shape[0]
    strip_width = adj_e.shape[2]
    step_count = fwd_e.shape[0]
    line_count = lax.axis_size("line")
    fields = jnp.concatenate([adj_e, adj_h], 0)
    inverse_rows = 1.0 / permittivity
    eps_turned = lax.all_to_all(
        fold_lines(permittivity, line_count), "line", split_axis=1, concat_axis=1, tiled=True
    )
    inverse_cols = 1.0 / unfold(eps_turned, strip_width)
    frequency = omega[0]
    plane_at = port_plane[0]
    offset = lax.axis_index("line") * strip_width
    column = (jnp.arange(line_cells, dtype=jnp.int32) == plane_at).astype(jnp.float32)
    profile_rows = lax.dynamic_slice_in_dim(port_mode, offset, strip_width)
    mask_weight = design_mask.astype(jnp.float32)
    gradient = jnp.zeros(permittivity.shape, jnp.float32)
    for instant in range(step_count):
        amplitude = jnp.cos(frequency * (instant + 1))
        fields = fields.at[2].add(amplitude * profile_rows[None, :, None] * column[None, None, :])
        fields = curl_along_y(fields, inverse_rows, row_rim, 2)
        fields = line_solve(fields.astype(jnp.bfloat16), inverse)
        turned = unfold(
            lax.all_to_all(
                fold_lines(fields, line_count), "line", split_axis=2, concat_axis=2, tiled=True
            ),
            strip_width,
        )
        turned = curl_along_xz(turned, inverse_cols, column_rim, 2)
        turned = line_solve(turned.astype(jnp.bfloat16), inverse)
        gradient = accumulate(gradient, turned, fwd_e[instant], mask_weight, inverse_cols)
        if instant + 1 < step_count:
            fields = unfold(
                lax.all_to_all(
                    fold_lines(turned, line_count), "line", split_axis=2, concat_axis=2, tiled=True
                ),
                strip_width,
            )
    return (turned[:3], turned[3:], gradient)


def solution(mesh):
    in_specs = (
        P(None, "exc", "line", None),
        P(None, "exc", "line", None),
        P(None, None, "exc", "line", None),
        P(None, "line", None),
        P(None, "line", None),
        P(),
        P("exc"),
        P("exc"),
        P("exc"),
    )
    out_specs = (P(None, "exc", "line", None), P(None, "exc", "line", None), P("exc", "line", None))
    return jax.shard_map(
        per_device, mesh=mesh, in_specs=in_specs, out_specs=out_specs, check_vma=False
    )
```

profile of v0, /device:TPU:54, one launch (start us, length us, event | category | flops | bytes accessed | tf_op | source)
XLA Modules:
  0.0 235.9 jit_solution(7053518898050523371)
XLA Ops:
  1.7 5.5 %collective-permute-start = (f32[2,1,1,1024]{3,2,1,0:T(1,128)S(1)}, f32[2,1,1,1024]{3,2,1,0:T(1,128)S(1)}, u32[]{:S(2)}, u32[]{:S(2)}) collective-permute-start(f32[2,1,1,1024]{3,2,1,0:T(1,128)S(1)} %fusion.77), channel_id=1, source_target_pairs={{0,1},{1,2},{2,3},{3,4},{4,5},{5,6},{6,7},{7,8},{8,9},{9,10},{10,1... | collective-permute-start | bytes 24584 | tf_op jit(solution)/shard_map/ppermute | solution.py:16
  14.8 4.7 %collective-permute-start.1 = (f32[2,1,1,1024]{3,2,1,0:T(1,128)S(1)}, f32[2,1,1,1024]{3,2,1,0:T(1,128)S(1)}, u32[]{:S(2)}, u32[]{:S(2)}) collective-permute-start(f32[2,1,1,1024]{3,2,1,0:T(1,128)S(1)} %fusion.76), channel_id=1, source_target_pairs={{1,0},{2,1},{3,2},{4,3},{5,4},{6,5},{7,6},{8,7},{9,8},{10,9},{11,1... | collective-permute-start | bytes 24584 | tf_op jit(solution)/shard_map/ppermute | solution.py:17
  21.5 19.4 %all-to-all-start.1 = ((f32[1,64,256]{2,0,1:T(1,128)}), f32[1,64,256]{2,0,1:T(1,128)S(1)}, u32[]{:S(2)}, u32[]{:S(2)}) async-start(f32[1,64,256]{2,0,1:T(1,128)} %copy.52), calls=%async_computation.1 | async-start | bytes 131072 | tf_op jit(solution)/shard_map/all_to_all | solution.py:117
  41.1 2.5 %fusion.2 = f32[6,16,64,16]{2,1,3,0:T(8,128)S(1)} fusion(bf16[64,16,1024]{2,1,0:T(8,128)(2,1)S(1)} %bitcast.246, bf16[6,16,1024]{2,1,0:T(8,128)(2,1)S(1)} %constant_dynamic-update-slice_fusion), kind=kOutput, calls=%fused_computation.2 | convolution fusion | flops 201326592 | bytes 2686976 | tf_op jit(solution)/shard_map/dot_general | solution.py:80
  44.7 4.3 %all-to-all-done.1 = f32[1,64,256]{2,0,1:T(1,128)S(1)} async-done(((f32[1,64,256]{2,0,1:T(1,128)}), f32[1,64,256]{2,0,1:T(1,128)S(1)}, u32[]{:S(2)}, u32[]{:S(2)}) %all-to-all-start.1) | async-done | bytes 65568 | tf_op jit(solution)/shard_map/all_to_all | solution.py:117
  49.0 11.0 %all-to-all-start = ((f32[6,1,64,256]{3,1,0,2:T(1,128)}), f32[6,1,64,256]{3,1,0,2:T(1,128)S(1)}, u32[]{:S(2)}, u32[]{:S(2)}) async-start(f32[6,1,64,256]{3,1,0,2:T(1,128)} %copy.48), calls=%async_computation | async-start | bytes 786432 | tf_op jit(solution)/shard_map/all_to_all | solution.py:134
  61.6 10.2 %all-to-all-done = f32[6,1,64,256]{3,1,0,2:T(1,128)S(1)} async-done(((f32[6,1,64,256]{3,1,0,2:T(1,128)}), f32[6,1,64,256]{3,1,0,2:T(1,128)S(1)}, u32[]{:S(2)}, u32[]{:S(2)}) %all-to-all-start) | async-done | bytes 393248 | tf_op jit(solution)/shard_map/all_to_all | solution.py:134
  74.4 1.9 copy.58
  79.7 8.7 %collective-permute-start.2 = (f32[2,1,1,1024]{3,2,1,0:T(1,128)}, f32[2,1,1,1024]{3,2,1,0:T(1,128)S(1)}, u32[]{:S(2)}, u32[]{:S(2)}) collective-permute-start(f32[2,1,1,1024]{3,2,1,0:T(1,128)} %slice.452), channel_id=1, source_target_pairs={{0,1},{1,2},{2,3},{3,4},{4,5},{5,6},{6,7},{7,8},{8,9},{9,10},{10,1... | collective-permute-start | bytes 24584 | tf_op jit(solution)/shard_map/ppermute | solution.py:16
  97.2 1.9 collective-permute-start.3
  99.1 10.5 %collective-permute-done.3 = f32[2,1,1,1024]{3,2,1,0:T(1,128)S(1)} collective-permute-done((f32[2,1,1,1024]{3,2,1,0:T(1,128)S(1)}, f32[2,1,1,1024]{3,2,1,0:T(1,128)S(1)}, u32[]{:S(2)}, u32[]{:S(2)}) %collective-permute-start.3) | collective-permute-done | bytes 8224 | tf_op jit(solution)/shard_map/ppermute | solution.py:17
  111.5 2.4 %fusion.93 = f32[96,1024]{1,0:T(8,128)} fusion(bf16[96,1024]{1,0:T(8,128)(2,1)} %bitcast.263, bf16[1024,1024]{1,0:T(8,128)(2,1)S(1)} %copy-done), kind=kOutput, calls=%fused_computation.185 | convolution fusion | flops 201326592 | bytes 2686976 | tf_op jit(solution)/shard_map/dot_general | solution.py:80
  114.0 2.1 reshape_reshape.2
  116.0 1.9 copy.63
  119.4 22.7 %all_to_all.20 = f32[6,1,64,256]{3,1,0,2:T(1,128)S(1)} all-to-all(f32[6,1,64,256]{3,1,0,2:T(1,128)S(1)} %copy.64), channel_id=1, replica_groups=mesh['exc'=8,'line'=64] {'line'}, dimensions={2} | all-to-all | bytes 786432 | tf_op jit(solution)/shard_map/all_to_all | solution.py:144
  143.7 6.9 %collective-permute-start.4 = (f32[2,1,1,1024]{3,2,1,0:T(1,128)S(1)}, f32[2,1,1,1024]{3,2,1,0:T(1,128)S(1)}, u32[]{:S(2)}, u32[]{:S(2)}) collective-permute-start(f32[2,1,1,1024]{3,2,1,0:T(1,128)S(1)} %slice.465), channel_id=1, source_target_pairs={{0,1},{1,2},{2,3},{3,4},{4,5},{5,6},{6,7},{7,8},{8,9},{9,10},{10,1... | collective-permute-start | bytes 24584 | tf_op jit(solution)/shard_map/ppermute | solution.py:16
  153.3 6.1 %collective-permute-start.5 = (f32[2,1,1,1024]{3,2,1,0:T(1,128)S(1)}, f32[2,1,1,1024]{3,2,1,0:T(1,128)S(1)}, u32[]{:S(2)}, u32[]{:S(2)}) collective-permute-start(f32[2,1,1,1024]{3,2,1,0:T(1,128)S(1)} %fusion.74), channel_id=1, source_target_pairs={{1,0},{2,1},{3,2},{4,3},{5,4},{6,5},{7,6},{8,7},{9,8},{10,9},{11,1... | collective-permute-start | bytes 24584 | tf_op jit(solution)/shard_map/ppermute | solution.py:17
  160.0 5.8 %collective-permute-done.5 = f32[2,1,1,1024]{3,2,1,0:T(1,128)S(1)} collective-permute-done((f32[2,1,1,1024]{3,2,1,0:T(1,128)S(1)}, f32[2,1,1,1024]{3,2,1,0:T(1,128)S(1)}, u32[]{:S(2)}, u32[]{:S(2)}) %collective-permute-start.5) | collective-permute-done | bytes 8224 | tf_op jit(solution)/shard_map/ppermute | solution.py:17
  165.9 2.5 %fusion = f32[6,16,64,16]{2,1,3,0:T(8,128)S(1)} fusion(bf16[64,16,1024]{2,1,0:T(8,128)(2,1)S(1)} %bitcast.247, bf16[6,16,1024]{2,1,0:T(8,128)(2,1)S(1)} %constant_dynamic-update-slice_fusion.16), kind=kOutput, calls=%fused_computation | convolution fusion | flops 201326592 | bytes 2686976 | tf_op jit(solution)/shard_map/dot_general | solution.py:80
  169.5 11.8 %all-to-all-start.3 = ((f32[6,1,64,256]{3,1,0,2:T(1,128)}), f32[6,1,64,256]{3,1,0,2:T(1,128)S(1)}, u32[]{:S(2)}, u32[]{:S(2)}) async-start(f32[6,1,64,256]{3,1,0,2:T(1,128)} %copy.73), calls=%async_computation.3 | async-start | bytes 786432 | tf_op jit(solution)/shard_map/all_to_all | solution.py:134
  185.0 7.4 %all-to-all-done.3 = f32[6,1,64,256]{3,1,0,2:T(1,128)S(1)} async-done(((f32[6,1,64,256]{3,1,0,2:T(1,128)}), f32[6,1,64,256]{3,1,0,2:T(1,128)S(1)}, u32[]{:S(2)}, u32[]{:S(2)}) %all-to-all-start.3) | async-done | bytes 393248 | tf_op jit(solution)/shard_map/all_to_all | solution.py:134
  199.6 7.0 %collective-permute-start.6 = (f32[2,1,1,1024]{3,2,1,0:T(1,128)S(1)}, f32[2,1,1,1024]{3,2,1,0:T(1,128)S(1)}, u32[]{:S(2)}, u32[]{:S(2)}) collective-permute-start(f32[2,1,1,1024]{3,2,1,0:T(1,128)S(1)} %slice.480), channel_id=1, source_target_pairs={{0,1},{1,2},{2,3},{3,4},{4,5},{5,6},{6,7},{7,8},{8,9},{9,10},{10,1... | collective-permute-start | bytes 24584 | tf_op jit(solution)/shard_map/ppermute | solution.py:16
  218.3 2.8 %collective-permute-start.7 = (f32[2,1,1,1024]{3,2,1,0:T(1,128)S(1)}, f32[2,1,1,1024]{3,2,1,0:T(1,128)S(1)}, u32[]{:S(2)}, u32[]{:S(2)}) collective-permute-start(f32[2,1,1,1024]{3,2,1,0:T(1,128)S(1)} %fusion.73), channel_id=1, source_target_pairs={{1,0},{2,1},{3,2},{4,3},{5,4},{6,5},{7,6},{8,7},{9,8},{10,9},{11,1... | collective-permute-start | bytes 24584 | tf_op jit(solution)/shard_map/ppermute | solution.py:17
  221.9 8.8 %collective-permute-done.7 = f32[2,1,1,1024]{3,2,1,0:T(1,128)S(1)} collective-permute-done((f32[2,1,1,1024]{3,2,1,0:T(1,128)S(1)}, f32[2,1,1,1024]{3,2,1,0:T(1,128)S(1)}, u32[]{:S(2)}, u32[]{:S(2)}) %collective-permute-start.7) | collective-permute-done | bytes 8224 | tf_op jit(solution)/shard_map/ppermute | solution.py:17
  (152 shorter events, 64.0 us)
Async XLA Ops:
  0.6 40.4 %copy-start.8 = (f32[3,1,16,1024]{3,2,1,0:T(8,128)S(1)}, f32[3,1,16,1024]{3,2,1,0:T(8,128)}, u32[]{:S(2)}) copy-start(f32[3,1,16,1024]{3,2,1,0:T(8,128)} %param.14) | copy-start | bytes 589828
  0.6 40.4 %copy-start = (bf16[1024,1024]{1,0:T(8,128)(2,1)S(1)}, bf16[1024,1024]{1,0:T(8,128)(2,1)}, u32[]{:S(2)}) copy-start(bf16[1024,1024]{1,0:T(8,128)(2,1)} %param.18) | copy-start | bytes 6291460
  1.7 9.5 %collective-permute-start = (f32[2,1,1,1024]{3,2,1,0:T(1,128)S(1)}, f32[2,1,1,1024]{3,2,1,0:T(1,128)S(1)}, u32[]{:S(2)}, u32[]{:S(2)}) collective-permute-start(f32[2,1,1,1024]{3,2,1,0:T(1,128)S(1)} %fusion.77), channel_id=1, source_target_pairs={{0,1},{1,2},{2,3},{3,4},{4,5},{5,6},{6,7},{7,8},{8,9},{9,10},{10,1... | collective-permute-start | bytes 24584 | tf_op jit(solution)/shard_map/ppermute | solution.py:16
  14.8 26.1 %collective-permute-start.1 = (f32[2,1,1,1024]{3,2,1,0:T(1,128)S(1)}, f32[2,1,1,1024]{3,2,1,0:T(1,128)S(1)}, u32[]{:S(2)}, u32[]{:S(2)}) collective-permute-start(f32[2,1,1,1024]{3,2,1,0:T(1,128)S(1)} %fusion.76), channel_id=1, source_target_pairs={{1,0},{2,1},{3,2},{4,3},{5,4},{6,5},{7,6},{8,7},{9,8},{10,9},{11,1... | collective-permute-start | bytes 24584 | tf_op jit(solution)/shard_map/ppermute | solution.py:17
  21.5 27.5 %all-to-all-start.1 = ((f32[1,64,256]{2,0,1:T(1,128)}), f32[1,64,256]{2,0,1:T(1,128)S(1)}, u32[]{:S(2)}, u32[]{:S(2)}) async-start(f32[1,64,256]{2,0,1:T(1,128)} %copy.52), calls=%async_computation.1 | async-start | bytes 131072 | tf_op jit(solution)/shard_map/all_to_all | solution.py:117
  49.0 22.8 %all-to-all-start = ((f32[6,1,64,256]{3,1,0,2:T(1,128)}), f32[6,1,64,256]{3,1,0,2:T(1,128)S(1)}, u32[]{:S(2)}, u32[]{:S(2)}) async-start(f32[6,1,64,256]{3,1,0,2:T(1,128)} %copy.48), calls=%async_computation | async-start | bytes 786432 | tf_op jit(solution)/shard_map/all_to_all | solution.py:134
  61.3 37.8 %copy-start.5 = (f32[1,16,1024]{2,1,0:T(8,128)}, f32[1,16,1024]{2,1,0:T(8,128)S(1)}, u32[]{:S(2)}) copy-start(f32[1,16,1024]{2,1,0:T(8,128)S(1)} %mul.346) | copy-start | bytes 196612
  79.7 16.2 %collective-permute-start.2 = (f32[2,1,1,1024]{3,2,1,0:T(1,128)}, f32[2,1,1,1024]{3,2,1,0:T(1,128)S(1)}, u32[]{:S(2)}, u32[]{:S(2)}) collective-permute-start(f32[2,1,1,1024]{3,2,1,0:T(1,128)} %slice.452), channel_id=1, source_target_pairs={{0,1},{1,2},{2,3},{3,4},{4,5},{5,6},{6,7},{7,8},{8,9},{9,10},{10,1... | collective-permute-start | bytes 24584 | tf_op jit(solution)/shard_map/ppermute | solution.py:16
  93.7 5.4 %copy-start.11 = (f32[1,16,1024]{2,1,0:T(8,128)S(1)}, f32[1,16,1024]{2,1,0:T(8,128)}, u32[]{:S(2)}) copy-start(f32[1,16,1024]{2,1,0:T(8,128)} %squeeze.52) | copy-start | bytes 196612
  93.7 5.4 %copy-start.12 = (f32[1,16,1024]{2,1,0:T(8,128)S(1)}, f32[1,16,1024]{2,1,0:T(8,128)}, u32[]{:S(2)}) copy-start(f32[1,16,1024]{2,1,0:T(8,128)} %stack.128) | copy-start | bytes 196612
  97.2 12.4 %collective-permute-start.3 = (f32[2,1,1,1024]{3,2,1,0:T(1,128)S(1)}, f32[2,1,1,1024]{3,2,1,0:T(1,128)S(1)}, u32[]{:S(2)}, u32[]{:S(2)}) collective-permute-start(f32[2,1,1,1024]{3,2,1,0:T(1,128)S(1)} %fusion.75), channel_id=1, source_target_pairs={{1,0},{2,1},{3,2},{4,3},{5,4},{6,5},{7,6},{8,7},{9,8},{10,9},{11,1... | collective-permute-start | bytes 24584 | tf_op jit(solution)/shard_map/ppermute | solution.py:17
  143.3 9.8 %copy-start.2 = (f32[1,16,1024]{2,1,0:T(8,128)S(1)}, f32[1,16,1024]{2,1,0:T(8,128)}, u32[]{:S(2)}) copy-start(f32[1,16,1024]{2,1,0:T(8,128)} %param.16) | copy-start | bytes 196612
  143.7 9.5 %collective-permute-start.4 = (f32[2,1,1,1024]{3,2,1,0:T(1,128)S(1)}, f32[2,1,1,1024]{3,2,1,0:T(1,128)S(1)}, u32[]{:S(2)}, u32[]{:S(2)}) collective-permute-start(f32[2,1,1,1024]{3,2,1,0:T(1,128)S(1)} %slice.465), channel_id=1, source_target_pairs={{0,1},{1,2},{2,3},{3,4},{4,5},{5,6},{6,7},{7,8},{8,9},{9,10},{10,1... | collective-permute-start | bytes 24584 | tf_op jit(solution)/shard_map/ppermute | solution.py:16
  151.3 14.6 %copy-start.1 = (bf16[1024,1024]{1,0:T(8,128)(2,1)S(1)}, bf16[1024,1024]{1,0:T(8,128)(2,1)}, u32[]{:S(2)}) copy-start(bf16[1024,1024]{1,0:T(8,128)(2,1)} %param.18) | copy-start | bytes 6291460
  153.3 12.5 %collective-permute-start.5 = (f32[2,1,1,1024]{3,2,1,0:T(1,128)S(1)}, f32[2,1,1,1024]{3,2,1,0:T(1,128)S(1)}, u32[]{:S(2)}, u32[]{:S(2)}) collective-permute-start(f32[2,1,1,1024]{3,2,1,0:T(1,128)S(1)} %fusion.74), channel_id=1, source_target_pairs={{1,0},{2,1},{3,2},{4,3},{5,4},{6,5},{7,6},{8,7},{9,8},{10,9},{11,1... | collective-permute-start | bytes 24584 | tf_op jit(solution)/shard_map/ppermute | solution.py:17
  169.5 22.9 %all-to-all-start.3 = ((f32[6,1,64,256]{3,1,0,2:T(1,128)}), f32[6,1,64,256]{3,1,0,2:T(1,128)S(1)}, u32[]{:S(2)}, u32[]{:S(2)}) async-start(f32[6,1,64,256]{3,1,0,2:T(1,128)} %copy.73), calls=%async_computation.3 | async-start | bytes 786432 | tf_op jit(solution)/shard_map/all_to_all | solution.py:134
  199.6 15.7 %collective-permute-start.6 = (f32[2,1,1,1024]{3,2,1,0:T(1,128)S(1)}, f32[2,1,1,1024]{3,2,1,0:T(1,128)S(1)}, u32[]{:S(2)}, u32[]{:S(2)}) collective-permute-start(f32[2,1,1,1024]{3,2,1,0:T(1,128)S(1)} %slice.480), channel_id=1, source_target_pairs={{0,1},{1,2},{2,3},{3,4},{4,5},{5,6},{6,7},{7,8},{8,9},{9,10},{10,1... | collective-permute-start | bytes 24584 | tf_op jit(solution)/shard_map/ppermute | solution.py:16
  210.7 4.6 %copy-start.10 = (f32[2,1,16,1024]{3,2,1,0:T(8,128)S(1)}, f32[2,1,16,1024]{3,2,1,0:T(8,128)}, u32[]{:S(2)}) copy-start(f32[2,1,16,1024]{3,2,1,0:T(8,128)} %constant_dynamic-update-slice_fusion.22) | copy-start | bytes 393220
  211.9 9.2 %copy-start.6 = (f32[1,16,1024]{2,1,0:T(8,128)S(1)}, f32[1,16,1024]{2,1,0:T(8,128)}, u32[]{:S(2)}) copy-start(f32[1,16,1024]{2,1,0:T(8,128)} %copy-done.5) | copy-start | bytes 196612
  218.3 12.4 %collective-permute-start.7 = (f32[2,1,1,1024]{3,2,1,0:T(1,128)S(1)}, f32[2,1,1,1024]{3,2,1,0:T(1,128)S(1)}, u32[]{:S(2)}, u32[]{:S(2)}) collective-permute-start(f32[2,1,1,1024]{3,2,1,0:T(1,128)S(1)} %fusion.73), channel_id=1, source_target_pairs={{1,0},{2,1},{3,2},{4,3},{5,4},{6,5},{7,6},{8,7},{9,8},{10,9},{11,1... | collective-permute-start | bytes 24584 | tf_op jit(solution)/shard_map/ppermute | solution.py:17
  230.8 4.4 %copy-start.3 = (f32[96,1024]{1,0:T(8,128)S(1)}, f32[96,1024]{1,0:T(8,128)}, u32[]{:S(2)}) copy-start(f32[96,1024]{1,0:T(8,128)} %fusion.93) | copy-start | bytes 1179652
  230.8 4.4 %copy-start.4 = (f32[1,3,1,16,1024]{4,3,2,1,0:T(8,128)S(1)}, f32[1,3,1,16,1024]{4,3,2,1,0:T(8,128)}, u32[]{:S(2)}) copy-start(f32[1,3,1,16,1024]{4,3,2,1,0:T(8,128)} %get-tuple-element.69) | copy-start | bytes 589828
  230.8 4.4 %copy-start.13 = (f32[1,16,1024]{2,1,0:T(8,128)S(1)}, f32[1,16,1024]{2,1,0:T(8,128)}, u32[]{:S(2)}) copy-start(f32[1,16,1024]{2,1,0:T(8,128)} %mul.375) | copy-start | bytes 196612
  230.8 4.4 %copy-start.14 = (s32[1,16,1024]{2,1,0:T(8,128)S(1)}, s32[1,16,1024]{2,1,0:T(8,128)}, u32[]{:S(2)}) copy-start(s32[1,16,1024]{2,1,0:T(8,128)} %param.17) | copy-start | bytes 196612
  (2 other events, 6.8 us)
where the time goes:
time: 237 us; the launch traced here: 236 us
  starting transfers between devices  86 us (36%)
  waiting for transfers between devices  49.7 us (21%)
  local copies, waits for them, and re-layouts  46.7 us (20%)
  blocking collectives  22.7 us (10%)
  other arithmetic  18.8 us (8%)
  matrix products  9.19 us (4%)
  between operations  2.78 us (1%)
    ppermute x4, starting transfers between devices, extended(): before = lax.ppermute(last, axis, up)  28.2 us
    ppermute x4, waiting for transfers between devices, extended(): after = lax.ppermute(first, axis, down)  25.1 us
    all_to_all x2, starting transfers between devices, per_device(): lax.all_to_all(fold_lines(fields, line_count), 'line', split_axis=2, conc...  22.8 us
    all_to_all x1, blocking collectives, per_device(): lax.all_to_all(fold_lines(turned, line_count), 'line', split_axis=2, conc...  22.7 us
    all_to_all x1, starting transfers between devices, per_device(): lax.all_to_all(fold_lines(permittivity, line_count), 'line', split_axis=1...  19.4 us
    all_to_all x2, waiting for transfers between devices, per_device(): lax.all_to_all(fold_lines(fields, line_count), 'line', split_axis=2, conc...  17.6 us
    ppermute x4, starting transfers between devices, extended(): after = lax.ppermute(first, axis, down)  15.5 us
    unnamed x16, other arithmetic  11.6 us
  transfers between devices with their start and end apart: 11, of which 8 were waited for; matrix products, arithmetic and copies ran while one was open for 13% of the time, Pallas kernels for 0%

commit v1 on v0

v1 whole, which is shorter than its diff:
```python
import jax
import jax.numpy as jnp
from jax import lax
from jax.sharding import PartitionSpec as P

COURANT = 0.4


def line_solve(rounded, inverse):
    flattened = rounded.reshape(-1, rounded.shape[-1])
    solved = lax.dot_general(
        flattened, inverse, (((1,), (1,)), ((), ())), preferred_element_type=jnp.float32
    )
    return solved.reshape(rounded.shape)


def turn(block, line_count):
    strip = block.shape[-2]
    lead = block.shape[:-2]
    n = len(lead)
    parts = block.reshape(lead + (strip, line_count, strip))
    parts = jnp.moveaxis(parts, n + 1, 0)
    parts = lax.all_to_all(parts, "line", 0, 0, tiled=True)
    order = tuple(range(1, n + 1)) + (n + 2, 0, n + 1)
    parts = jnp.transpose(parts, order)
    return parts.reshape(lead + (strip, line_count * strip))


def shift_down(f, along, first):
    inner = f.shape[along]
    return jnp.concatenate([first, lax.slice_in_dim(f, 0, inner - 1, axis=along)], axis=along)


def shift_up(f, along, last):
    inner = f.shape[along]
    return jnp.concatenate([lax.slice_in_dim(f, 1, inner, axis=along), last], axis=along)


def zeros_like_slice(f, along):
    shape = list(f.shape)
    shape[along] = 1
    return jnp.zeros(shape, f.dtype)


def curl_y(fields, scaled, along, below=None, above=None):
    ex, ey, ez, hx, hy, hz = fields
    if below is None:
        below = (zeros_like_slice(hx, along), zeros_like_slice(hz, along))
    if above is None:
        z = zeros_like_slice(hx, along)
        above = (z, z, z, z, z)
    hx_prev = shift_down(hx, along, below[0])
    hz_prev = shift_down(hz, along, below[1])
    ex = ex + scaled * (hz - hz_prev)
    ez = ez - scaled * (hx - hx_prev)
    last = lax.slice_in_dim(hx, hx.shape[along] - 1, hx.shape[along], axis=along)
    last_z = lax.slice_in_dim(hz, hz.shape[along] - 1, hz.shape[along], axis=along)
    ex_a, ez_a, hx_a, hz_a, scaled_a = above
    ex_next_edge = ex_a + scaled_a * (hz_a - last_z)
    ez_next_edge = ez_a - scaled_a * (hx_a - last)
    ex_next = shift_up(ex, along, ex_next_edge)
    ez_next = shift_up(ez, along, ez_next_edge)
    hx = hx - COURANT * (ez_next - ez)
    hz = hz + COURANT * (ex_next - ex)
    return (ex, ey, ez, hx, hy, hz)


def curl_xz(fields, scaled, along_x, along_z):
    ex, ey, ez, hx, hy, hz = fields

    def lower(f, along):
        return f - shift_down(f, along, zeros_like_slice(f, along))

    def upper(f, along):
        return shift_up(f, along, zeros_like_slice(f, along)) - f

    ex = ex - scaled * lower(hy, along_z)
    ey = ey + scaled * (lower(hx, along_z) - lower(hz, along_x))
    ez = ez + scaled * lower(hy, along_x)
    hx = hx + COURANT * upper(ey, along_z)
    hy = hy + COURANT * (upper(ez, along_x) - upper(ex, along_z))
    hz = hz - COURANT * upper(ey, along_x)
    return (ex, ey, ez, hx, hy, hz)


def per_device(
    adj_e, adj_h, fwd_e, permittivity, design_mask, inverse, omega, port_mode, port_plane
):
    line_cells = inverse.shape[0]
    strip = adj_e.shape[2]
    step_count = fwd_e.shape[0]
    line_count = lax.axis_size("line")
    index = lax.axis_index("line")
    offset = index * strip
    inverse_rows = 1.0 / permittivity
    inverse_cols = turn(inverse_rows, line_count)
    scaled_rows = COURANT * inverse_rows
    scaled_cols = COURANT * inverse_cols
    frequency = omega[0]
    plane_at = port_plane[0]
    mask_weight = design_mask.astype(jnp.float32)
    gradient = jnp.zeros(design_mask.shape, jnp.float32)

    fields = tuple(adj_e[i] for i in range(3)) + tuple(adj_h[i] for i in range(3))
    column = (jnp.arange(line_cells, dtype=jnp.int32) == plane_at).astype(jnp.float32)
    profile_rows = lax.dynamic_slice_in_dim(port_mode, offset, strip)
    amplitude = jnp.cos(frequency * 1.0)
    ex, ey, ez, hx, hy, hz = fields
    ez = ez + (amplitude * profile_rows[None, :, None]) * column[None, None, :]
    fields = (ex, ey, ez, hx, hy, hz)
    rows_along = 1
    up = [(i, i + 1) for i in range(line_count - 1)]
    down = [(i + 1, i) for i in range(line_count - 1)]
    last_rows = jnp.stack([hx[:, -1:], hz[:, -1:]])
    first_rows = jnp.stack(
        [ex[:, :1], ez[:, :1], hx[:, :1], hz[:, :1], scaled_rows[:, :1]]
    )
    below = lax.ppermute(last_rows, "line", up)
    above = lax.ppermute(first_rows, "line", down)
    fields = curl_y(
        fields,
        scaled_rows,
        rows_along,
        below=(below[0], below[1]),
        above=tuple(above[i] for i in range(5)),
    )
    for instant in range(step_count):
        if instant > 0:
            amplitude = jnp.cos(frequency * (instant + 1))
            x_local = offset + jnp.arange(strip, dtype=jnp.int32)
            column_local = (x_local == plane_at).astype(jnp.float32)
            ex, ey, ez, hx, hy, hz = fields
            ez = ez + (amplitude * column_local[None, :, None]) * port_mode[None, None, :]
            fields = curl_y((ex, ey, ez, hx, hy, hz), scaled_cols, 2)
            rounded = jnp.stack(fields).astype(jnp.bfloat16)
            rounded = turn(rounded, line_count)
        else:
            rounded = jnp.stack(fields).astype(jnp.bfloat16)
        solved = line_solve(rounded, inverse)
        fields = tuple(solved[i] for i in range(6))
        fields = curl_xz(fields, scaled_rows, 2, 0)
        rounded = jnp.stack(fields).astype(jnp.bfloat16)
        rounded = turn(rounded, line_count)
        solved = line_solve(rounded, inverse)
        fields = tuple(solved[i] for i in range(6))
        snapshot = fwd_e[instant].astype(jnp.float32)
        intersection = fields[0] * snapshot[0] + fields[1] * snapshot[1] + fields[2] * snapshot[2]
        gradient = gradient + mask_weight * intersection * (inverse_cols * inverse_cols)
    out = jnp.stack(fields)
    return (out[:3], out[3:], gradient)


def solution(mesh):
    in_specs = (
        P(None, "exc", "line", None),
        P(None, "exc", "line", None),
        P(None, None, "exc", "line", None),
        P(None, "line", None),
        P(None, "line", None),
        P(),
        P("exc"),
        P("exc"),
        P("exc"),
    )
    out_specs = (P(None, "exc", "line", None), P(None, "exc", "line", None), P("exc", "line", None))
    return jax.shard_map(
        per_device, mesh=mesh, in_specs=in_specs, out_specs=out_specs, check_vma=False
    )
```

time: 237 us -> 218 us (0.920)
  the two profiles are of different devices: /device:TPU:54 before, /device:TPU:8 now
where the time goes in v1:
time: 218 us; the launch traced here: 216 us
  local copies, waits for them, and re-layouts  95.9 us (44%)
  starting transfers between devices  46.9 us (22%)
  waiting for transfers between devices  31.8 us (15%)
  blocking collectives  20.8 us (10%)
  other arithmetic  14.1 us (6%)
  matrix products  4.03 us (2%)
  between operations  2.54 us (1%)
    all_to_all x3, starting transfers between devices, turn(): parts = lax.all_to_all(parts, 'line', 0, 0, tiled=True)  38.8 us
    unnamed x53, local copies, waits for them, and re-layouts  36.4 us
    all_to_all x3, waiting for transfers between devices, turn(): parts = lax.all_to_all(parts, 'line', 0, 0, tiled=True)  23.5 us
    all_to_all x1, blocking collectives, turn(): parts = lax.all_to_all(parts, 'line', 0, 0, tiled=True)  20.8 us
    another operation x21, local copies, waits for them, and re-layouts, per_device(): rounded = jnp.stack(fields).astype(jnp.bfloat16)  17.1 us
    transpose x3, local copies, waits for them, and re-layouts, turn(): parts = jnp.transpose(parts, order)  13.2 us
    transpose x4, local copies, waits for them, and re-layouts, turn(): parts = jnp.moveaxis(parts, n + 1, 0)  11.8 us
    another operation x3, local copies, waits for them, and re-layouts, line_solve(): flattened = rounded.reshape(-1, rounded.shape[-1])  11.6 us
  transfers between devices with their start and end apart: 5, of which 4 were waited for; matrix products, arithmetic and copies ran while one was open for 11% of the time, Pallas kernels for 0%

profile of v1, /device:TPU:8, one launch (start us, length us, event | category | flops | bytes accessed | tf_op | source)
XLA Modules:
  0.0 216.0 jit_solution(15286583436862368396)
XLA Ops:
  1.7 6.8 %collective-permute-start = (f32[2,1,1,1024]{3,2,1,0:T(1,128)S(1)}, f32[2,1,1,1024]{3,2,1,0:T(1,128)S(1)}, u32[]{:S(2)}, u32[]{:S(2)}) collective-permute-start(f32[2,1,1,1024]{3,2,1,0:T(1,128)S(1)} %pad_maximum_fusion.2), channel_id=1, source_target_pairs={{0,1},{1,2},{2,3},{3,4},{4,5},{5,6},{6,7},{7,8},{8,9},{9,10},{10,1... | collective-permute-start | bytes 24584 | tf_op jit(solution)/shard_map/ppermute | solution.py:118
  16.6 8.3 %collective-permute-done.1 = f32[5,1,1,1024]{3,2,1,0:T(1,128)S(1)} collective-permute-done((f32[5,1,1,1024]{3,2,1,0:T(1,128)S(1)}, f32[5,1,1,1024]{3,2,1,0:T(1,128)S(1)}, u32[]{:S(2)}, u32[]{:S(2)}) %collective-permute-start.1) | collective-permute-done | bytes 20512 | tf_op jit(solution)/shard_map/ppermute | solution.py:119
  29.1 19.6 %all-to-all-start.1 = ((f32[64,1,256]{2,1,0:T(1,128)}), f32[64,1,256]{2,1,0:T(1,128)S(1)}, u32[]{:S(2)}, u32[]{:S(2)}) async-start(f32[64,1,256]{2,1,0:T(1,128)} %reshape.691), calls=%async_computation.1 | async-start | bytes 131072 | tf_op jit(solution)/shard_map/all_to_all | solution.py:23
  54.7 3.6 %copy.45 = bf16[64,6,1,16,16]{4,3,2,1,0:T(8,128)(2,1)} copy(bf16[64,6,1,16,16]{4,0,3,2,1:T(8,128)(2,1)} %bitcast.313) | data formatting | bytes 393216 | tf_op jit(solution)/shard_map/transpose | solution.py:22
  58.3 3.6 %reshape.693 = bf16[64,2,768]{2,1,0:T(2,128)(2,1)} reshape(bf16[64,6,1,16,16]{4,3,2,1,0:T(8,128)(2,1)} %copy.45) | data formatting | bytes 393216
  63.2 14.0 %all-to-all-start = ((bf16[64,2,768]{2,1,0:T(2,128)(2,1)}), bf16[64,2,768]{2,1,0:T(2,128)(2,1)S(1)}, u32[]{:S(2)}, u32[]{:S(2)}) async-start(bf16[64,2,768]{2,1,0:T(2,128)(2,1)} %reshape.693), calls=%async_computation | async-start | bytes 393216 | tf_op jit(solution)/shard_map/all_to_all | solution.py:23
  80.0 1.9 broadcast_multiply_fusion
  83.1 8.8 %all-to-all-done = bf16[64,2,768]{2,1,0:T(2,128)(2,1)S(1)} async-done(((bf16[64,2,768]{2,1,0:T(2,128)(2,1)}), bf16[64,2,768]{2,1,0:T(2,128)(2,1)S(1)}, u32[]{:S(2)}, u32[]{:S(2)}) %all-to-all-start) | async-done | bytes 196640 | tf_op jit(solution)/shard_map/all_to_all | solution.py:23
  92.0 2.3 %reshape.694 = bf16[64,6,1,16,16]{4,3,2,1,0:T(8,128)(2,1)} reshape(bf16[64,2,768]{2,1,0:T(2,128)(2,1)S(1)} %all-to-all-done) | data formatting | bytes 393216
  94.3 4.4 %copy.46 = bf16[6,1,16,64,16]{4,3,2,0,1:T(8,128)(2,1)} copy(bf16[6,1,16,64,16]{2,4,1,0,3:T(8,128)(2,1)} %bitcast.309) | data formatting | bytes 393216 | tf_op jit(solution)/shard_map/transpose | solution.py:25
  98.7 3.7 %reshape_reshape.9 = bf16[96,1024]{1,0:T(8,128)(2,1)S(1)} reshape(bf16[6,1,16,64,16]{4,3,2,0,1:T(8,128)(2,1)} %copy.46) | data formatting | bytes 393216 | tf_op jit(solution)/shard_map/reshape;reshape | solution.py:10
  116.9 3.6 %copy.49 = bf16[64,6,1,16,16]{4,3,2,1,0:T(8,128)(2,1)} copy(bf16[64,6,1,16,16]{4,0,3,2,1:T(8,128)(2,1)} %bitcast.314) | data formatting | bytes 393216 | tf_op jit(solution)/shard_map/transpose | solution.py:22
  120.5 2.9 %reshape.695 = bf16[64,2,768]{2,1,0:T(2,128)(2,1)S(1)} reshape(bf16[64,6,1,16,16]{4,3,2,1,0:T(8,128)(2,1)} %copy.49) | data formatting | bytes 393216
  123.5 20.8 %all_to_all.20 = bf16[64,2,768]{2,1,0:T(2,128)(2,1)S(1)} all-to-all(bf16[64,2,768]{2,1,0:T(2,128)(2,1)S(1)} %reshape.695), channel_id=1, replica_groups=mesh['exc'=8,'line'=64] {'line'}, dimensions={0} | all-to-all | bytes 393216 | tf_op jit(solution)/shard_map/all_to_all | solution.py:23
  144.3 2.3 %reshape.696 = bf16[64,6,1,16,16]{4,3,2,1,0:T(8,128)(2,1)} reshape(bf16[64,2,768]{2,1,0:T(2,128)(2,1)S(1)} %all_to_all.20) | data formatting | bytes 393216
  146.6 4.4 %copy.50 = bf16[6,1,16,64,16]{4,3,2,0,1:T(8,128)(2,1)} copy(bf16[6,1,16,64,16]{2,4,1,0,3:T(8,128)(2,1)} %bitcast.310) | data formatting | bytes 393216 | tf_op jit(solution)/shard_map/transpose | solution.py:25
  151.0 4.3 %reshape_reshape.10 = bf16[96,1024]{1,0:T(8,128)(2,1)} reshape(bf16[6,1,16,64,16]{4,3,2,0,1:T(8,128)(2,1)} %copy.50) | data formatting | bytes 393216 | tf_op jit(solution)/shard_map/reshape;reshape | solution.py:10
  175.2 3.6 %copy.51 = bf16[64,6,1,16,16]{4,3,2,1,0:T(8,128)(2,1)} copy(bf16[64,6,1,16,16]{4,0,3,2,1:T(8,128)(2,1)} %bitcast.312) | data formatting | bytes 393216 | tf_op jit(solution)/shard_map/transpose | solution.py:22
  178.8 3.6 %reshape.697 = bf16[64,2,768]{2,1,0:T(2,128)(2,1)} reshape(bf16[64,6,1,16,16]{4,3,2,1,0:T(8,128)(2,1)} %copy.51) | data formatting | bytes 393216
  182.3 5.2 %all-to-all-start.3 = ((bf16[64,2,768]{2,1,0:T(2,128)(2,1)}), bf16[64,2,768]{2,1,0:T(2,128)(2,1)S(1)}, u32[]{:S(2)}, u32[]{:S(2)}) async-start(bf16[64,2,768]{2,1,0:T(2,128)(2,1)} %reshape.697), calls=%async_computation.3 | async-start | bytes 393216 | tf_op jit(solution)/shard_map/all_to_all | solution.py:23
  189.4 13.4 %all-to-all-done.3 = bf16[64,2,768]{2,1,0:T(2,128)(2,1)S(1)} async-done(((bf16[64,2,768]{2,1,0:T(2,128)(2,1)}), bf16[64,2,768]{2,1,0:T(2,128)(2,1)S(1)}, u32[]{:S(2)}, u32[]{:S(2)}) %all-to-all-start.3) | async-done | bytes 196640 | tf_op jit(solution)/shard_map/all_to_all | solution.py:23
  202.7 2.3 %reshape.698 = bf16[64,6,1,16,16]{4,3,2,1,0:T(8,128)(2,1)} reshape(bf16[64,2,768]{2,1,0:T(2,128)(2,1)S(1)} %all-to-all-done.3) | data formatting | bytes 393216
  205.0 4.4 %copy.52 = bf16[6,1,16,64,16]{4,3,2,0,1:T(8,128)(2,1)} copy(bf16[6,1,16,64,16]{2,4,1,0,3:T(8,128)(2,1)} %bitcast.311) | data formatting | bytes 393216 | tf_op jit(solution)/shard_map/transpose | solution.py:25
  209.4 3.7 %reshape_reshape.11 = bf16[96,1024]{1,0:T(8,128)(2,1)S(1)} reshape(bf16[6,1,16,64,16]{4,3,2,0,1:T(8,128)(2,1)} %copy.52) | data formatting | bytes 393216 | tf_op jit(solution)/shard_map/reshape;reshape | solution.py:10
  (123 shorter events, 62.1 us)
Async XLA Ops:
  0.6 24.4 %copy-start = (bf16[1024,1024]{1,0:T(8,128)(2,1)S(1)}, bf16[1024,1024]{1,0:T(8,128)(2,1)}, u32[]{:S(2)}) copy-start(bf16[1024,1024]{1,0:T(8,128)(2,1)} %param.14) | copy-start | bytes 6291460
  0.6 24.3 %copy-start.6 = (f32[3,1,16,1024]{3,2,1,0:T(8,128)S(1)}, f32[3,1,16,1024]{3,2,1,0:T(8,128)}, u32[]{:S(2)}) copy-start(f32[3,1,16,1024]{3,2,1,0:T(8,128)} %param.10) | copy-start | bytes 589828
  1.7 10.7 %collective-permute-start = (f32[2,1,1,1024]{3,2,1,0:T(1,128)S(1)}, f32[2,1,1,1024]{3,2,1,0:T(1,128)S(1)}, u32[]{:S(2)}, u32[]{:S(2)}) collective-permute-start(f32[2,1,1,1024]{3,2,1,0:T(1,128)S(1)} %pad_maximum_fusion.2), channel_id=1, source_target_pairs={{0,1},{1,2},{2,3},{3,4},{4,5},{5,6},{6,7},{7,8},{8,9},{9,10},{10,1... | collective-permute-start | bytes 24584 | tf_op jit(solution)/shard_map/ppermute | solution.py:118
  15.3 9.6 %collective-permute-start.1 = (f32[5,1,1,1024]{3,2,1,0:T(1,128)S(1)}, f32[5,1,1,1024]{3,2,1,0:T(1,128)S(1)}, u32[]{:S(2)}, u32[]{:S(2)}) collective-permute-start(f32[5,1,1,1024]{3,2,1,0:T(1,128)S(1)} %constant_dynamic-update-slice_fusion), channel_id=1, source_target_pairs={{1,0},{2,1},{3,2},{4,3},{5,4},{6,5},{7,6},{8,7},{9,8},{10,9},{11,1... | collective-permute-start | bytes 61448 | tf_op jit(solution)/shard_map/ppermute | solution.py:119
  24.9 0.9 copy-start.1
  29.1 34.0 %all-to-all-start.1 = ((f32[64,1,256]{2,1,0:T(1,128)}), f32[64,1,256]{2,1,0:T(1,128)S(1)}, u32[]{:S(2)}, u32[]{:S(2)}) async-start(f32[64,1,256]{2,1,0:T(1,128)} %reshape.691), calls=%async_computation.1 | async-start | bytes 131072 | tf_op jit(solution)/shard_map/all_to_all | solution.py:23
  63.2 28.8 %all-to-all-start = ((bf16[64,2,768]{2,1,0:T(2,128)(2,1)}), bf16[64,2,768]{2,1,0:T(2,128)(2,1)S(1)}, u32[]{:S(2)}, u32[]{:S(2)}) async-start(bf16[64,2,768]{2,1,0:T(2,128)(2,1)} %reshape.693), calls=%async_computation | async-start | bytes 393216 | tf_op jit(solution)/shard_map/all_to_all | solution.py:23
  102.4 1.6 copy-start.10
  102.4 1.6 copy-start.11
  104.4 5.2 %copy-start.8 = (bf16[16,1024]{1,0:T(8,128)(2,1)S(1)}, bf16[16,1024]{1,0:T(8,128)(2,1)}, u32[]{:S(2)}) copy-start(bf16[16,1024]{1,0:T(8,128)(2,1)} %get-tuple-element.38) | copy-start | bytes 98308
  111.4 4.1 %copy-start.2 = (bf16[1,1,16,64,16]{4,3,2,1,0:T(8,128)(2,1)S(1)}, bf16[1,1,16,64,16]{4,3,2,1,0:T(8,128)(2,1)}, u32[]{:S(2)}) copy-start(bf16[1,1,16,64,16]{4,3,2,1,0:T(8,128)(2,1)} %stack.133) | copy-start | bytes 98308
  111.4 4.8 %copy-start.3 = (bf16[1,1,16,64,16]{4,3,2,1,0:T(8,128)(2,1)S(1)}, bf16[1,1,16,64,16]{4,3,2,1,0:T(8,128)(2,1)}, u32[]{:S(2)}) copy-start(bf16[1,1,16,64,16]{4,3,2,1,0:T(8,128)(2,1)} %stack.134) | copy-start | bytes 98308
  169.7 4.1 %copy-start.4 = (bf16[1,1,16,64,16]{4,3,2,1,0:T(8,128)(2,1)S(1)}, bf16[1,1,16,64,16]{4,3,2,1,0:T(8,128)(2,1)}, u32[]{:S(2)}) copy-start(bf16[1,1,16,64,16]{4,3,2,1,0:T(8,128)(2,1)} %stack.140) | copy-start | bytes 98308
  169.7 4.8 %copy-start.5 = (bf16[1,1,16,64,16]{4,3,2,1,0:T(8,128)(2,1)S(1)}, bf16[1,1,16,64,16]{4,3,2,1,0:T(8,128)(2,1)}, u32[]{:S(2)}) copy-start(bf16[1,1,16,64,16]{4,3,2,1,0:T(8,128)(2,1)} %stack.141) | copy-start | bytes 98308
  182.3 20.4 %all-to-all-start.3 = ((bf16[64,2,768]{2,1,0:T(2,128)(2,1)}), bf16[64,2,768]{2,1,0:T(2,128)(2,1)S(1)}, u32[]{:S(2)}, u32[]{:S(2)}) async-start(bf16[64,2,768]{2,1,0:T(2,128)(2,1)} %reshape.697), calls=%async_computation.3 | async-start | bytes 393216 | tf_op jit(solution)/shard_map/all_to_all | solution.py:23
  213.1 2.2 %copy-start.7 = (f32[1,3,1,16,1024]{4,3,2,1,0:T(8,128)S(1)}, f32[1,3,1,16,1024]{4,3,2,1,0:T(8,128)}, u32[]{:S(2)}) copy-start(f32[1,3,1,16,1024]{4,3,2,1,0:T(8,128)} %get-tuple-element.45) | copy-start | bytes 589828
  213.1 2.2 %copy-start.9 = (s32[1,16,1024]{2,1,0:T(8,128)S(1)}, s32[1,16,1024]{2,1,0:T(8,128)}, u32[]{:S(2)}) copy-start(s32[1,16,1024]{2,1,0:T(8,128)} %param.13) | copy-start | bytes 196612

commit v2 on v1

--- a/solution.py
+++ b/solution.py
@@ -14,16 +14,25 @@
     return solved.reshape(rounded.shape)
 
 
-def turn(block, line_count):
-    strip = block.shape[-2]
-    lead = block.shape[:-2]
-    n = len(lead)
-    parts = block.reshape(lead + (strip, line_count, strip))
-    parts = jnp.moveaxis(parts, n + 1, 0)
+def turn_rows(block, line_count):
+    comps, strip, cells = block.shape
+    parts = block.reshape(comps, strip, line_count, strip)
+    parts = jnp.transpose(parts, (2, 1, 0, 3)).reshape(line_count, strip, comps * strip)
     parts = lax.all_to_all(parts, "line", 0, 0, tiled=True)
-    order = tuple(range(1, n + 1)) + (n + 2, 0, n + 1)
-    parts = jnp.transpose(parts, order)
-    return parts.reshape(lead + (strip, line_count * strip))
+    return parts.reshape(line_count * strip, comps * strip)
+
+
+def solve_turned(turned, inverse):
+    return lax.dot_general(
+        turned, inverse, (((0,), (1,)), ((), ())), preferred_element_type=jnp.float32
+    )
+
+
+def bf16_parts(values):
+    high = lax.reduce_precision(values, exponent_bits=8, mantissa_bits=7)
+    rest = values - high
+    middle = lax.reduce_precision(rest, exponent_bits=8, mantissa_bits=7)
+    return [high, middle, rest - middle]
 
 
 def shift_down(f, along, first):
@@ -88,42 +97,42 @@
 ):
     line_cells = inverse.shape[0]
     strip = adj_e.shape[2]
+    planes = adj_e.shape[1]
+    eps_planes = permittivity.shape[0]
     step_count = fwd_e.shape[0]
     line_count = lax.axis_size("line")
     index = lax.axis_index("line")
     offset = index * strip
     inverse_rows = 1.0 / permittivity
-    inverse_cols = turn(inverse_rows, line_count)
     scaled_rows = COURANT * inverse_rows
-    scaled_cols = COURANT * inverse_cols
     frequency = omega[0]
     plane_at = port_plane[0]
     mask_weight = design_mask.astype(jnp.float32)
     gradient = jnp.zeros(design_mask.shape, jnp.float32)
+    comps = 6 * planes
 
-    fields = tuple(adj_e[i] for i in range(3)) + tuple(adj_h[i] for i in range(3))
     column = (jnp.arange(line_cells, dtype=jnp.int32) == plane_at).astype(jnp.float32)
     profile_rows = lax.dynamic_slice_in_dim(port_mode, offset, strip)
     amplitude = jnp.cos(frequency * 1.0)
-    ex, ey, ez, hx, hy, hz = fields
+    ex, ey, ez = adj_e[0], adj_e[1], adj_e[2]
+    hx, hy, hz = adj_h[0], adj_h[1], adj_h[2]
     ez = ez + (amplitude * profile_rows[None, :, None]) * column[None, None, :]
-    fields = (ex, ey, ez, hx, hy, hz)
-    rows_along = 1
     up = [(i, i + 1) for i in range(line_count - 1)]
     down = [(i + 1, i) for i in range(line_count - 1)]
     last_rows = jnp.stack([hx[:, -1:], hz[:, -1:]])
     first_rows = jnp.stack(
-        [ex[:, :1], ez[:, :1], hx[:, :1], hz[:, :1], scaled_rows[:, :1]]
+        [ex[:, :1], ez[:, :1], hx[:, :1], hz[:, :1], jnp.broadcast_to(scaled_rows[:, :1], ex[:, :1].shape)]
     )
     below = lax.ppermute(last_rows, "line", up)
     above = lax.ppermute(first_rows, "line", down)
     fields = curl_y(
-        fields,
+        (ex, ey, ez, hx, hy, hz),
         scaled_rows,
-        rows_along,
+        1,
         below=(below[0], below[1]),
         above=tuple(above[i] for i in range(5)),
     )
+    inverse_cols = None
     for instant in range(step_count):
         if instant > 0:
             amplitude = jnp.cos(frequency * (instant + 1))
@@ -131,17 +140,28 @@
             column_local = (x_local == plane_at).astype(jnp.float32)
             ex, ey, ez, hx, hy, hz = fields
             ez = ez + (amplitude * column_local[None, :, None]) * port_mode[None, None, :]
-            fields = curl_y((ex, ey, ez, hx, hy, hz), scaled_cols, 2)
-            rounded = jnp.stack(fields).astype(jnp.bfloat16)
-            rounded = turn(rounded, line_count)
+            fields = curl_y((ex, ey, ez, hx, hy, hz), COURANT * inverse_cols, 2)
+            rounded = jnp.stack(fields).reshape(comps, strip, line_cells).astype(jnp.bfloat16)
+            solved = solve_turned(turn_rows(rounded, line_count), inverse)
         else:
             rounded = jnp.stack(fields).astype(jnp.bfloat16)
-        solved = line_solve(rounded, inverse)
-        fields = tuple(solved[i] for i in range(6))
-        fields = curl_xz(fields, scaled_rows, 2, 0)
-        rounded = jnp.stack(fields).astype(jnp.bfloat16)
-        rounded = turn(rounded, line_count)
-        solved = line_solve(rounded, inverse)
+            solved = line_solve(rounded, inverse)
+        solved = solved.reshape(6, planes, strip, line_cells)
+        fields = curl_xz(tuple(solved[i] for i in range(6)), scaled_rows, 2, 0)
+        stacked = jnp.stack(fields).reshape(comps, strip, line_cells)
+        if inverse_cols is None:
+            stacked = jnp.concatenate([stacked] + bf16_parts(inverse_rows), 0)
+        turned = turn_rows(stacked.astype(jnp.bfloat16), line_count)
+        if inverse_cols is None:
+            width = eps_planes * strip
+            pieces = [
+                turned[:, comps * strip + k * width : comps * strip + (k + 1) * width].astype(jnp.float32)
+                for k in range(3)
+            ]
+            joined = (pieces[0] + pieces[1]) + pieces[2]
+            inverse_cols = joined.T.reshape(eps_planes, strip, line_cells)
+            turned = turned[:, : comps * strip]
+        solved = solve_turned(turned, inverse).reshape(6, planes, strip, line_cells)
         fields = tuple(solved[i] for i in range(6))
         snapshot = fwd_e[instant].astype(jnp.float32)
         intersection = fields[0] * snapshot[0] + fields[1] * snapshot[1] + fields[2] * snapshot[2]

time: 218 us -> 140 us (0.64)
  the two profiles are of different devices: /device:TPU:8 before, /device:TPU:1 now
where the time goes in v2:
time: 140 us; the launch traced here: 139 us
  waiting for transfers between devices  36.5 us (26%)
  starting transfers between devices  35.4 us (25%)
  blocking collectives  25.2 us (18%)
  local copies, waits for them, and re-layouts  24.9 us (18%)
  other arithmetic  11 us (8%)
  matrix products  3.13 us (2%)
  between operations  2.71 us (2%)
    all_to_all x2, waiting for transfers between devices, turn_rows(): parts = lax.all_to_all(parts, 'line', 0, 0, tiled=True)  29.4 us
    all_to_all x2, starting transfers between devices, turn_rows(): parts = lax.all_to_all(parts, 'line', 0, 0, tiled=True)  25.8 us
    all_to_all x1, blocking collectives, turn_rows(): parts = lax.all_to_all(parts, 'line', 0, 0, tiled=True)  25.2 us
    ppermute x1, starting transfers between devices, per_device(): below = lax.ppermute(last_rows, 'line', up)  8.28 us
    ppermute x1, waiting for transfers between devices, per_device(): above = lax.ppermute(first_rows, 'line', down)  7.17 us
    another operation x25, local copies, waits for them, and re-layouts, per_device(): stacked = jnp.stack(fields).reshape(comps, strip, line_cells)  6.47 us
    unnamed x35, local copies, waits for them, and re-layouts  5.05 us
    another operation x13, local copies, waits for them, and re-layouts, per_device(): jnp.stack(fields).reshape(comps, strip, line_cells).astype(jnp.bfloat16)  4.99 us
  transfers between devices with their start and end apart: 4, of which 3 were waited for; matrix products, arithmetic and copies ran while one was open for 3% of the time, Pallas kernels for 0%

profile of v2, /device:TPU:1, one launch (start us, length us, event | category | flops | bytes accessed | tf_op | source)
XLA Modules:
  0.0 138.9 jit_solution(16286988606786405044)
XLA Ops:
  0.6 1.0 slice_bitcast_fusion.23
  1.7 8.3 %collective-permute-start = (f32[2,1,1,1024]{3,2,1,0:T(1,128)S(1)}, f32[2,1,1,1024]{3,2,1,0:T(1,128)S(1)}, u32[]{:S(2)}, u32[]{:S(2)}) collective-permute-start(f32[2,1,1,1024]{3,2,1,0:T(1,128)S(1)} %pad_maximum_fusion.2), channel_id=1, source_target_pairs={{0,1},{1,2},{2,3},{3,4},{4,5},{5,6},{6,7},{7,8},{8,9},{9,10},{10,1... | collective-permute-start | bytes 24584 | tf_op jit(solution)/shard_map/ppermute | solution.py:126
  12.2 0.9 broadcast_multiply_fusion
  13.9 0.9 constant_dynamic-update-slice_fusion.10
  15.7 1.0 constant_dynamic-update-slice_fusion.8
  16.7 1.3 collective-permute-start.1
  18.1 7.2 %collective-permute-done.1 = f32[5,1,1,1024]{3,2,1,0:T(1,128)S(1)} collective-permute-done((f32[5,1,1,1024]{3,2,1,0:T(1,128)S(1)}, f32[5,1,1,1024]{3,2,1,0:T(1,128)S(1)}, u32[]{:S(2)}, u32[]{:S(2)}) %collective-permute-start.1) | collective-permute-done | bytes 20512 | tf_op jit(solution)/shard_map/ppermute | solution.py:127
  25.3 0.9 constant_dynamic-update-slice_fusion.7
  27.0 0.9 constant_dynamic-update-slice_fusion.5
  32.5 1.0 concatenate.102
  33.9 1.6 %copy.38 = bf16[64,16,144]{2,1,0:T(8,128)(2,1)} copy(bf16[64,16,144]{0,2,1:T(8,128)(2,1)S(1)} %bitcast.309) | data formatting | bytes 589824 | tf_op jit(solution)/shard_map/reshape | solution.py:20
  35.6 18.4 %all-to-all-start = ((bf16[64,16,144]{2,1,0:T(8,128)(2,1)}), bf16[64,16,144]{2,1,0:T(8,128)(2,1)S(1)}, u32[]{:S(2)}, u32[]{:S(2)}) async-start(bf16[64,16,144]{2,1,0:T(8,128)(2,1)} %copy.38), calls=%async_computation | async-start | bytes 1048576 | tf_op jit(solution)/shard_map/all_to_all | solution.py:21
  54.1 15.1 %all-to-all-done = bf16[64,16,144]{2,1,0:T(8,128)(2,1)S(1)} async-done(((bf16[64,16,144]{2,1,0:T(8,128)(2,1)}), bf16[64,16,144]{2,1,0:T(8,128)(2,1)S(1)}, u32[]{:S(2)}, u32[]{:S(2)}) %all-to-all-start) | async-done | bytes 294944 | tf_op jit(solution)/shard_map/all_to_all | solution.py:21
  69.2 1.0 fusion.67
  71.1 1.1 copy.58
  72.1 1.1 copy.59
  76.9 1.0 stack.131
  79.6 0.9 constant_dynamic-update-slice_fusion.20
  80.7 25.2 %all_to_all.15 = bf16[64,16,96]{2,1,0:T(8,128)(2,1)S(1)} all-to-all(bf16[64,16,96]{2,1,0:T(8,128)(2,1)S(1)} %copy.49), channel_id=1, replica_groups=mesh['exc'=8,'line'=64] {'line'}, dimensions={0} | all-to-all | bytes 393216 | tf_op jit(solution)/shard_map/all_to_all | solution.py:21
  109.6 1.0 stack.138
  112.3 0.9 copy.57
  113.3 7.4 %all-to-all-start.2 = ((bf16[64,16,96]{2,1,0:T(8,128)(2,1)}), bf16[64,16,96]{2,1,0:T(8,128)(2,1)S(1)}, u32[]{:S(2)}, u32[]{:S(2)}) async-start(bf16[64,16,96]{2,1,0:T(8,128)(2,1)} %copy.57), calls=%async_computation.2 | async-start | bytes 524288 | tf_op jit(solution)/shard_map/all_to_all | solution.py:21
  120.7 1.0 slice_convert_fusion.1
  121.7 14.3 %all-to-all-done.2 = bf16[64,16,96]{2,1,0:T(8,128)(2,1)S(1)} async-done(((bf16[64,16,96]{2,1,0:T(8,128)(2,1)}), bf16[64,16,96]{2,1,0:T(8,128)(2,1)S(1)}, u32[]{:S(2)}, u32[]{:S(2)}) %all-to-all-start.2) | async-done | bytes 196640 | tf_op jit(solution)/shard_map/all_to_all | solution.py:21
  (118 shorter events, 22.9 us)
Async XLA Ops:
  0.6 27.2 %copy-start = (bf16[1024,1024]{1,0:T(8,128)(2,1)S(1)}, bf16[1024,1024]{1,0:T(8,128)(2,1)}, u32[]{:S(2)}) copy-start(bf16[1024,1024]{1,0:T(8,128)(2,1)} %param.14) | copy-start | bytes 6291460
  1.7 12.2 %collective-permute-start = (f32[2,1,1,1024]{3,2,1,0:T(1,128)S(1)}, f32[2,1,1,1024]{3,2,1,0:T(1,128)S(1)}, u32[]{:S(2)}, u32[]{:S(2)}) collective-permute-start(f32[2,1,1,1024]{3,2,1,0:T(1,128)S(1)} %pad_maximum_fusion.2), channel_id=1, source_target_pairs={{0,1},{1,2},{2,3},{3,4},{4,5},{5,6},{6,7},{7,8},{8,9},{9,10},{10,1... | collective-permute-start | bytes 24584 | tf_op jit(solution)/shard_map/ppermute | solution.py:126
  15.7 13.0 %copy-start.1 = (f32[1,16,1024]{2,1,0:T(8,128)S(1)}, f32[1,16,1024]{2,1,0:T(8,128)}, u32[]{:S(2)}) copy-start(f32[1,16,1024]{2,1,0:T(8,128)} %param.12) | copy-start | bytes 196612
  16.7 8.5 %collective-permute-start.1 = (f32[5,1,1,1024]{3,2,1,0:T(1,128)S(1)}, f32[5,1,1,1024]{3,2,1,0:T(1,128)S(1)}, u32[]{:S(2)}, u32[]{:S(2)}) collective-permute-start(f32[5,1,1,1024]{3,2,1,0:T(1,128)S(1)} %constant_dynamic-update-slice_fusion), channel_id=1, source_target_pairs={{1,0},{2,1},{3,2},{4,3},{5,4},{6,5},{7,6},{8,7},{9,8},{10,9},{11,1... | collective-permute-start | bytes 61448 | tf_op jit(solution)/shard_map/ppermute | solution.py:127
  35.6 33.6 %all-to-all-start = ((bf16[64,16,144]{2,1,0:T(8,128)(2,1)}), bf16[64,16,144]{2,1,0:T(8,128)(2,1)S(1)}, u32[]{:S(2)}, u32[]{:S(2)}) async-start(bf16[64,16,144]{2,1,0:T(8,128)(2,1)} %copy.38), calls=%async_computation | async-start | bytes 1048576 | tf_op jit(solution)/shard_map/all_to_all | solution.py:21
  70.2 3.2 %copy-start.3 = (f32[1024]{0:T(1024)S(1)}, f32[1024]{0:T(1024)}, u32[]{:S(2)}) copy-start(f32[1024]{0:T(1024)} %param.16) | copy-start | bytes 12292
  113.3 22.7 %all-to-all-start.2 = ((bf16[64,16,96]{2,1,0:T(8,128)(2,1)}), bf16[64,16,96]{2,1,0:T(8,128)(2,1)S(1)}, u32[]{:S(2)}, u32[]{:S(2)}) async-start(bf16[64,16,96]{2,1,0:T(8,128)(2,1)} %copy.57), calls=%async_computation.2 | async-start | bytes 524288 | tf_op jit(solution)/shard_map/all_to_all | solution.py:21
  120.7 16.1 %copy-start.2 = (s32[1,16,1024]{2,1,0:T(8,128)S(1)}, s32[1,16,1024]{2,1,0:T(8,128)}, u32[]{:S(2)}) copy-start(s32[1,16,1024]{2,1,0:T(8,128)} %param.13) | copy-start | bytes 196612

commit v3 on v2

--- a/solution.py
+++ b/solution.py
@@ -30,9 +30,7 @@
 
 def bf16_parts(values):
     high = lax.reduce_precision(values, exponent_bits=8, mantissa_bits=7)
-    rest = values - high
-    middle = lax.reduce_precision(rest, exponent_bits=8, mantissa_bits=7)
-    return [high, middle, rest - middle]
+    return [high, values - high]
 
 
 def shift_down(f, along, first):
@@ -117,21 +115,37 @@
     ex, ey, ez = adj_e[0], adj_e[1], adj_e[2]
     hx, hy, hz = adj_h[0], adj_h[1], adj_h[2]
     ez = ez + (amplitude * profile_rows[None, :, None]) * column[None, None, :]
-    up = [(i, i + 1) for i in range(line_count - 1)]
-    down = [(i + 1, i) for i in range(line_count - 1)]
-    last_rows = jnp.stack([hx[:, -1:], hz[:, -1:]])
-    first_rows = jnp.stack(
-        [ex[:, :1], ez[:, :1], hx[:, :1], hz[:, :1], jnp.broadcast_to(scaled_rows[:, :1], ex[:, :1].shape)]
-    )
-    below = lax.ppermute(last_rows, "line", up)
-    above = lax.ppermute(first_rows, "line", down)
-    fields = curl_y(
-        (ex, ey, ez, hx, hy, hz),
-        scaled_rows,
-        1,
-        below=(below[0], below[1]),
-        above=tuple(above[i] for i in range(5)),
-    )
+    is_first = index == 0
+    ring = [(i, (i + 1) % line_count) for i in range(line_count)]
+    scaled_planes = jnp.broadcast_to(scaled_rows, ex.shape)
+    message = jnp.stack(
+        [f[:, -1:] for f in (ex, ey, ez, hx, hy, hz, scaled_planes)] + [hx[:, -2:-1], hz[:, -2:-1]]
+    )
+    message = lax.ppermute(message, "line", ring)
+    p_ex, p_ey, p_ez, p_hx, p_hy, p_hz, p_r, p_hx2, p_hz2 = (message[i] for i in range(9))
+    zero_row = jnp.zeros_like(p_hx)
+    hx_prev = shift_down(hx, 1, jnp.where(is_first, zero_row, p_hx))
+    hz_prev = shift_down(hz, 1, jnp.where(is_first, zero_row, p_hz))
+    ex1 = ex + scaled_rows * (hz - hz_prev)
+    ez1 = ez - scaled_rows * (hx - hx_prev)
+    hx1 = hx[:, :-1] - COURANT * (ez1[:, 1:] - ez1[:, :-1])
+    hz1 = hz[:, :-1] + COURANT * (ex1[:, 1:] - ex1[:, :-1])
+    ex_y = p_ex + p_r * (p_hz - p_hz2)
+    ez_y = p_ez - p_r * (p_hx - p_hx2)
+    ex_next = jnp.where(is_first, zero_row, ex1[:, :1])
+    ez_next = jnp.where(is_first, zero_row, ez1[:, :1])
+    hx_y = p_hx - COURANT * (ez_next - ez_y)
+    hz_y = p_hz + COURANT * (ex_next - ex_y)
+    fields = (
+        jnp.concatenate([ex_y, ex1[:, :-1]], 1),
+        jnp.concatenate([p_ey, ey[:, :-1]], 1),
+        jnp.concatenate([ez_y, ez1[:, :-1]], 1),
+        jnp.concatenate([hx_y, hx1], 1),
+        jnp.concatenate([p_hy, hy[:, :-1]], 1),
+        jnp.concatenate([hz_y, hz1], 1),
+    )
+    scaled_held = jnp.concatenate([p_r[:eps_planes], scaled_rows[:, :-1]], 1)
+    inverse_held = jnp.roll(inverse, 1, axis=1)
     inverse_cols = None
     for instant in range(step_count):
         if instant > 0:
@@ -147,7 +161,9 @@
             rounded = jnp.stack(fields).astype(jnp.bfloat16)
             solved = line_solve(rounded, inverse)
         solved = solved.reshape(6, planes, strip, line_cells)
-        fields = curl_xz(tuple(solved[i] for i in range(6)), scaled_rows, 2, 0)
+        fields = curl_xz(
+            tuple(solved[i] for i in range(6)), scaled_held if instant == 0 else scaled_rows, 2, 0
+        )
         stacked = jnp.stack(fields).reshape(comps, strip, line_cells)
         if inverse_cols is None:
             stacked = jnp.concatenate([stacked] + bf16_parts(inverse_rows), 0)
@@ -156,12 +172,13 @@
             width = eps_planes * strip
             pieces = [
                 turned[:, comps * strip + k * width : comps * strip + (k + 1) * width].astype(jnp.float32)
-                for k in range(3)
+                for k in range(2)
             ]
-            joined = (pieces[0] + pieces[1]) + pieces[2]
+            joined = pieces[0] + pieces[1]
             inverse_cols = joined.T.reshape(eps_planes, strip, line_cells)
             turned = turned[:, : comps * strip]
-        solved = solve_turned(turned, inverse).reshape(6, planes, strip, line_cells)
+        solved = solve_turned(turned, inverse_held if instant == 0 else inverse)
+        solved = solved.reshape(6, planes, strip, line_cells)
         fields = tuple(solved[i] for i in range(6))
         snapshot = fwd_e[instant].astype(jnp.float32)
         intersection = fields[0] * snapshot[0] + fields[1] * snapshot[1] + fields[2] * snapshot[2]

time: 140 us -> 112 us (0.80)
  the two profiles are of different devices: /device:TPU:1 before, /device:TPU:8 now
where the time goes in v3:
time: 112 us; the launch traced here: 111 us
  waiting for transfers between devices  45.4 us (41%)
  blocking collectives  20.4 us (18%)
  starting transfers between devices  19.7 us (18%)
  local copies, waits for them, and re-layouts  12.7 us (11%)
  other arithmetic  6.68 us (6%)
  matrix products  3.48 us (3%)
  between operations  3.02 us (3%)
    all_to_all x2, waiting for transfers between devices, turn_rows(): parts = lax.all_to_all(parts, 'line', 0, 0, tiled=True)  32.5 us
    all_to_all x1, blocking collectives, turn_rows(): parts = lax.all_to_all(parts, 'line', 0, 0, tiled=True)  20.4 us
    ppermute x1, waiting for transfers between devices, per_device(): message = lax.ppermute(message, 'line', ring)  12.9 us
    all_to_all x2, starting transfers between devices, turn_rows(): parts = lax.all_to_all(parts, 'line', 0, 0, tiled=True)  12.8 us
    ppermute x1, starting transfers between devices, per_device(): message = lax.ppermute(message, 'line', ring)  6.83 us
    another operation x25, local copies, waits for them, and re-layouts, per_device(): stacked = jnp.stack(fields).reshape(comps, strip, line_cells)  4.22 us
    dot_general x3, matrix products, solve_turned(): lax.dot_general(turned, inverse, (((0,), (1,)), ((), ())), preferred_elem...  2.71 us
  transfers between devices with their start and end apart: 3, of which 3 were waited for; matrix products, arithmetic and copies ran while one was open for 0% of the time, Pallas kernels for 0%

profile of v3, /device:TPU:8, one launch (start us, length us, event | category | flops | bytes accessed | tf_op | source)
XLA Modules:
  0.0 111.3 jit_solution(15544511617570461516)
XLA Ops:
  2.2 0.9 slice_bitcast_fusion.24
  3.1 0.9 slice_bitcast_fusion.22
  4.0 0.9 broadcast_multiply_fusion
  4.9 0.8 dynamic-slice_multiply_fusion
  5.6 0.9 bitcast_add_fusion
  6.7 6.8 %collective-permute-start = (f32[9,1,1,1024]{3,2,1,0:T(1,128)S(1)}, f32[9,1,1,1024]{3,2,1,0:T(1,128)S(1)}, u32[]{:S(2)}, u32[]{:S(2)}) collective-permute-start(f32[9,1,1,1024]{3,2,1,0:T(1,128)S(1)} %constant_dynamic-update-slice_fusion), channel_id=1, source_target_pairs={{0,1},{1,2},{2,3},{3,4},{4,5},{5,6},{6,7},{7,8},{8,9},{9,10},{10,1... | collective-permute-start | bytes 110600 | tf_op jit(solution)/shard_map/ppermute | solution.py:124
  13.6 12.9 %collective-permute-done = f32[9,1,1,1024]{3,2,1,0:T(1,128)S(1)} collective-permute-done((f32[9,1,1,1024]{3,2,1,0:T(1,128)S(1)}, f32[9,1,1,1024]{3,2,1,0:T(1,128)S(1)}, u32[]{:S(2)}, u32[]{:S(2)}) %collective-permute-start) | collective-permute-done | bytes 36896 | tf_op jit(solution)/shard_map/ppermute | solution.py:124
  26.5 1.1 fusion.34
  27.9 0.8 fusion.83
  32.1 1.0 copy.35
  33.1 8.2 %all-to-all-start = ((bf16[64,16,128]{2,1,0:T(8,128)(2,1)}), bf16[64,16,128]{2,1,0:T(8,128)(2,1)S(1)}, u32[]{:S(2)}, u32[]{:S(2)}) async-start(bf16[64,16,128]{2,1,0:T(8,128)(2,1)} %copy.35), calls=%async_computation | async-start | bytes 524288 | tf_op jit(solution)/shard_map/all_to_all | solution.py:21
  41.6 16.7 %all-to-all-done = bf16[64,16,128]{2,1,0:T(8,128)(2,1)S(1)} async-done(((bf16[64,16,128]{2,1,0:T(8,128)(2,1)}), bf16[64,16,128]{2,1,0:T(8,128)(2,1)S(1)}, u32[]{:S(2)}, u32[]{:S(2)}) %all-to-all-start) | async-done | bytes 262176 | tf_op jit(solution)/shard_map/all_to_all | solution.py:21
  58.5 1.1 %fusion = f32[96,1024]{1,0:T(8,128)S(1)} fusion(bf16[1024,1023]{1,0:T(8,128)(2,1)S(1)} %bitcast.353, bf16[1024,1]{1,0:T(8,128)(2,1)S(1)} %slice.361, bf16[1024,128]{1,0:T(8,128)(2,1)S(1)} %bitcast.355), kind=kOutput, calls=%fused_computation | convolution fusion | flops 205520896 | bytes 2752512 | tf_op jit(solution)/shard_map/dot_general | solution.py:26
  60.4 0.2 stack.141
  62.8 0.3 copy.45
  63.0 20.4 %all_to_all.15 = bf16[64,16,96]{2,1,0:T(8,128)(2,1)S(1)} all-to-all(bf16[64,16,96]{2,1,0:T(8,128)(2,1)S(1)} %copy.45), channel_id=1, replica_groups=mesh['exc'=8,'line'=64] {'line'}, dimensions={0} | all-to-all | bytes 393216 | tf_op jit(solution)/shard_map/all_to_all | solution.py:21
  83.5 0.8 fusion.84
  87.0 0.9 copy.53
  88.0 4.6 %all-to-all-start.2 = ((bf16[64,16,96]{2,1,0:T(8,128)(2,1)}), bf16[64,16,96]{2,1,0:T(8,128)(2,1)S(1)}, u32[]{:S(2)}, u32[]{:S(2)}) async-start(bf16[64,16,96]{2,1,0:T(8,128)(2,1)} %copy.53), calls=%async_computation.2 | async-start | bytes 524288 | tf_op jit(solution)/shard_map/all_to_all | solution.py:21
  92.6 15.8 %all-to-all-done.2 = bf16[64,16,96]{2,1,0:T(8,128)(2,1)S(1)} async-done(((bf16[64,16,96]{2,1,0:T(8,128)(2,1)}), bf16[64,16,96]{2,1,0:T(8,128)(2,1)S(1)}, u32[]{:S(2)}, u32[]{:S(2)}) %all-to-all-start.2) | async-done | bytes 196640 | tf_op jit(solution)/shard_map/all_to_all | solution.py:21
  108.4 0.8 fusion.85
  109.3 0.7 fusion.11
  110.0 0.7 pad_maximum_fusion.1
  110.7 0.7 pad_maximum_fusion
  (125 shorter events, 9.5 us)
Async XLA Ops:
  0.6 27.2 %copy-start = (bf16[1024,1024]{1,0:T(8,128)(2,1)S(1)}, bf16[1024,1024]{1,0:T(8,128)(2,1)}, u32[]{:S(2)}) copy-start(bf16[1024,1024]{1,0:T(8,128)(2,1)} %param.14) | copy-start | bytes 6291460
  6.7 19.8 %collective-permute-start = (f32[9,1,1,1024]{3,2,1,0:T(1,128)S(1)}, f32[9,1,1,1024]{3,2,1,0:T(1,128)S(1)}, u32[]{:S(2)}, u32[]{:S(2)}) collective-permute-start(f32[9,1,1,1024]{3,2,1,0:T(1,128)S(1)} %constant_dynamic-update-slice_fusion), channel_id=1, source_target_pairs={{0,1},{1,2},{2,3},{3,4},{4,5},{5,6},{6,7},{7,8},{8,9},{9,10},{10,1... | collective-permute-start | bytes 110600 | tf_op jit(solution)/shard_map/ppermute | solution.py:124
  33.1 25.2 %all-to-all-start = ((bf16[64,16,128]{2,1,0:T(8,128)(2,1)}), bf16[64,16,128]{2,1,0:T(8,128)(2,1)S(1)}, u32[]{:S(2)}, u32[]{:S(2)}) async-start(bf16[64,16,128]{2,1,0:T(8,128)(2,1)} %copy.35), calls=%async_computation | async-start | bytes 524288 | tf_op jit(solution)/shard_map/all_to_all | solution.py:21
  58.5 1.6 %copy-start.4 = (f32[1024]{0:T(1024)S(1)}, f32[1024]{0:T(1024)}, u32[]{:S(2)}) copy-start(f32[1024]{0:T(1024)} %param.16) | copy-start | bytes 12292
  62.8 21.5 %copy-start.1 = (f32[1,16,1024]{2,1,0:T(8,128)S(1)}, f32[1,16,1024]{2,1,0:T(8,128)}, u32[]{:S(2)}) copy-start(f32[1,16,1024]{2,1,0:T(8,128)} %param.12) | copy-start | bytes 196612
  87.0 5.6 %copy-start.2 = (bf16[2,3,1,16,1024]{4,3,2,1,0:T(8,128)(2,1)S(1)}, bf16[2,3,1,16,1024]{4,3,2,1,0:T(8,128)(2,1)}, u32[]{:S(2)}) copy-start(bf16[2,3,1,16,1024]{4,3,2,1,0:T(8,128)(2,1)} %param.11) | copy-start | bytes 589828
  88.0 20.5 %all-to-all-start.2 = ((bf16[64,16,96]{2,1,0:T(8,128)(2,1)}), bf16[64,16,96]{2,1,0:T(8,128)(2,1)S(1)}, u32[]{:S(2)}, u32[]{:S(2)}) async-start(bf16[64,16,96]{2,1,0:T(8,128)(2,1)} %copy.53), calls=%async_computation.2 | async-start | bytes 524288 | tf_op jit(solution)/shard_map/all_to_all | solution.py:21
  92.6 16.7 %copy-start.3 = (s32[1,16,1024]{2,1,0:T(8,128)S(1)}, s32[1,16,1024]{2,1,0:T(8,128)}, u32[]{:S(2)}) copy-start(s32[1,16,1024]{2,1,0:T(8,128)} %param.13) | copy-start | bytes 196612

commit v4 on v3

--- a/solution.py
+++ b/solution.py
@@ -109,42 +109,57 @@
     gradient = jnp.zeros(design_mask.shape, jnp.float32)
     comps = 6 * planes
 
+    ring = [(i, (i + 1) % line_count) for i in range(line_count)]
+    eps_planes_b = jnp.broadcast_to(permittivity, adj_e[0].shape)
+    message = jnp.concatenate(
+        [adj_e[:, :, -1:], adj_h[:, :, -1:], eps_planes_b[None, :, -1:], adj_h[::2, :, -2:-1]], 0
+    )
+    message = lax.ppermute(message, "line", ring)
+    is_first = index == 0
     column = (jnp.arange(line_cells, dtype=jnp.int32) == plane_at).astype(jnp.float32)
     profile_rows = lax.dynamic_slice_in_dim(port_mode, offset, strip)
     amplitude = jnp.cos(frequency * 1.0)
     ex, ey, ez = adj_e[0], adj_e[1], adj_e[2]
     hx, hy, hz = adj_h[0], adj_h[1], adj_h[2]
     ez = ez + (amplitude * profile_rows[None, :, None]) * column[None, None, :]
-    is_first = index == 0
-    ring = [(i, (i + 1) % line_count) for i in range(line_count)]
-    scaled_planes = jnp.broadcast_to(scaled_rows, ex.shape)
-    message = jnp.stack(
-        [f[:, -1:] for f in (ex, ey, ez, hx, hy, hz, scaled_planes)] + [hx[:, -2:-1], hz[:, -2:-1]]
-    )
-    message = lax.ppermute(message, "line", ring)
-    p_ex, p_ey, p_ez, p_hx, p_hy, p_hz, p_r, p_hx2, p_hz2 = (message[i] for i in range(9))
+    ex1 = ex[:, 1:] + scaled_rows[:, 1:] * (hz[:, 1:] - hz[:, :-1])
+    ez1 = ez[:, 1:] - scaled_rows[:, 1:] * (hx[:, 1:] - hx[:, :-1])
+    hx1 = hx[:, 1:-1] - COURANT * (ez1[:, 1:] - ez1[:, :-1])
+    hz1 = hz[:, 1:-1] + COURANT * (ex1[:, 1:] - ex1[:, :-1])
+    inner = (ex1[:, :-1], ey[:, 1:-1], ez1[:, :-1], hx1, hy[:, 1:-1], hz1)
+    inner_solved = line_solve(jnp.stack(inner).astype(jnp.bfloat16), inverse)
+    inner_fields = curl_xz(tuple(inner_solved[i] for i in range(6)), scaled_rows[:, 1:-1], 2, 0)
+    p_ex, p_ey, p_ez, p_hx, p_hy, p_hz = (message[i] for i in range(6))
+    p_eps, p_hx2, p_hz2 = message[6], message[7], message[8]
+    row_before = (offset + line_cells - 1) % line_cells
+    profile_before = lax.dynamic_slice_in_dim(port_mode, row_before, 1)
+    p_ez = p_ez + (amplitude * profile_before[None, :, None]) * column[None, None, :]
+    p_r = COURANT * (1.0 / p_eps)
     zero_row = jnp.zeros_like(p_hx)
-    hx_prev = shift_down(hx, 1, jnp.where(is_first, zero_row, p_hx))
-    hz_prev = shift_down(hz, 1, jnp.where(is_first, zero_row, p_hz))
-    ex1 = ex + scaled_rows * (hz - hz_prev)
-    ez1 = ez - scaled_rows * (hx - hx_prev)
-    hx1 = hx[:, :-1] - COURANT * (ez1[:, 1:] - ez1[:, :-1])
-    hz1 = hz[:, :-1] + COURANT * (ex1[:, 1:] - ex1[:, :-1])
+    below_hx = jnp.where(is_first, zero_row, p_hx)
+    below_hz = jnp.where(is_first, zero_row, p_hz)
+    ex_0 = ex[:, :1] + scaled_rows[:, :1] * (hz[:, :1] - below_hz)
+    ez_0 = ez[:, :1] - scaled_rows[:, :1] * (hx[:, :1] - below_hx)
+    hx_0 = hx[:, :1] - COURANT * (ez1[:, :1] - ez_0)
+    hz_0 = hz[:, :1] + COURANT * (ex1[:, :1] - ex_0)
     ex_y = p_ex + p_r * (p_hz - p_hz2)
     ez_y = p_ez - p_r * (p_hx - p_hx2)
-    ex_next = jnp.where(is_first, zero_row, ex1[:, :1])
-    ez_next = jnp.where(is_first, zero_row, ez1[:, :1])
+    ex_next = jnp.where(is_first, zero_row, ex_0)
+    ez_next = jnp.where(is_first, zero_row, ez_0)
     hx_y = p_hx - COURANT * (ez_next - ez_y)
     hz_y = p_hz + COURANT * (ex_next - ex_y)
-    fields = (
-        jnp.concatenate([ex_y, ex1[:, :-1]], 1),
-        jnp.concatenate([p_ey, ey[:, :-1]], 1),
-        jnp.concatenate([ez_y, ez1[:, :-1]], 1),
-        jnp.concatenate([hx_y, hx1], 1),
-        jnp.concatenate([p_hy, hy[:, :-1]], 1),
-        jnp.concatenate([hz_y, hz1], 1),
-    )
-    scaled_held = jnp.concatenate([p_r[:eps_planes], scaled_rows[:, :-1]], 1)
+    edge = (
+        jnp.concatenate([ex_y, ex_0], 1),
+        jnp.concatenate([p_ey, ey[:, :1]], 1),
+        jnp.concatenate([ez_y, ez_0], 1),
+        jnp.concatenate([hx_y, hx_0], 1),
+        jnp.concatenate([p_hy, hy[:, :1]], 1),
+        jnp.concatenate([hz_y, hz_0], 1),
+    )
+    edge_solved = line_solve(jnp.stack(edge).astype(jnp.bfloat16), inverse)
+    scaled_edge = jnp.concatenate([p_r[:eps_planes], scaled_rows[:, :1]], 1)
+    edge_fields = curl_xz(tuple(edge_solved[i] for i in range(6)), scaled_edge, 2, 0)
+    first_fields = tuple(jnp.concatenate([a, b], 1) for a, b in zip(edge_fields, inner_fields))
     inverse_held = jnp.roll(inverse, 1, axis=1)
     inverse_cols = None
     for instant in range(step_count):
@@ -157,13 +172,10 @@
             fields = curl_y((ex, ey, ez, hx, hy, hz), COURANT * inverse_cols, 2)
             rounded = jnp.stack(fields).reshape(comps, strip, line_cells).astype(jnp.bfloat16)
             solved = solve_turned(turn_rows(rounded, line_count), inverse)
+            solved = solved.reshape(6, planes, strip, line_cells)
+            fields = curl_xz(tuple(solved[i] for i in range(6)), scaled_rows, 2, 0)
         else:
-            rounded = jnp.stack(fields).astype(jnp.bfloat16)
-            solved = line_solve(rounded, inverse)
-        solved = solved.reshape(6, planes, strip, line_cells)
-        fields = curl_xz(
-            tuple(solved[i] for i in range(6)), scaled_held if instant == 0 else scaled_rows, 2, 0
-        )
+            fields = first_fields
         stacked = jnp.stack(fields).reshape(comps, strip, line_cells)
         if inverse_cols is None:
             stacked = jnp.concatenate([stacked] + bf16_parts(inverse_rows), 0)

time: 112 us -> 115 us (1.027)
  the two profiles are of different devices: /device:TPU:8 before, /device:TPU:16 now
where the time goes in v4:
time: 115 us; the launch traced here: 114 us
  waiting for transfers between devices  35.6 us (31%)
  starting transfers between devices  24.6 us (21%)
  blocking collectives  21.4 us (19%)
  local copies, waits for them, and re-layouts  18.7 us (16%)
  other arithmetic  6.08 us (5%)
  matrix products  4.11 us (4%)
  between operations  3.61 us (3%)
    all_to_all x2, waiting for transfers between devices, turn_rows(): parts = lax.all_to_all(parts, 'line', 0, 0, tiled=True)  33.9 us
    all_to_all x1, blocking collectives, turn_rows(): parts = lax.all_to_all(parts, 'line', 0, 0, tiled=True)  21.4 us
    all_to_all x2, starting transfers between devices, turn_rows(): parts = lax.all_to_all(parts, 'line', 0, 0, tiled=True)  18.7 us
    ppermute x1, starting transfers between devices, per_device(): message = lax.ppermute(message, 'line', ring)  5.94 us
    another operation x23, local copies, waits for them, and re-layouts, per_device(): stacked = jnp.stack(fields).reshape(comps, strip, line_cells)  3.85 us
    dot_general x3, matrix products, solve_turned(): lax.dot_general(turned, inverse, (((0,), (1,)), ((), ())), preferred_elem...  2.7 us
  transfers between devices with their start and end apart: 3, of which 3 were waited for; matrix products, arithmetic and copies ran while one was open for 8% of the time, Pallas kernels for 0%

profile of v4, /device:TPU:16, one launch (start us, length us, event | category | flops | bytes accessed | tf_op | source)
XLA Modules:
  0.0 114.2 jit_solution(8771176816196938944)
XLA Ops:
  0.6 1.1 slice.384
  1.7 0.9 slice.386
  2.5 0.9 slice.383
  3.5 0.8 slice_bitcast_fusion.44
  4.3 5.9 %collective-permute-start = (f32[9,1,1,1024]{3,0,2,1:T(8,128)S(1)}, f32[9,1,1,1024]{3,0,2,1:T(8,128)S(1)}, u32[]{:S(2)}, u32[]{:S(2)}) collective-permute-start(f32[9,1,1,1024]{3,0,2,1:T(8,128)S(1)} %pad_maximum_fusion.2), channel_id=1, source_target_pairs={{0,1},{1,2},{2,3},{3,4},{4,5},{5,6},{6,7},{7,8},{8,9},{9,10},{10,1... | collective-permute-start | bytes 110600 | tf_op jit(solution)/shard_map/ppermute | solution.py:117
  10.2 0.9 fusion.5
  11.1 0.9 slice_bitcast_fusion.23
  12.0 0.8 slice_bitcast_fusion.25
  12.8 0.8 fusion.47
  13.7 0.8 fusion.48
  15.9 0.8 dynamic-slice_multiply_fusion
  16.7 0.9 bitcast_add_fusion
  17.9 0.8 fusion.112
  21.4 1.7 %collective-permute-done = f32[9,1,1,1024]{3,0,2,1:T(8,128)S(1)} collective-permute-done((f32[9,1,1,1024]{3,0,2,1:T(8,128)S(1)}, f32[9,1,1,1024]{3,0,2,1:T(8,128)S(1)}, u32[]{:S(2)}, u32[]{:S(2)}) %collective-permute-start) | collective-permute-done | bytes 36896 | tf_op jit(solution)/shard_map/ppermute | solution.py:117
  26.7 1.0 copy.39
  27.7 14.1 %all-to-all-start = ((bf16[64,16,128]{2,1,0:T(8,128)(2,1)}), bf16[64,16,128]{2,1,0:T(8,128)(2,1)S(1)}, u32[]{:S(2)}, u32[]{:S(2)}) async-start(bf16[64,16,128]{2,1,0:T(8,128)(2,1)} %copy.39), calls=%async_computation | async-start | bytes 524288 | tf_op jit(solution)/shard_map/all_to_all | solution.py:21
  42.0 16.9 %all-to-all-done = bf16[64,16,128]{2,1,0:T(8,128)(2,1)S(1)} async-done(((bf16[64,16,128]{2,1,0:T(8,128)(2,1)}), bf16[64,16,128]{2,1,0:T(8,128)(2,1)S(1)}, u32[]{:S(2)}, u32[]{:S(2)}) %all-to-all-start) | async-done | bytes 262176 | tf_op jit(solution)/shard_map/all_to_all | solution.py:21
  59.1 1.1 fusion
  63.7 21.4 %all_to_all.15 = bf16[64,16,96]{2,1,0:T(8,128)(2,1)S(1)} all-to-all(bf16[64,16,96]{2,1,0:T(8,128)(2,1)S(1)} %copy.49), channel_id=1, replica_groups=mesh['exc'=8,'line'=64] {'line'}, dimensions={0} | all-to-all | bytes 393216 | tf_op jit(solution)/shard_map/all_to_all | solution.py:21
  85.1 0.8 fusion.113
  88.7 0.9 copy.57
  89.6 4.6 %all-to-all-start.2 = ((bf16[64,16,96]{2,1,0:T(8,128)(2,1)}), bf16[64,16,96]{2,1,0:T(8,128)(2,1)S(1)}, u32[]{:S(2)}, u32[]{:S(2)}) async-start(bf16[64,16,96]{2,1,0:T(8,128)(2,1)} %copy.57), calls=%async_computation.2 | async-start | bytes 524288 | tf_op jit(solution)/shard_map/all_to_all | solution.py:21
  94.3 17.0 %all-to-all-done.2 = bf16[64,16,96]{2,1,0:T(8,128)(2,1)S(1)} async-done(((bf16[64,16,96]{2,1,0:T(8,128)(2,1)}), bf16[64,16,96]{2,1,0:T(8,128)(2,1)S(1)}, u32[]{:S(2)}, u32[]{:S(2)}) %all-to-all-start.2) | async-done | bytes 196640 | tf_op jit(solution)/shard_map/all_to_all | solution.py:21
  111.3 0.8 fusion.114
  (146 shorter events, 14.0 us)
Async XLA Ops:
  0.6 17.2 %copy-start = (bf16[1024,1024]{1,0:T(8,128)(2,1)S(1)}, bf16[1024,1024]{1,0:T(8,128)(2,1)}, u32[]{:S(2)}) copy-start(bf16[1024,1024]{1,0:T(8,128)(2,1)} %param.14) | copy-start | bytes 6291460
  4.3 18.8 %collective-permute-start = (f32[9,1,1,1024]{3,0,2,1:T(8,128)S(1)}, f32[9,1,1,1024]{3,0,2,1:T(8,128)S(1)}, u32[]{:S(2)}, u32[]{:S(2)}) collective-permute-start(f32[9,1,1,1024]{3,0,2,1:T(8,128)S(1)} %pad_maximum_fusion.2), channel_id=1, source_target_pairs={{0,1},{1,2},{2,3},{3,4},{4,5},{5,6},{6,7},{7,8},{8,9},{9,10},{10,1... | collective-permute-start | bytes 110600 | tf_op jit(solution)/shard_map/ppermute | solution.py:117
  17.8 1.3 %copy-start.4 = (f32[1024]{0:T(1024)S(1)}, f32[1024]{0:T(1024)}, u32[]{:S(2)}) copy-start(f32[1024]{0:T(1024)} %param.16) | copy-start | bytes 12292
  27.7 31.2 %all-to-all-start = ((bf16[64,16,128]{2,1,0:T(8,128)(2,1)}), bf16[64,16,128]{2,1,0:T(8,128)(2,1)S(1)}, u32[]{:S(2)}, u32[]{:S(2)}) async-start(bf16[64,16,128]{2,1,0:T(8,128)(2,1)} %copy.39), calls=%async_computation | async-start | bytes 524288 | tf_op jit(solution)/shard_map/all_to_all | solution.py:21
  63.4 22.5 %copy-start.1 = (f32[1,16,1024]{2,1,0:T(8,128)S(1)}, f32[1,16,1024]{2,1,0:T(8,128)}, u32[]{:S(2)}) copy-start(f32[1,16,1024]{2,1,0:T(8,128)} %param.12) | copy-start | bytes 196612
  88.6 5.6 %copy-start.2 = (bf16[2,3,1,16,1024]{4,3,2,1,0:T(8,128)(2,1)S(1)}, bf16[2,3,1,16,1024]{4,3,2,1,0:T(8,128)(2,1)}, u32[]{:S(2)}) copy-start(bf16[2,3,1,16,1024]{4,3,2,1,0:T(8,128)(2,1)} %param.11) | copy-start | bytes 589828
  89.6 21.7 %all-to-all-start.2 = ((bf16[64,16,96]{2,1,0:T(8,128)(2,1)}), bf16[64,16,96]{2,1,0:T(8,128)(2,1)S(1)}, u32[]{:S(2)}, u32[]{:S(2)}) async-start(bf16[64,16,96]{2,1,0:T(8,128)(2,1)} %copy.57), calls=%async_computation.2 | async-start | bytes 524288 | tf_op jit(solution)/shard_map/all_to_all | solution.py:21
  94.2 17.9 %copy-start.3 = (s32[1,16,1024]{2,1,0:T(8,128)S(1)}, s32[1,16,1024]{2,1,0:T(8,128)}, u32[]{:S(2)}) copy-start(s32[1,16,1024]{2,1,0:T(8,128)} %param.13) | copy-start | bytes 196612

commit v5 on v4

--- a/solution.py
+++ b/solution.py
@@ -14,12 +14,21 @@
     return solved.reshape(rounded.shape)
 
 
+def pack_rows(block, line_count):
+    comps, rows, cells = block.shape
+    strip = cells // line_count
+    parts = block.reshape(comps, rows, line_count, strip)
+    return jnp.transpose(parts, (2, 1, 0, 3)).reshape(line_count, rows, comps * strip)
+
+
+def send_rows(parts):
+    line_count, strip, width = parts.shape
+    parts = lax.all_to_all(parts, "line", 0, 0, tiled=True)
+    return parts.reshape(line_count * strip, width)
+
+
 def turn_rows(block, line_count):
-    comps, strip, cells = block.shape
-    parts = block.reshape(comps, strip, line_count, strip)
-    parts = jnp.transpose(parts, (2, 1, 0, 3)).reshape(line_count, strip, comps * strip)
-    parts = lax.all_to_all(parts, "line", 0, 0, tiled=True)
-    return parts.reshape(line_count * strip, comps * strip)
+    return send_rows(pack_rows(block, line_count))
 
 
 def solve_turned(turned, inverse):
@@ -159,7 +168,14 @@
     edge_solved = line_solve(jnp.stack(edge).astype(jnp.bfloat16), inverse)
     scaled_edge = jnp.concatenate([p_r[:eps_planes], scaled_rows[:, :1]], 1)
     edge_fields = curl_xz(tuple(edge_solved[i] for i in range(6)), scaled_edge, 2, 0)
-    first_fields = tuple(jnp.concatenate([a, b], 1) for a, b in zip(edge_fields, inner_fields))
+    def packed(fields, eps_rows):
+        stacked = jnp.stack(fields).reshape((comps,) + fields[0].shape[1:])
+        stacked = jnp.concatenate([stacked] + bf16_parts(eps_rows), 0)
+        return pack_rows(stacked.astype(jnp.bfloat16), line_count)
+
+    first_parts = jnp.concatenate(
+        [packed(edge_fields, inverse_rows[:, :2]), packed(inner_fields, inverse_rows[:, 2:])], 1
+    )
     inverse_held = jnp.roll(inverse, 1, axis=1)
     inverse_cols = None
     for instant in range(step_count):
@@ -174,12 +190,10 @@
             solved = solve_turned(turn_rows(rounded, line_count), inverse)
             solved = solved.reshape(6, planes, strip, line_cells)
             fields = curl_xz(tuple(solved[i] for i in range(6)), scaled_rows, 2, 0)
+            stacked = jnp.stack(fields).reshape(comps, strip, line_cells)
+            turned = turn_rows(stacked.astype(jnp.bfloat16), line_count)
         else:
-            fields = first_fields
-        stacked = jnp.stack(fields).reshape(comps, strip, line_cells)
-        if inverse_cols is None:
-            stacked = jnp.concatenate([stacked] + bf16_parts(inverse_rows), 0)
-        turned = turn_rows(stacked.astype(jnp.bfloat16), line_count)
+            turned = send_rows(first_parts)
         if inverse_cols is None:
             width = eps_planes * strip
             pieces = [
@@ -189,14 +203,15 @@
             joined = pieces[0] + pieces[1]
             inverse_cols = joined.T.reshape(eps_planes, strip, line_cells)
             turned = turned[:, : comps * strip]
-        solved = solve_turned(turned, inverse_held if instant == 0 else inverse)
-        solved = solved.reshape(6, planes, strip, line_cells)
-        fields = tuple(solved[i] for i in range(6))
+        held = inverse_held if instant == 0 else inverse
+        half = 3 * planes * strip
+        solved_e = solve_turned(turned[:, :half], held).reshape(3, planes, strip, line_cells)
+        solved_h = solve_turned(turned[:, half:], held).reshape(3, planes, strip, line_cells)
+        fields = tuple(solved_e[i] for i in range(3)) + tuple(solved_h[i] for i in range(3))
         snapshot = fwd_e[instant].astype(jnp.float32)
         intersection = fields[0] * snapshot[0] + fields[1] * snapshot[1] + fields[2] * snapshot[2]
         gradient = gradient + mask_weight * intersection * (inverse_cols * inverse_cols)
-    out = jnp.stack(fields)
-    return (out[:3], out[3:], gradient)
+    return (solved_e, solved_h, gradient)
 
 
 def solution(mesh):

time: 115 us -> 128 us (1.11)
  local copies, waits for them, and re-layouts: 18.7 us -> 25.8 us
  other arithmetic: 6.08 us -> 9.4 us
  matrix products: 4.11 us -> 6.8 us
  waiting for transfers between devices: 35.6 us -> 33 us
  starting transfers between devices: 24.6 us -> 26.3 us
    concatenate x9 -> x11, local copies, waits for them, and re-layouts: 1.22 us -> 5.59 us  [the longest x10 4.64 us: packed(): stacked = jnp.concatenate([stacked] + bf16_parts(eps_rows), 0)]
    another operation x2 -> x26, local copies, waits for them, and re-layouts: 1.69 us -> 4.77 us  [the longest x24 3.07 us: packed(): stacked = jnp.stack(fields).reshape((comps,) + fields[0].shape[1:])]
    dot_general x3 -> x5, matrix products: 2.7 us -> 5.39 us  [solve_turned(): lax.dot_general(turned, inverse, (((0,), (1,)), ((), ())), preferred_elem...]
    another operation x23 -> x13, local copies, waits for them, and re-layouts: 3.85 us -> 2.12 us  [per_device(): stacked = jnp.stack(fields).reshape(comps, strip, line_cells)]
    ppermute x1, waiting for transfers between devices: 1.73 us -> 0.01 us  [per_device(): message = lax.ppermute(message, 'line', ring)]
    all_to_all x2, starting transfers between devices: 18.7 us -> 20.4 us  [send_rows(): parts = lax.all_to_all(parts, 'line', 0, 0, tiled=True)]
    another operation x18 -> x16, other arithmetic: 3.14 us -> 4.06 us
  transfers between devices with their start and end apart: 3 -> 3, of which waited for: 3 -> 2; matrix products, arithmetic and copies ran while one was open for 8% -> 15% of each run, Pallas kernels for 0% -> 0%
where the time goes in v5:
time: 128 us; the launch traced here: 126 us
  waiting for transfers between devices  33 us (26%)
  starting transfers between devices  26.3 us (21%)
  local copies, waits for them, and re-layouts  25.8 us (20%)
  blocking collectives  21.4 us (17%)
  other arithmetic  9.4 us (7%)
  matrix products  6.8 us (5%)
  between operations  3.59 us (3%)
    all_to_all x2, waiting for transfers between devices, send_rows(): parts = lax.all_to_all(parts, 'line', 0, 0, tiled=True)  33 us
    all_to_all x1, blocking collectives, send_rows(): parts = lax.all_to_all(parts, 'line', 0, 0, tiled=True)  21.4 us
    all_to_all x2, starting transfers between devices, send_rows(): parts = lax.all_to_all(parts, 'line', 0, 0, tiled=True)  20.4 us
    ppermute x1, starting transfers between devices, per_device(): message = lax.ppermute(message, 'line', ring)  5.92 us
    dot_general x5, matrix products, solve_turned(): lax.dot_general(turned, inverse, (((0,), (1,)), ((), ())), preferred_elem...  5.39 us
    concatenate x10, local copies, waits for them, and re-layouts, packed(): stacked = jnp.concatenate([stacked] + bf16_parts(eps_rows), 0)  4.64 us
    another operation x16, other arithmetic  4.06 us
    another operation x24, local copies, waits for them, and re-layouts, packed(): stacked = jnp.stack(fields).reshape((comps,) + fields[0].shape[1:])  3.07 us
  transfers between devices with their start and end apart: 3, of which 2 were waited for; matrix products, arithmetic and copies ran while one was open for 15% of the time, Pallas kernels for 0%

profile of v5, /device:TPU:16, one launch (start us, length us, event | category | flops | bytes accessed | tf_op | source)
XLA Modules:
  0.0 126.3 jit_solution(5886840794808153031)
XLA Ops:
  0.6 1.1 slice.374
  1.7 0.9 slice.376
  2.5 0.9 slice.373
  4.9 5.9 %collective-permute-start = (f32[9,1,1,1024]{3,0,2,1:T(8,128)}, f32[9,1,1,1024]{3,0,2,1:T(8,128)}, u32[]{:S(2)}, u32[]{:S(2)}) collective-permute-start(f32[9,1,1,1024]{3,0,2,1:T(8,128)} %pad_maximum_fusion.4), channel_id=1, source_target_pairs={{0,1},{1,2},{2,3},{3,4},{4,5},{5,6},{6,7},{7,8},{8,9},{9,10},{10,1... | collective-permute-start | bytes 110600 | tf_op jit(solution)/shard_map/ppermute | solution.py:126
  10.9 0.9 broadcast_divide_fusion
  11.7 0.9 slice_bitcast_fusion.20
  12.6 0.8 slice_bitcast_fusion.22
  14.3 0.9 fusion.51
  17.3 0.9 bitcast_add_fusion
  22.4 1.0 concatenate.143
  24.1 1.0 concatenate.144
  31.6 0.9 fusion.92
  32.5 0.9 fusion.93
  35.9 1.0 copy.55
  36.8 15.8 %all-to-all-start = ((bf16[64,16,128]{2,1,0:T(8,128)(2,1)}), bf16[64,16,128]{2,1,0:T(8,128)(2,1)S(1)}, u32[]{:S(2)}, u32[]{:S(2)}) async-start(bf16[64,16,128]{2,1,0:T(8,128)(2,1)} %copy.55), calls=%async_computation | async-start | bytes 524288 | tf_op jit(solution)/shard_map/all_to_all | solution.py:26
  52.8 16.9 %all-to-all-done = bf16[64,16,128]{2,1,0:T(8,128)(2,1)S(1)} async-done(((bf16[64,16,128]{2,1,0:T(8,128)(2,1)}), bf16[64,16,128]{2,1,0:T(8,128)(2,1)S(1)}, u32[]{:S(2)}, u32[]{:S(2)}) %all-to-all-start) | async-done | bytes 262176 | tf_op jit(solution)/shard_map/all_to_all | solution.py:26
  70.0 1.1 fusion.1
  71.0 1.2 fusion
  75.6 21.4 %all_to_all.15 = bf16[64,16,96]{2,1,0:T(8,128)(2,1)S(1)} all-to-all(bf16[64,16,96]{2,1,0:T(8,128)(2,1)S(1)} %copy.65), channel_id=1, replica_groups=mesh['exc'=8,'line'=64] {'line'}, dimensions={0} | all-to-all | bytes 393216 | tf_op jit(solution)/shard_map/all_to_all | solution.py:26
  100.6 0.9 copy.73
  101.5 4.6 %all-to-all-start.2 = ((bf16[64,16,96]{2,1,0:T(8,128)(2,1)}), bf16[64,16,96]{2,1,0:T(8,128)(2,1)S(1)}, u32[]{:S(2)}, u32[]{:S(2)}) async-start(bf16[64,16,96]{2,1,0:T(8,128)(2,1)} %copy.73), calls=%async_computation.2 | async-start | bytes 524288 | tf_op jit(solution)/shard_map/all_to_all | solution.py:26
  106.2 1.0 slice_convert_fusion.1
  107.1 16.1 %all-to-all-done.2 = bf16[64,16,96]{2,1,0:T(8,128)(2,1)S(1)} async-done(((bf16[64,16,96]{2,1,0:T(8,128)(2,1)}), bf16[64,16,96]{2,1,0:T(8,128)(2,1)S(1)}, u32[]{:S(2)}, u32[]{:S(2)}) %all-to-all-start.2) | async-done | bytes 196640 | tf_op jit(solution)/shard_map/all_to_all | solution.py:26
  124.0 1.6 %fusion.2 = f32[48,1024]{1,0:T(8,128)} fusion(bf16[1024,1024]{1,0:T(8,128)(2,1)S(1)} %copy-done, bf16[1024,96]{1,0:T(8,128)(2,1)S(1)} %bitcast.378), kind=kOutput, calls=%fused_computation.4 | convolution fusion | flops 100663296 | bytes 2490368 | tf_op jit(solution)/shard_map/dot_general | solution.py:35
  (170 shorter events, 24.3 us)
Async XLA Ops:
  0.6 17.9 %copy-start = (bf16[1024,1024]{1,0:T(8,128)(2,1)S(1)}, bf16[1024,1024]{1,0:T(8,128)(2,1)}, u32[]{:S(2)}) copy-start(bf16[1024,1024]{1,0:T(8,128)(2,1)} %param.14) | copy-start | bytes 6291460
  4.9 25.8 %collective-permute-start = (f32[9,1,1,1024]{3,0,2,1:T(8,128)}, f32[9,1,1,1024]{3,0,2,1:T(8,128)}, u32[]{:S(2)}, u32[]{:S(2)}) collective-permute-start(f32[9,1,1,1024]{3,0,2,1:T(8,128)} %pad_maximum_fusion.4), channel_id=1, source_target_pairs={{0,1},{1,2},{2,3},{3,4},{4,5},{5,6},{6,7},{7,8},{8,9},{9,10},{10,1... | collective-permute-start | bytes 110600 | tf_op jit(solution)/shard_map/ppermute | solution.py:126
  14.3 4.1 %copy-start.4 = (bf16[1,16,1024]{2,1,0:T(8,128)(2,1)}, bf16[1,16,1024]{2,1,0:T(8,128)(2,1)S(1)}, u32[]{:S(2)}) copy-start(bf16[1,16,1024]{2,1,0:T(8,128)(2,1)S(1)} %fusion.50) | copy-start | bytes 98308
  15.2 3.3 %copy-start.3 = (bf16[1,16,1024]{2,1,0:T(8,128)(2,1)}, bf16[1,16,1024]{2,1,0:T(8,128)(2,1)S(1)}, u32[]{:S(2)}) copy-start(bf16[1,16,1024]{2,1,0:T(8,128)(2,1)S(1)} %fusion.51) | copy-start | bytes 98308
  21.0 8.1 %copy-start.6 = (f32[1024]{0:T(1024)S(1)}, f32[1024]{0:T(1024)}, u32[]{:S(2)}) copy-start(f32[1024]{0:T(1024)} %param.16) | copy-start | bytes 12292
  36.8 32.9 %all-to-all-start = ((bf16[64,16,128]{2,1,0:T(8,128)(2,1)}), bf16[64,16,128]{2,1,0:T(8,128)(2,1)S(1)}, u32[]{:S(2)}, u32[]{:S(2)}) async-start(bf16[64,16,128]{2,1,0:T(8,128)(2,1)} %copy.55), calls=%async_computation | async-start | bytes 524288 | tf_op jit(solution)/shard_map/all_to_all | solution.py:26
  75.4 22.5 %copy-start.2 = (f32[1,16,1024]{2,1,0:T(8,128)S(1)}, f32[1,16,1024]{2,1,0:T(8,128)}, u32[]{:S(2)}) copy-start(f32[1,16,1024]{2,1,0:T(8,128)} %param.12) | copy-start | bytes 196612
  101.5 21.7 %all-to-all-start.2 = ((bf16[64,16,96]{2,1,0:T(8,128)(2,1)}), bf16[64,16,96]{2,1,0:T(8,128)(2,1)S(1)}, u32[]{:S(2)}, u32[]{:S(2)}) async-start(bf16[64,16,96]{2,1,0:T(8,128)(2,1)} %copy.73), calls=%async_computation.2 | async-start | bytes 524288 | tf_op jit(solution)/shard_map/all_to_all | solution.py:26
  123.2 2.4 %copy-start.5 = (s32[1,16,1024]{2,1,0:T(8,128)S(1)}, s32[1,16,1024]{2,1,0:T(8,128)}, u32[]{:S(2)}) copy-start(s32[1,16,1024]{2,1,0:T(8,128)} %param.13) | copy-start | bytes 196612
  123.9 2.3 %copy-start.1 = (f32[48,1024]{1,0:T(8,128)}, f32[48,1024]{1,0:T(8,128)S(1)}, u32[]{:S(2)}) copy-start(f32[48,1024]{1,0:T(8,128)S(1)} %fusion.4) | copy-start | bytes 589828

commit v6 on v3

--- a/solution.py
+++ b/solution.py
@@ -2,6 +2,7 @@
 import jax.numpy as jnp
 from jax import lax
 from jax.sharding import PartitionSpec as P
+from jax.experimental import pallas as pl
 
 COURANT = 0.4
 
@@ -14,12 +15,25 @@
     return solved.reshape(rounded.shape)
 
 
+def _pack_kernel(x_ref, o_ref):
+    comps = x_ref.shape[0]
+    blocks = o_ref.shape[0]
+    width = o_ref.shape[2] // comps
+    for c in range(comps):
+        values = x_ref[c]
+        for e in range(blocks):
+            o_ref[e, :, c * width : (c + 1) * width] = values[:, e * width : (e + 1) * width]
+
+
 def turn_rows(block, line_count):
     comps, strip, cells = block.shape
-    parts = block.reshape(comps, strip, line_count, strip)
-    parts = jnp.transpose(parts, (2, 1, 0, 3)).reshape(line_count, strip, comps * strip)
-    parts = lax.all_to_all(parts, "line", 0, 0, tiled=True)
-    return parts.reshape(line_count * strip, comps * strip)
+    width = cells // line_count
+    parts = pl.pallas_call(
+        _pack_kernel,
+        out_shape=jax.ShapeDtypeStruct((line_count, strip, comps * width), block.dtype),
+    )(block)
+    parts = lax.all_to_all(parts.astype(jnp.bfloat16), "line", 0, 0, tiled=True)
+    return parts.reshape(line_count * strip, comps * width)
 
 
 def solve_turned(turned, inverse):
@@ -155,7 +169,7 @@
             ex, ey, ez, hx, hy, hz = fields
             ez = ez + (amplitude * column_local[None, :, None]) * port_mode[None, None, :]
             fields = curl_y((ex, ey, ez, hx, hy, hz), COURANT * inverse_cols, 2)
-            rounded = jnp.stack(fields).reshape(comps, strip, line_cells).astype(jnp.bfloat16)
+            rounded = jnp.stack(fields).reshape(comps, strip, line_cells)
             solved = solve_turned(turn_rows(rounded, line_count), inverse)
         else:
             rounded = jnp.stack(fields).astype(jnp.bfloat16)
@@ -167,7 +181,7 @@
         stacked = jnp.stack(fields).reshape(comps, strip, line_cells)
         if inverse_cols is None:
             stacked = jnp.concatenate([stacked] + bf16_parts(inverse_rows), 0)
-        turned = turn_rows(stacked.astype(jnp.bfloat16), line_count)
+        turned = turn_rows(stacked, line_count)
         if inverse_cols is None:
             width = eps_planes * strip
             pieces = [

time: 112 us -> 118 us (1.054)
  local copies, waits for them, and re-layouts: 12.7 us -> 4.62 us
  Pallas kernels: 0 us -> 8.01 us
  other arithmetic: 6.68 us -> 12.5 us
    pallas_call x0 -> x3, Pallas kernels: none -> 8.01 us  [turn_rows(): pl.pallas_call(_pack_kernel, out_shape=jax.ShapeDtypeStruct((line_count,...]
    another operation x38 -> x0, local copies, waits for them, and re-layouts: 6.35 us -> none  [the longest x25 4.22 us: per_device(): stacked = jnp.stack(fields).reshape(comps, strip, line_cells)]
    convert_element_type x0 -> x3, other arithmetic: none -> 4.67 us  [turn_rows(): parts = lax.all_to_all(parts.astype(jnp.bfloat16), 'line', 0, 0, tiled=True)]
    reshape x3 -> x0, local copies, waits for them, and re-layouts: 2.17 us -> none  [turn_rows(): jnp.transpose(parts, (2, 1, 0, 3)).reshape(line_count, strip, comps * strip)]
    unnamed x37 -> x26, local copies, waits for them, and re-layouts: 0.57 us -> 1.88 us
where the time goes in v6:
time: 118 us; the launch traced here: 117 us
  waiting for transfers between devices  45.4 us (38%)
  blocking collectives  20.4 us (17%)
  starting transfers between devices  19.7 us (17%)
  other arithmetic  12.5 us (11%)
  Pallas kernels  8.01 us (7%)
  local copies, waits for them, and re-layouts  4.62 us (4%)
  matrix products  3.49 us (3%)
  between operations  2.69 us (2%)
    all_to_all x2, waiting for transfers between devices, turn_rows(): parts = lax.all_to_all(parts.astype(jnp.bfloat16), 'line', 0, 0, tiled=True)  32.5 us
    all_to_all x1, blocking collectives, turn_rows(): parts = lax.all_to_all(parts.astype(jnp.bfloat16), 'line', 0, 0, tiled=True)  20.4 us
    ppermute x1, waiting for transfers between devices, per_device(): message = lax.ppermute(message, 'line', ring)  12.9 us
    all_to_all x2, starting transfers between devices, turn_rows(): parts = lax.all_to_all(parts.astype(jnp.bfloat16), 'line', 0, 0, tiled=True)  12.8 us
    pallas_call x3, Pallas kernels, turn_rows(): pl.pallas_call(_pack_kernel, out_shape=jax.ShapeDtypeStruct((line_count,...  8.01 us
    ppermute x1, starting transfers between devices, per_device(): message = lax.ppermute(message, 'line', ring)  6.83 us
    convert_element_type x3, other arithmetic, turn_rows(): parts = lax.all_to_all(parts.astype(jnp.bfloat16), 'line', 0, 0, tiled=True)  4.67 us
    dot_general x3, matrix products, solve_turned(): lax.dot_general(turned, inverse, (((0,), (1,)), ((), ())), preferred_elem...  2.71 us
  transfers between devices with their start and end apart: 3, of which 3 were waited for; matrix products, arithmetic and copies ran while one was open for 0% of the time, Pallas kernels for 0%

profile of v6, /device:TPU:8, one launch (start us, length us, event | category | flops | bytes accessed | tf_op | source)
XLA Modules:
  0.0 116.8 jit_solution(6456816445271785059)
XLA Ops:
  2.2 0.9 slice_bitcast_fusion.25
  3.1 0.9 slice_bitcast_fusion.23
  4.0 0.9 broadcast_multiply_fusion
  4.9 0.8 dynamic-slice_multiply_fusion
  5.6 0.9 bitcast_add_fusion
  6.7 6.8 %collective-permute-start = (f32[9,1,1,1024]{3,2,1,0:T(1,128)S(1)}, f32[9,1,1,1024]{3,2,1,0:T(1,128)S(1)}, u32[]{:S(2)}, u32[]{:S(2)}) collective-permute-start(f32[9,1,1,1024]{3,2,1,0:T(1,128)S(1)} %constant_dynamic-update-slice_fusion), channel_id=1, source_target_pairs={{0,1},{1,2},{2,3},{3,4},{4,5},{5,6},{6,7},{7,8},{8,9},{9,10},{10,1... | collective-permute-start | bytes 110600 | tf_op jit(solution)/shard_map/ppermute | solution.py:138
  13.6 12.9 %collective-permute-done = f32[9,1,1,1024]{3,2,1,0:T(1,128)S(1)} collective-permute-done((f32[9,1,1,1024]{3,2,1,0:T(1,128)S(1)}, f32[9,1,1,1024]{3,2,1,0:T(1,128)S(1)}, u32[]{:S(2)}, u32[]{:S(2)}) %collective-permute-start) | collective-permute-done | bytes 36896 | tf_op jit(solution)/shard_map/ppermute | solution.py:138
  26.5 1.1 fusion.33
  27.9 0.8 fusion.77
  29.1 0.9 pad_maximum_fusion.x_ref
  30.0 2.9 %shard_map.112 = f32[64,16,128]{2,1,0:T(8,128)} custom-call(f32[8,16,1024]{2,1,0:T(8,128)} %pad_maximum_fusion.x_ref), custom_call_target="tpu_custom_call" | custom-call | tf_op jit(solution)/shard_map/pallas_call | solution.py:31
  32.9 1.8 %convert_element_type.60 = bf16[64,16,128]{2,1,0:T(8,128)(2,1)} convert(f32[64,16,128]{2,1,0:T(8,128)} %shard_map.112) | non-fusion elementwise | flops 131072 | bytes 786432 | tf_op jit(solution)/shard_map/convert_element_type | solution.py:35
  34.6 8.2 %all-to-all-start = ((bf16[64,16,128]{2,1,0:T(8,128)(2,1)}), bf16[64,16,128]{2,1,0:T(8,128)(2,1)S(1)}, u32[]{:S(2)}, u32[]{:S(2)}) async-start(bf16[64,16,128]{2,1,0:T(8,128)(2,1)} %convert_element_type.60), calls=%async_computation | async-start | bytes 524288 | tf_op jit(solution)/shard_map/all_to_all | solution.py:35
  43.1 16.7 %all-to-all-done = bf16[64,16,128]{2,1,0:T(8,128)(2,1)S(1)} async-done(((bf16[64,16,128]{2,1,0:T(8,128)(2,1)}), bf16[64,16,128]{2,1,0:T(8,128)(2,1)S(1)}, u32[]{:S(2)}, u32[]{:S(2)}) %all-to-all-start) | async-done | bytes 262176 | tf_op jit(solution)/shard_map/all_to_all | solution.py:35
  60.3 1.1 fusion
  62.9 2.6 %shard_map.113 = f32[64,16,96]{2,1,0:T(8,128)} custom-call(f32[6,16,1024]{2,1,0:T(8,128)} %bitcast.410), custom_call_target="tpu_custom_call" | custom-call | tf_op jit(solution)/shard_map/pallas_call | solution.py:31
  65.5 1.1 convert_element_type.63
  66.6 20.4 %all_to_all.15 = bf16[64,16,96]{2,1,0:T(8,128)(2,1)S(1)} all-to-all(bf16[64,16,96]{2,1,0:T(8,128)(2,1)S(1)} %convert_element_type.63), channel_id=1, replica_groups=mesh['exc'=8,'line'=64] {'line'}, dimensions={0} | all-to-all | bytes 393216 | tf_op jit(solution)/shard_map/all_to_all | solution.py:35
  87.0 0.8 fusion.78
  89.1 2.6 %shard_map.114 = f32[64,16,96]{2,1,0:T(8,128)} custom-call(f32[6,16,1024]{2,1,0:T(8,128)} %bitcast.409), custom_call_target="tpu_custom_call" | custom-call | tf_op jit(solution)/shard_map/pallas_call | solution.py:31
  91.6 1.8 %convert_element_type.64 = bf16[64,16,96]{2,1,0:T(8,128)(2,1)} convert(f32[64,16,96]{2,1,0:T(8,128)} %shard_map.114) | non-fusion elementwise | flops 98304 | bytes 589824 | tf_op jit(solution)/shard_map/convert_element_type | solution.py:35
  93.4 4.6 %all-to-all-start.2 = ((bf16[64,16,96]{2,1,0:T(8,128)(2,1)}), bf16[64,16,96]{2,1,0:T(8,128)(2,1)S(1)}, u32[]{:S(2)}, u32[]{:S(2)}) async-start(bf16[64,16,96]{2,1,0:T(8,128)(2,1)} %convert_element_type.64), calls=%async_computation.2 | async-start | bytes 524288 | tf_op jit(solution)/shard_map/all_to_all | solution.py:35
  98.1 15.8 %all-to-all-done.2 = bf16[64,16,96]{2,1,0:T(8,128)(2,1)S(1)} async-done(((bf16[64,16,96]{2,1,0:T(8,128)(2,1)}), bf16[64,16,96]{2,1,0:T(8,128)(2,1)S(1)}, u32[]{:S(2)}, u32[]{:S(2)}) %all-to-all-start.2) | async-done | bytes 196640 | tf_op jit(solution)/shard_map/all_to_all | solution.py:35
  113.9 0.8 fusion.79
  (79 shorter events, 6.2 us)
Async XLA Ops:
  0.6 27.2 %copy-start = (bf16[1024,1024]{1,0:T(8,128)(2,1)S(1)}, bf16[1024,1024]{1,0:T(8,128)(2,1)}, u32[]{:S(2)}) copy-start(bf16[1024,1024]{1,0:T(8,128)(2,1)} %param.14) | copy-start | bytes 6291460
  6.7 19.8 %collective-permute-start = (f32[9,1,1,1024]{3,2,1,0:T(1,128)S(1)}, f32[9,1,1,1024]{3,2,1,0:T(1,128)S(1)}, u32[]{:S(2)}, u32[]{:S(2)}) collective-permute-start(f32[9,1,1,1024]{3,2,1,0:T(1,128)S(1)} %constant_dynamic-update-slice_fusion), channel_id=1, source_target_pairs={{0,1},{1,2},{2,3},{3,4},{4,5},{5,6},{6,7},{7,8},{8,9},{9,10},{10,1... | collective-permute-start | bytes 110600 | tf_op jit(solution)/shard_map/ppermute | solution.py:138
  34.6 25.2 %all-to-all-start = ((bf16[64,16,128]{2,1,0:T(8,128)(2,1)}), bf16[64,16,128]{2,1,0:T(8,128)(2,1)S(1)}, u32[]{:S(2)}, u32[]{:S(2)}) async-start(bf16[64,16,128]{2,1,0:T(8,128)(2,1)} %convert_element_type.60), calls=%async_computation | async-start | bytes 524288 | tf_op jit(solution)/shard_map/all_to_all | solution.py:35
  60.3 1.4 %copy-start.6 = (f32[1024]{0:T(1024)S(1)}, f32[1024]{0:T(1024)}, u32[]{:S(2)}) copy-start(f32[1024]{0:T(1024)} %param.16) | copy-start | bytes 12292
  62.1 0.8 copy-start.3
  65.5 22.3 %copy-start.1 = (f32[1,16,1024]{2,1,0:T(8,128)S(1)}, f32[1,16,1024]{2,1,0:T(8,128)}, u32[]{:S(2)}) copy-start(f32[1,16,1024]{2,1,0:T(8,128)} %param.12) | copy-start | bytes 196612
  87.8 10.2 %copy-start.4 = (bf16[2,3,1,16,1024]{4,3,2,1,0:T(8,128)(2,1)S(1)}, bf16[2,3,1,16,1024]{4,3,2,1,0:T(8,128)(2,1)}, u32[]{:S(2)}) copy-start(bf16[2,3,1,16,1024]{4,3,2,1,0:T(8,128)(2,1)} %param.11) | copy-start | bytes 589828
  88.3 0.8 copy-start.2
  93.4 20.5 %all-to-all-start.2 = ((bf16[64,16,96]{2,1,0:T(8,128)(2,1)}), bf16[64,16,96]{2,1,0:T(8,128)(2,1)S(1)}, u32[]{:S(2)}, u32[]{:S(2)}) async-start(bf16[64,16,96]{2,1,0:T(8,128)(2,1)} %convert_element_type.64), calls=%async_computation.2 | async-start | bytes 524288 | tf_op jit(solution)/shard_map/all_to_all | solution.py:35
  98.1 16.7 %copy-start.5 = (s32[1,16,1024]{2,1,0:T(8,128)S(1)}, s32[1,16,1024]{2,1,0:T(8,128)}, u32[]{:S(2)}) copy-start(s32[1,16,1024]{2,1,0:T(8,128)} %param.13) | copy-start | bytes 196612

commit v7 on v3

--- a/solution.py
+++ b/solution.py
@@ -109,6 +109,12 @@
     gradient = jnp.zeros(design_mask.shape, jnp.float32)
     comps = 6 * planes
 
+    ring = [(i, (i + 1) % line_count) for i in range(line_count)]
+    eps_planes_b = jnp.broadcast_to(permittivity, adj_e[0].shape)
+    message = jnp.concatenate(
+        [adj_e[:, :, -1:], adj_h[:, :, -1:], eps_planes_b[None, :, -1:], adj_h[::2, :, -2:-1]], 0
+    )
+    message = lax.ppermute(message, "line", ring)
     column = (jnp.arange(line_cells, dtype=jnp.int32) == plane_at).astype(jnp.float32)
     profile_rows = lax.dynamic_slice_in_dim(port_mode, offset, strip)
     amplitude = jnp.cos(frequency * 1.0)
@@ -116,13 +122,12 @@
     hx, hy, hz = adj_h[0], adj_h[1], adj_h[2]
     ez = ez + (amplitude * profile_rows[None, :, None]) * column[None, None, :]
     is_first = index == 0
-    ring = [(i, (i + 1) % line_count) for i in range(line_count)]
-    scaled_planes = jnp.broadcast_to(scaled_rows, ex.shape)
-    message = jnp.stack(
-        [f[:, -1:] for f in (ex, ey, ez, hx, hy, hz, scaled_planes)] + [hx[:, -2:-1], hz[:, -2:-1]]
-    )
-    message = lax.ppermute(message, "line", ring)
-    p_ex, p_ey, p_ez, p_hx, p_hy, p_hz, p_r, p_hx2, p_hz2 = (message[i] for i in range(9))
+    p_ex, p_ey, p_ez, p_hx, p_hy, p_hz = (message[i] for i in range(6))
+    p_eps, p_hx2, p_hz2 = message[6], message[7], message[8]
+    row_before = (offset + line_cells - 1) % line_cells
+    profile_before = lax.dynamic_slice_in_dim(port_mode, row_before, 1)
+    p_ez = p_ez + (amplitude * profile_before[None, :, None]) * column[None, None, :]
+    p_r = COURANT * (1.0 / p_eps)
     zero_row = jnp.zeros_like(p_hx)
     hx_prev = shift_down(hx, 1, jnp.where(is_first, zero_row, p_hx))
     hz_prev = shift_down(hz, 1, jnp.where(is_first, zero_row, p_hz))

time: 112 us -> 117 us (1.045)
  local copies, waits for them, and re-layouts: 12.7 us -> 21.8 us
  waiting for transfers between devices: 45.4 us -> 40.9 us
    ppermute x1, waiting for transfers between devices: 12.9 us -> 7.59 us  [per_device(): message = lax.ppermute(message, 'line', ring)]
    slice x2 -> x3, local copies, waits for them, and re-layouts: 0.01 us -> 2.81 us  [the longest x1 1.06 us: per_device(): adj_h[:, :, -1:]]
    another operation x25, local copies, waits for them, and re-layouts: 4.22 us -> 5.7 us  [per_device(): stacked = jnp.stack(fields).reshape(comps, strip, line_cells)]
    another operation x13, local copies, waits for them, and re-layouts: 2.13 us -> 3.6 us  [per_device(): jnp.stack(fields).reshape(comps, strip, line_cells).astype(jnp.bfloat16)]
    dynamic_slice x0 -> x1, local copies, waits for them, and re-layouts: none -> 1.27 us  [per_device(): profile_before = lax.dynamic_slice_in_dim(port_mode, row_before, 1)]
  transfers between devices with their start and end apart: 3 -> 3, of which waited for: 3 -> 3; matrix products, arithmetic and copies ran while one was open for 0% -> 6% of each run, Pallas kernels for 0% -> 0%
where the time goes in v7:
time: 117 us; the launch traced here: 116 us
  waiting for transfers between devices  40.9 us (35%)
  local copies, waits for them, and re-layouts  21.8 us (19%)
  blocking collectives  20.5 us (18%)
  starting transfers between devices  19.3 us (16%)
  other arithmetic  5.9 us (5%)
  matrix products  4.42 us (4%)
  between operations  3.47 us (3%)
    all_to_all x2, waiting for transfers between devices, turn_rows(): parts = lax.all_to_all(parts, 'line', 0, 0, tiled=True)  33.3 us
    all_to_all x1, blocking collectives, turn_rows(): parts = lax.all_to_all(parts, 'line', 0, 0, tiled=True)  20.5 us
    all_to_all x2, starting transfers between devices, turn_rows(): parts = lax.all_to_all(parts, 'line', 0, 0, tiled=True)  12.4 us
    ppermute x1, waiting for transfers between devices, per_device(): message = lax.ppermute(message, 'line', ring)  7.59 us
    ppermute x1, starting transfers between devices, per_device(): message = lax.ppermute(message, 'line', ring)  6.83 us
    another operation x25, local copies, waits for them, and re-layouts, per_device(): stacked = jnp.stack(fields).reshape(comps, strip, line_cells)  5.7 us
    dot_general x3, matrix products, solve_turned(): lax.dot_general(turned, inverse, (((0,), (1,)), ((), ())), preferred_elem...  3.65 us
    another operation x13, local copies, waits for them, and re-layouts, per_device(): jnp.stack(fields).reshape(comps, strip, line_cells).astype(jnp.bfloat16)  3.6 us
  transfers between devices with their start and end apart: 3, of which 3 were waited for; matrix products, arithmetic and copies ran while one was open for 6% of the time, Pallas kernels for 0%

profile of v7, /device:TPU:8, one launch (start us, length us, event | category | flops | bytes accessed | tf_op | source)
XLA Modules:
  0.0 116.2 jit_solution(16987296035381735126)
XLA Ops:
  0.6 1.1 slice.303
  1.7 0.9 slice.305
  2.5 0.9 slice.302
  4.3 6.8 %collective-permute-start = (f32[9,1,1,1024]{3,0,2,1:T(8,128)S(1)}, f32[9,1,1,1024]{3,0,2,1:T(8,128)S(1)}, u32[]{:S(2)}, u32[]{:S(2)}) collective-permute-start(f32[9,1,1,1024]{3,0,2,1:T(8,128)S(1)} %pad_maximum_fusion.2), channel_id=1, source_target_pairs={{0,1},{1,2},{2,3},{3,4},{4,5},{5,6},{6,7},{7,8},{8,9},{9,10},{10,1... | collective-permute-start | bytes 110600 | tf_op jit(solution)/shard_map/ppermute | solution.py:117
  11.1 0.9 slice_bitcast_fusion.21
  12.0 0.8 fusion.47
  12.9 0.8 fusion.48
  15.9 1.3 %dynamic_slice.6 = f32[1]{0:T(128)} dynamic-slice(f32[1024]{0:T(1024)} %param.16, s32[]{:T(128)S(6)} %select_n.70), dynamic_slice_sizes={1} | dynamic-slice | bytes 12 | tf_op jit(solution)/shard_map/dynamic_slice | solution.py:128
  17.8 7.6 %collective-permute-done = f32[9,1,1,1024]{3,0,2,1:T(8,128)S(1)} collective-permute-done((f32[9,1,1,1024]{3,0,2,1:T(8,128)S(1)}, f32[9,1,1,1024]{3,0,2,1:T(8,128)S(1)}, u32[]{:S(2)}, u32[]{:S(2)}) %collective-permute-start) | collective-permute-done | bytes 36896 | tf_op jit(solution)/shard_map/ppermute | solution.py:117
  25.4 1.1 fusion.34
  31.1 1.0 copy.38
  32.1 7.8 %all-to-all-start = ((bf16[64,16,128]{2,1,0:T(8,128)(2,1)}), bf16[64,16,128]{2,1,0:T(8,128)(2,1)S(1)}, u32[]{:S(2)}, u32[]{:S(2)}) async-start(bf16[64,16,128]{2,1,0:T(8,128)(2,1)} %copy.38), calls=%async_computation | async-start | bytes 524288 | tf_op jit(solution)/shard_map/all_to_all | solution.py:21
  39.9 0.8 slice.343
  40.8 16.8 %all-to-all-done = bf16[64,16,128]{2,1,0:T(8,128)(2,1)S(1)} async-done(((bf16[64,16,128]{2,1,0:T(8,128)(2,1)}), bf16[64,16,128]{2,1,0:T(8,128)(2,1)S(1)}, u32[]{:S(2)}, u32[]{:S(2)}) %all-to-all-start) | async-done | bytes 262176 | tf_op jit(solution)/shard_map/all_to_all | solution.py:21
  57.8 2.1 %fusion = f32[96,1024]{1,0:T(8,128)S(1)} fusion(bf16[1024,1023]{1,0:T(8,128)(2,1)S(1)} %bitcast.317, bf16[1024,1]{1,0:T(8,128)(2,1)} %slice.343, bf16[1024,128]{1,0:T(8,128)(2,1)S(1)} %bitcast.319), kind=kOutput, calls=%fused_computation | convolution fusion | flops 205520896 | bytes 2752512 | tf_op jit(solution)/shard_map/dot_general | solution.py:26
  63.6 0.9 constant_dynamic-update-slice_fusion.14
  64.8 20.5 %all_to_all.15 = bf16[64,16,96]{2,1,0:T(8,128)(2,1)S(1)} all-to-all(bf16[64,16,96]{2,1,0:T(8,128)(2,1)S(1)} %copy.48), channel_id=1, replica_groups=mesh['exc'=8,'line'=64] {'line'}, dimensions={0} | all-to-all | bytes 393216 | tf_op jit(solution)/shard_map/all_to_all | solution.py:21
  85.2 0.8 fusion.89
  89.3 0.9 constant_dynamic-update-slice_fusion.20
  90.2 0.9 copy.56
  91.2 4.6 %all-to-all-start.2 = ((bf16[64,16,96]{2,1,0:T(8,128)(2,1)}), bf16[64,16,96]{2,1,0:T(8,128)(2,1)S(1)}, u32[]{:S(2)}, u32[]{:S(2)}) async-start(bf16[64,16,96]{2,1,0:T(8,128)(2,1)} %copy.56), calls=%async_computation.2 | async-start | bytes 524288 | tf_op jit(solution)/shard_map/all_to_all | solution.py:21
  95.8 1.0 slice_convert_fusion.1
  96.8 16.5 %all-to-all-done.2 = bf16[64,16,96]{2,1,0:T(8,128)(2,1)S(1)} async-done(((bf16[64,16,96]{2,1,0:T(8,128)(2,1)}), bf16[64,16,96]{2,1,0:T(8,128)(2,1)S(1)}, u32[]{:S(2)}, u32[]{:S(2)}) %all-to-all-start.2) | async-done | bytes 196640 | tf_op jit(solution)/shard_map/all_to_all | solution.py:21
  113.3 0.8 fusion.90
  (121 shorter events, 15.3 us)
Async XLA Ops:
  0.6 26.2 %copy-start = (bf16[1024,1024]{1,0:T(8,128)(2,1)S(1)}, bf16[1024,1024]{1,0:T(8,128)(2,1)}, u32[]{:S(2)}) copy-start(bf16[1024,1024]{1,0:T(8,128)(2,1)} %param.14) | copy-start | bytes 6291460
  4.3 21.1 %collective-permute-start = (f32[9,1,1,1024]{3,0,2,1:T(8,128)S(1)}, f32[9,1,1,1024]{3,0,2,1:T(8,128)S(1)}, u32[]{:S(2)}, u32[]{:S(2)}) collective-permute-start(f32[9,1,1,1024]{3,0,2,1:T(8,128)S(1)} %pad_maximum_fusion.2), channel_id=1, source_target_pairs={{0,1},{1,2},{2,3},{3,4},{4,5},{5,6},{6,7},{7,8},{8,9},{9,10},{10,1... | collective-permute-start | bytes 110600 | tf_op jit(solution)/shard_map/ppermute | solution.py:117
  32.1 25.5 %all-to-all-start = ((bf16[64,16,128]{2,1,0:T(8,128)(2,1)}), bf16[64,16,128]{2,1,0:T(8,128)(2,1)S(1)}, u32[]{:S(2)}, u32[]{:S(2)}) async-start(bf16[64,16,128]{2,1,0:T(8,128)(2,1)} %copy.38), calls=%async_computation | async-start | bytes 524288 | tf_op jit(solution)/shard_map/all_to_all | solution.py:21
  57.8 2.5 %copy-start.3 = (f32[1024]{0:T(1024)S(1)}, f32[1024]{0:T(1024)}, u32[]{:S(2)}) copy-start(f32[1024]{0:T(1024)} %param.16) | copy-start | bytes 12292
  64.5 21.6 %copy-start.1 = (f32[1,16,1024]{2,1,0:T(8,128)S(1)}, f32[1,16,1024]{2,1,0:T(8,128)}, u32[]{:S(2)}) copy-start(f32[1,16,1024]{2,1,0:T(8,128)} %param.12) | copy-start | bytes 196612
  91.2 22.1 %all-to-all-start.2 = ((bf16[64,16,96]{2,1,0:T(8,128)(2,1)}), bf16[64,16,96]{2,1,0:T(8,128)(2,1)S(1)}, u32[]{:S(2)}, u32[]{:S(2)}) async-start(bf16[64,16,96]{2,1,0:T(8,128)(2,1)} %copy.56), calls=%async_computation.2 | async-start | bytes 524288 | tf_op jit(solution)/shard_map/all_to_all | solution.py:21
  95.8 18.3 %copy-start.2 = (s32[1,16,1024]{2,1,0:T(8,128)S(1)}, s32[1,16,1024]{2,1,0:T(8,128)}, u32[]{:S(2)}) copy-start(s32[1,16,1024]{2,1,0:T(8,128)} %param.13) | copy-start | bytes 196612

commit v8 on v3

--- a/solution.py
+++ b/solution.py
@@ -2,6 +2,7 @@
 import jax.numpy as jnp
 from jax import lax
 from jax.sharding import PartitionSpec as P
+from jax.experimental.layout import Layout, with_layout_constraint
 
 COURANT = 0.4
 
@@ -16,6 +17,7 @@
 
 def turn_rows(block, line_count):
     comps, strip, cells = block.shape
+    block = with_layout_constraint(block, Layout(major_to_minor=(0, 1, 2)))
     parts = block.reshape(comps, strip, line_count, strip)
     parts = jnp.transpose(parts, (2, 1, 0, 3)).reshape(line_count, strip, comps * strip)
     parts = lax.all_to_all(parts, "line", 0, 0, tiled=True)

time: 112 us -> 118 us (1.054)
  local copies, waits for them, and re-layouts: 12.7 us -> 18.3 us
    reshape x0 -> x3, local copies, waits for them, and re-layouts: none -> 7.62 us  [turn_rows(): parts = block.reshape(comps, strip, line_count, strip)]
    another operation x38 -> x0, local copies, waits for them, and re-layouts: 6.35 us -> none  [the longest x25 4.22 us: per_device(): stacked = jnp.stack(fields).reshape(comps, strip, line_cells)]
    transpose x3, local copies, waits for them, and re-layouts: 0.1 us -> 5.36 us  [turn_rows(): jnp.transpose(parts, (2, 1, 0, 3)).reshape(line_count, strip, comps * strip)]
where the time goes in v8:
time: 118 us; the launch traced here: 117 us
  waiting for transfers between devices  45.4 us (38%)
  blocking collectives  20.4 us (17%)
  starting transfers between devices  19.7 us (17%)
  local copies, waits for them, and re-layouts  18.3 us (16%)
  other arithmetic  7.02 us (6%)
  matrix products  3.48 us (3%)
  between operations  2.73 us (2%)
    all_to_all x2, waiting for transfers between devices, turn_rows(): parts = lax.all_to_all(parts, 'line', 0, 0, tiled=True)  32.5 us
    all_to_all x1, blocking collectives, turn_rows(): parts = lax.all_to_all(parts, 'line', 0, 0, tiled=True)  20.4 us
    ppermute x1, waiting for transfers between devices, per_device(): message = lax.ppermute(message, 'line', ring)  12.9 us
    all_to_all x2, starting transfers between devices, turn_rows(): parts = lax.all_to_all(parts, 'line', 0, 0, tiled=True)  12.8 us
    reshape x3, local copies, waits for them, and re-layouts, turn_rows(): parts = block.reshape(comps, strip, line_count, strip)  7.62 us
    ppermute x1, starting transfers between devices, per_device(): message = lax.ppermute(message, 'line', ring)  6.83 us
    transpose x3, local copies, waits for them, and re-layouts, turn_rows(): jnp.transpose(parts, (2, 1, 0, 3)).reshape(line_count, strip, comps * strip)  5.36 us
    dot_general x3, matrix products, solve_turned(): lax.dot_general(turned, inverse, (((0,), (1,)), ((), ())), preferred_elem...  2.7 us
  transfers between devices with their start and end apart: 3, of which 3 were waited for; matrix products, arithmetic and copies ran while one was open for 0% of the time, Pallas kernels for 0%

profile of v8, /device:TPU:8, one launch (start us, length us, event | category | flops | bytes accessed | tf_op | source)
XLA Modules:
  0.0 117.0 jit_solution(11548250064403139152)
XLA Ops:
  2.2 0.9 slice_bitcast_fusion.24
  3.1 0.9 slice_bitcast_fusion.22
  4.0 0.9 broadcast_multiply_fusion
  5.6 0.9 bitcast_add_fusion
  6.7 6.8 %collective-permute-start = (f32[9,1,1,1024]{3,2,1,0:T(1,128)S(1)}, f32[9,1,1,1024]{3,2,1,0:T(1,128)S(1)}, u32[]{:S(2)}, u32[]{:S(2)}) collective-permute-start(f32[9,1,1,1024]{3,2,1,0:T(1,128)S(1)} %constant_dynamic-update-slice_fusion), channel_id=1, source_target_pairs={{0,1},{1,2},{2,3},{3,4},{4,5},{5,6},{6,7},{7,8},{8,9},{9,10},{10,1... | collective-permute-start | bytes 110600 | tf_op jit(solution)/shard_map/ppermute | solution.py:126
  13.6 12.9 %collective-permute-done = f32[9,1,1,1024]{3,2,1,0:T(1,128)S(1)} collective-permute-done((f32[9,1,1,1024]{3,2,1,0:T(1,128)S(1)}, f32[9,1,1,1024]{3,2,1,0:T(1,128)S(1)}, u32[]{:S(2)}, u32[]{:S(2)}) %collective-permute-start) | collective-permute-done | bytes 36896 | tf_op jit(solution)/shard_map/ppermute | solution.py:126
  26.5 1.1 fusion.34
  27.9 0.8 fusion.88
  29.2 2.7 %reshape.471 = bf16[8,16,64,16]{3,2,1,0:T(8,128)(2,1)} reshape(bf16[8,16,1024]{2,1,0:T(8,128)(2,1)S(1)} %pad_maximum_fusion) | data formatting | bytes 524288 | tf_op jit(solution)/shard_map/reshape | solution.py:21
  31.9 2.0 %copy.40 = bf16[64,16,8,16]{0,3,2,1:T(8,128)(2,1)S(1)} copy(bf16[64,16,8,16]{3,0,1,2:T(8,128)(2,1)} %bitcast.435) | data formatting | bytes 524288 | tf_op jit(solution)/shard_map/transpose | solution.py:22
  33.8 1.0 copy.41
  34.8 8.2 %all-to-all-start = ((bf16[64,16,128]{2,1,0:T(8,128)(2,1)}), bf16[64,16,128]{2,1,0:T(8,128)(2,1)S(1)}, u32[]{:S(2)}, u32[]{:S(2)}) async-start(bf16[64,16,128]{2,1,0:T(8,128)(2,1)} %copy.41), calls=%async_computation | async-start | bytes 524288 | tf_op jit(solution)/shard_map/all_to_all | solution.py:23
  43.3 16.7 %all-to-all-done = bf16[64,16,128]{2,1,0:T(8,128)(2,1)S(1)} async-done(((bf16[64,16,128]{2,1,0:T(8,128)(2,1)}), bf16[64,16,128]{2,1,0:T(8,128)(2,1)S(1)}, u32[]{:S(2)}, u32[]{:S(2)}) %all-to-all-start) | async-done | bytes 262176 | tf_op jit(solution)/shard_map/all_to_all | solution.py:23
  60.4 1.1 fusion
  62.3 2.5 %reshape.474 = bf16[6,16,64,16]{3,2,1,0:T(8,128)(2,1)} reshape(bf16[6,16,1024]{2,1,0:T(8,128)(2,1)S(1)} %bitcast.450) | data formatting | bytes 393216 | tf_op jit(solution)/shard_map/reshape | solution.py:21
  64.8 1.7 %copy.44 = bf16[64,16,6,16]{0,3,2,1:T(8,128)(2,1)S(1)} copy(bf16[64,16,6,16]{3,0,1,2:T(8,128)(2,1)} %bitcast.436) | data formatting | bytes 393216 | tf_op jit(solution)/shard_map/transpose | solution.py:22
  66.7 20.4 %all_to_all.15 = bf16[64,16,96]{2,1,0:T(8,128)(2,1)S(1)} all-to-all(bf16[64,16,96]{2,1,0:T(8,128)(2,1)S(1)} %copy.45), channel_id=1, replica_groups=mesh['exc'=8,'line'=64] {'line'}, dimensions={0} | all-to-all | bytes 393216 | tf_op jit(solution)/shard_map/all_to_all | solution.py:23
  87.2 0.8 fusion.89
  88.5 2.5 %reshape.477 = bf16[6,16,64,16]{3,2,1,0:T(8,128)(2,1)} reshape(bf16[6,16,1024]{2,1,0:T(8,128)(2,1)S(1)} %bitcast.449) | data formatting | bytes 393216 | tf_op jit(solution)/shard_map/reshape | solution.py:21
  90.9 1.7 %copy.51 = bf16[64,16,6,16]{0,3,2,1:T(8,128)(2,1)S(1)} copy(bf16[64,16,6,16]{3,0,1,2:T(8,128)(2,1)} %bitcast.437) | data formatting | bytes 393216 | tf_op jit(solution)/shard_map/transpose | solution.py:22
  92.7 0.9 copy.52
  93.6 4.6 %all-to-all-start.2 = ((bf16[64,16,96]{2,1,0:T(8,128)(2,1)}), bf16[64,16,96]{2,1,0:T(8,128)(2,1)S(1)}, u32[]{:S(2)}, u32[]{:S(2)}) async-start(bf16[64,16,96]{2,1,0:T(8,128)(2,1)} %copy.52), calls=%async_computation.2 | async-start | bytes 524288 | tf_op jit(solution)/shard_map/all_to_all | solution.py:23
  98.3 15.8 %all-to-all-done.2 = bf16[64,16,96]{2,1,0:T(8,128)(2,1)S(1)} async-done(((bf16[64,16,96]{2,1,0:T(8,128)(2,1)}), bf16[64,16,96]{2,1,0:T(8,128)(2,1)S(1)}, u32[]{:S(2)}, u32[]{:S(2)}) %all-to-all-start.2) | async-done | bytes 196640 | tf_op jit(solution)/shard_map/all_to_all | solution.py:23
  114.1 0.8 fusion.90
  (78 shorter events, 5.7 us)
Async XLA Ops:
  0.6 27.2 %copy-start = (bf16[1024,1024]{1,0:T(8,128)(2,1)S(1)}, bf16[1024,1024]{1,0:T(8,128)(2,1)}, u32[]{:S(2)}) copy-start(bf16[1024,1024]{1,0:T(8,128)(2,1)} %param.14) | copy-start | bytes 6291460
  6.7 19.8 %collective-permute-start = (f32[9,1,1,1024]{3,2,1,0:T(1,128)S(1)}, f32[9,1,1,1024]{3,2,1,0:T(1,128)S(1)}, u32[]{:S(2)}, u32[]{:S(2)}) collective-permute-start(f32[9,1,1,1024]{3,2,1,0:T(1,128)S(1)} %constant_dynamic-update-slice_fusion), channel_id=1, source_target_pairs={{0,1},{1,2},{2,3},{3,4},{4,5},{5,6},{6,7},{7,8},{8,9},{9,10},{10,1... | collective-permute-start | bytes 110600 | tf_op jit(solution)/shard_map/ppermute | solution.py:126
  34.8 25.2 %all-to-all-start = ((bf16[64,16,128]{2,1,0:T(8,128)(2,1)}), bf16[64,16,128]{2,1,0:T(8,128)(2,1)S(1)}, u32[]{:S(2)}, u32[]{:S(2)}) async-start(bf16[64,16,128]{2,1,0:T(8,128)(2,1)} %copy.41), calls=%async_computation | async-start | bytes 524288 | tf_op jit(solution)/shard_map/all_to_all | solution.py:23
  60.4 1.4 %copy-start.4 = (f32[1024]{0:T(1024)S(1)}, f32[1024]{0:T(1024)}, u32[]{:S(2)}) copy-start(f32[1024]{0:T(1024)} %param.16) | copy-start | bytes 12292
  66.5 21.5 %copy-start.1 = (f32[1,16,1024]{2,1,0:T(8,128)S(1)}, f32[1,16,1024]{2,1,0:T(8,128)}, u32[]{:S(2)}) copy-start(f32[1,16,1024]{2,1,0:T(8,128)} %param.12) | copy-start | bytes 196612
  88.5 9.8 %copy-start.2 = (bf16[2,3,1,16,1024]{4,3,2,1,0:T(8,128)(2,1)S(1)}, bf16[2,3,1,16,1024]{4,3,2,1,0:T(8,128)(2,1)}, u32[]{:S(2)}) copy-start(bf16[2,3,1,16,1024]{4,3,2,1,0:T(8,128)(2,1)} %param.11) | copy-start | bytes 589828
  93.6 20.5 %all-to-all-start.2 = ((bf16[64,16,96]{2,1,0:T(8,128)(2,1)}), bf16[64,16,96]{2,1,0:T(8,128)(2,1)S(1)}, u32[]{:S(2)}, u32[]{:S(2)}) async-start(bf16[64,16,96]{2,1,0:T(8,128)(2,1)} %copy.52), calls=%async_computation.2 | async-start | bytes 524288 | tf_op jit(solution)/shard_map/all_to_all | solution.py:23
  98.2 16.7 %copy-start.3 = (s32[1,16,1024]{2,1,0:T(8,128)S(1)}, s32[1,16,1024]{2,1,0:T(8,128)}, u32[]{:S(2)}) copy-start(s32[1,16,1024]{2,1,0:T(8,128)} %param.13) | copy-start | bytes 196612

commit v9 on v3

--- a/solution.py
+++ b/solution.py
@@ -147,6 +147,7 @@
     scaled_held = jnp.concatenate([p_r[:eps_planes], scaled_rows[:, :-1]], 1)
     inverse_held = jnp.roll(inverse, 1, axis=1)
     inverse_cols = None
+    intersections = []
     for instant in range(step_count):
         if instant > 0:
             amplitude = jnp.cos(frequency * (instant + 1))
@@ -180,8 +181,10 @@
         solved = solve_turned(turned, inverse_held if instant == 0 else inverse)
         solved = solved.reshape(6, planes, strip, line_cells)
         fields = tuple(solved[i] for i in range(6))
+        intersections.append((instant, fields[:3]))
+    for instant, electric in intersections:
         snapshot = fwd_e[instant].astype(jnp.float32)
-        intersection = fields[0] * snapshot[0] + fields[1] * snapshot[1] + fields[2] * snapshot[2]
+        intersection = electric[0] * snapshot[0] + electric[1] * snapshot[1] + electric[2] * snapshot[2]
         gradient = gradient + mask_weight * intersection * (inverse_cols * inverse_cols)
     out = jnp.stack(fields)
     return (out[:3], out[3:], gradient)

time: 112 us -> 112 us (level)
  no operation moved by 1% of the time
where the time goes in v9:
time: 112 us; the launch traced here: 111 us
  waiting for transfers between devices  45.4 us (41%)
  blocking collectives  20.4 us (18%)
  starting transfers between devices  19.7 us (18%)
  local copies, waits for them, and re-layouts  12.7 us (11%)
  other arithmetic  6.68 us (6%)
  matrix products  3.48 us (3%)
  between operations  3.02 us (3%)
    all_to_all x2, waiting for transfers between devices, turn_rows(): parts = lax.all_to_all(parts, 'line', 0, 0, tiled=True)  32.5 us
    all_to_all x1, blocking collectives, turn_rows(): parts = lax.all_to_all(parts, 'line', 0, 0, tiled=True)  20.4 us
    ppermute x1, waiting for transfers between devices, per_device(): message = lax.ppermute(message, 'line', ring)  12.9 us
    all_to_all x2, starting transfers between devices, turn_rows(): parts = lax.all_to_all(parts, 'line', 0, 0, tiled=True)  12.8 us
    ppermute x1, starting transfers between devices, per_device(): message = lax.ppermute(message, 'line', ring)  6.83 us
    another operation x25, local copies, waits for them, and re-layouts, per_device(): stacked = jnp.stack(fields).reshape(comps, strip, line_cells)  4.22 us
    dot_general x3, matrix products, solve_turned(): lax.dot_general(turned, inverse, (((0,), (1,)), ((), ())), preferred_elem...  2.71 us
  transfers between devices with their start and end apart: 3, of which 3 were waited for; matrix products, arithmetic and copies ran while one was open for 0% of the time, Pallas kernels for 0%

profile of v9, /device:TPU:8, one launch (start us, length us, event | category | flops | bytes accessed | tf_op | source)
XLA Modules:
  0.0 111.3 jit_solution(15544511617570461516)
XLA Ops:
  2.2 0.9 slice_bitcast_fusion.24
  3.1 0.9 slice_bitcast_fusion.22
  4.0 0.9 broadcast_multiply_fusion
  4.9 0.8 dynamic-slice_multiply_fusion
  5.6 0.9 bitcast_add_fusion
  6.7 6.8 %collective-permute-start = (f32[9,1,1,1024]{3,2,1,0:T(1,128)S(1)}, f32[9,1,1,1024]{3,2,1,0:T(1,128)S(1)}, u32[]{:S(2)}, u32[]{:S(2)}) collective-permute-start(f32[9,1,1,1024]{3,2,1,0:T(1,128)S(1)} %constant_dynamic-update-slice_fusion), channel_id=1, source_target_pairs={{0,1},{1,2},{2,3},{3,4},{4,5},{5,6},{6,7},{7,8},{8,9},{9,10},{10,1... | collective-permute-start | bytes 110600 | tf_op jit(solution)/shard_map/ppermute | solution.py:124
  13.6 12.9 %collective-permute-done = f32[9,1,1,1024]{3,2,1,0:T(1,128)S(1)} collective-permute-done((f32[9,1,1,1024]{3,2,1,0:T(1,128)S(1)}, f32[9,1,1,1024]{3,2,1,0:T(1,128)S(1)}, u32[]{:S(2)}, u32[]{:S(2)}) %collective-permute-start) | collective-permute-done | bytes 36896 | tf_op jit(solution)/shard_map/ppermute | solution.py:124
  26.5 1.1 fusion.34
  27.9 0.8 fusion.83
  32.1 1.0 copy.35
  33.1 8.2 %all-to-all-start = ((bf16[64,16,128]{2,1,0:T(8,128)(2,1)}), bf16[64,16,128]{2,1,0:T(8,128)(2,1)S(1)}, u32[]{:S(2)}, u32[]{:S(2)}) async-start(bf16[64,16,128]{2,1,0:T(8,128)(2,1)} %copy.35), calls=%async_computation | async-start | bytes 524288 | tf_op jit(solution)/shard_map/all_to_all | solution.py:21
  41.6 16.7 %all-to-all-done = bf16[64,16,128]{2,1,0:T(8,128)(2,1)S(1)} async-done(((bf16[64,16,128]{2,1,0:T(8,128)(2,1)}), bf16[64,16,128]{2,1,0:T(8,128)(2,1)S(1)}, u32[]{:S(2)}, u32[]{:S(2)}) %all-to-all-start) | async-done | bytes 262176 | tf_op jit(solution)/shard_map/all_to_all | solution.py:21
  58.5 1.1 %fusion = f32[96,1024]{1,0:T(8,128)S(1)} fusion(bf16[1024,1023]{1,0:T(8,128)(2,1)S(1)} %bitcast.353, bf16[1024,1]{1,0:T(8,128)(2,1)S(1)} %slice.361, bf16[1024,128]{1,0:T(8,128)(2,1)S(1)} %bitcast.355), kind=kOutput, calls=%fused_computation | convolution fusion | flops 205520896 | bytes 2752512 | tf_op jit(solution)/shard_map/dot_general | solution.py:26
  60.4 0.2 stack.141
  62.8 0.3 copy.45
  63.0 20.4 %all_to_all.15 = bf16[64,16,96]{2,1,0:T(8,128)(2,1)S(1)} all-to-all(bf16[64,16,96]{2,1,0:T(8,128)(2,1)S(1)} %copy.45), channel_id=1, replica_groups=mesh['exc'=8,'line'=64] {'line'}, dimensions={0} | all-to-all | bytes 393216 | tf_op jit(solution)/shard_map/all_to_all | solution.py:21
  83.5 0.8 fusion.84
  87.0 0.9 copy.53
  88.0 4.6 %all-to-all-start.2 = ((bf16[64,16,96]{2,1,0:T(8,128)(2,1)}), bf16[64,16,96]{2,1,0:T(8,128)(2,1)S(1)}, u32[]{:S(2)}, u32[]{:S(2)}) async-start(bf16[64,16,96]{2,1,0:T(8,128)(2,1)} %copy.53), calls=%async_computation.2 | async-start | bytes 524288 | tf_op jit(solution)/shard_map/all_to_all | solution.py:21
  92.6 15.8 %all-to-all-done.2 = bf16[64,16,96]{2,1,0:T(8,128)(2,1)S(1)} async-done(((bf16[64,16,96]{2,1,0:T(8,128)(2,1)}), bf16[64,16,96]{2,1,0:T(8,128)(2,1)S(1)}, u32[]{:S(2)}, u32[]{:S(2)}) %all-to-all-start.2) | async-done | bytes 196640 | tf_op jit(solution)/shard_map/all_to_all | solution.py:21
  108.4 0.8 fusion.85
  109.3 0.7 fusion.11
  110.0 0.7 pad_maximum_fusion.1
  110.7 0.7 pad_maximum_fusion
  (125 shorter events, 9.5 us)
Async XLA Ops:
  0.6 27.2 %copy-start = (bf16[1024,1024]{1,0:T(8,128)(2,1)S(1)}, bf16[1024,1024]{1,0:T(8,128)(2,1)}, u32[]{:S(2)}) copy-start(bf16[1024,1024]{1,0:T(8,128)(2,1)} %param.14) | copy-start | bytes 6291460
  6.7 19.8 %collective-permute-start = (f32[9,1,1,1024]{3,2,1,0:T(1,128)S(1)}, f32[9,1,1,1024]{3,2,1,0:T(1,128)S(1)}, u32[]{:S(2)}, u32[]{:S(2)}) collective-permute-start(f32[9,1,1,1024]{3,2,1,0:T(1,128)S(1)} %constant_dynamic-update-slice_fusion), channel_id=1, source_target_pairs={{0,1},{1,2},{2,3},{3,4},{4,5},{5,6},{6,7},{7,8},{8,9},{9,10},{10,1... | collective-permute-start | bytes 110600 | tf_op jit(solution)/shard_map/ppermute | solution.py:124
  33.1 25.2 %all-to-all-start = ((bf16[64,16,128]{2,1,0:T(8,128)(2,1)}), bf16[64,16,128]{2,1,0:T(8,128)(2,1)S(1)}, u32[]{:S(2)}, u32[]{:S(2)}) async-start(bf16[64,16,128]{2,1,0:T(8,128)(2,1)} %copy.35), calls=%async_computation | async-start | bytes 524288 | tf_op jit(solution)/shard_map/all_to_all | solution.py:21
  58.5 1.6 %copy-start.4 = (f32[1024]{0:T(1024)S(1)}, f32[1024]{0:T(1024)}, u32[]{:S(2)}) copy-start(f32[1024]{0:T(1024)} %param.16) | copy-start | bytes 12292
  62.8 21.5 %copy-start.1 = (f32[1,16,1024]{2,1,0:T(8,128)S(1)}, f32[1,16,1024]{2,1,0:T(8,128)}, u32[]{:S(2)}) copy-start(f32[1,16,1024]{2,1,0:T(8,128)} %param.12) | copy-start | bytes 196612
  87.0 5.6 %copy-start.2 = (bf16[2,3,1,16,1024]{4,3,2,1,0:T(8,128)(2,1)S(1)}, bf16[2,3,1,16,1024]{4,3,2,1,0:T(8,128)(2,1)}, u32[]{:S(2)}) copy-start(bf16[2,3,1,16,1024]{4,3,2,1,0:T(8,128)(2,1)} %param.11) | copy-start | bytes 589828
  88.0 20.5 %all-to-all-start.2 = ((bf16[64,16,96]{2,1,0:T(8,128)(2,1)}), bf16[64,16,96]{2,1,0:T(8,128)(2,1)S(1)}, u32[]{:S(2)}, u32[]{:S(2)}) async-start(bf16[64,16,96]{2,1,0:T(8,128)(2,1)} %copy.53), calls=%async_computation.2 | async-start | bytes 524288 | tf_op jit(solution)/shard_map/all_to_all | solution.py:21
  92.6 16.7 %copy-start.3 = (s32[1,16,1024]{2,1,0:T(8,128)S(1)}, s32[1,16,1024]{2,1,0:T(8,128)}, u32[]{:S(2)}) copy-start(s32[1,16,1024]{2,1,0:T(8,128)} %param.13) | copy-start | bytes 196612

commit v10 on v3

--- a/solution.py
+++ b/solution.py
@@ -115,36 +115,34 @@
     ex, ey, ez = adj_e[0], adj_e[1], adj_e[2]
     hx, hy, hz = adj_h[0], adj_h[1], adj_h[2]
     ez = ez + (amplitude * profile_rows[None, :, None]) * column[None, None, :]
-    is_first = index == 0
-    ring = [(i, (i + 1) % line_count) for i in range(line_count)]
+    up = [(i, i + 1) for i in range(line_count - 1)]
     scaled_planes = jnp.broadcast_to(scaled_rows, ex.shape)
     message = jnp.stack(
         [f[:, -1:] for f in (ex, ey, ez, hx, hy, hz, scaled_planes)] + [hx[:, -2:-1], hz[:, -2:-1]]
     )
-    message = lax.ppermute(message, "line", ring)
+    message = lax.ppermute(message, "line", up)
     p_ex, p_ey, p_ez, p_hx, p_hy, p_hz, p_r, p_hx2, p_hz2 = (message[i] for i in range(9))
-    zero_row = jnp.zeros_like(p_hx)
-    hx_prev = shift_down(hx, 1, jnp.where(is_first, zero_row, p_hx))
-    hz_prev = shift_down(hz, 1, jnp.where(is_first, zero_row, p_hz))
+    hx_prev = shift_down(hx, 1, p_hx)
+    hz_prev = shift_down(hz, 1, p_hz)
     ex1 = ex + scaled_rows * (hz - hz_prev)
     ez1 = ez - scaled_rows * (hx - hx_prev)
     hx1 = hx[:, :-1] - COURANT * (ez1[:, 1:] - ez1[:, :-1])
     hz1 = hz[:, :-1] + COURANT * (ex1[:, 1:] - ex1[:, :-1])
+    hx_last = hx[:, -1:] - COURANT * (0.0 - ez1[:, -1:])
+    hz_last = hz[:, -1:] + COURANT * (0.0 - ex1[:, -1:])
     ex_y = p_ex + p_r * (p_hz - p_hz2)
     ez_y = p_ez - p_r * (p_hx - p_hx2)
-    ex_next = jnp.where(is_first, zero_row, ex1[:, :1])
-    ez_next = jnp.where(is_first, zero_row, ez1[:, :1])
-    hx_y = p_hx - COURANT * (ez_next - ez_y)
-    hz_y = p_hz + COURANT * (ex_next - ex_y)
+    hx_y = p_hx - COURANT * (ez1[:, :1] - ez_y)
+    hz_y = p_hz + COURANT * (ex1[:, :1] - ex_y)
     fields = (
-        jnp.concatenate([ex_y, ex1[:, :-1]], 1),
-        jnp.concatenate([p_ey, ey[:, :-1]], 1),
-        jnp.concatenate([ez_y, ez1[:, :-1]], 1),
-        jnp.concatenate([hx_y, hx1], 1),
-        jnp.concatenate([p_hy, hy[:, :-1]], 1),
-        jnp.concatenate([hz_y, hz1], 1),
-    )
-    scaled_held = jnp.concatenate([p_r[:eps_planes], scaled_rows[:, :-1]], 1)
+        jnp.concatenate([ex_y, ex1], 1),
+        jnp.concatenate([p_ey, ey], 1),
+        jnp.concatenate([ez_y, ez1], 1),
+        jnp.concatenate([hx_y, hx1, hx_last], 1),
+        jnp.concatenate([p_hy, hy], 1),
+        jnp.concatenate([hz_y, hz1, hz_last], 1),
+    )
+    scaled_held = jnp.concatenate([p_r[:eps_planes], scaled_rows], 1)
     inverse_held = jnp.roll(inverse, 1, axis=1)
     inverse_cols = None
     for instant in range(step_count):
@@ -160,14 +158,24 @@
         else:
             rounded = jnp.stack(fields).astype(jnp.bfloat16)
             solved = line_solve(rounded, inverse)
-        solved = solved.reshape(6, planes, strip, line_cells)
+        solved = solved.reshape(6, planes, -1, line_cells)
         fields = curl_xz(
             tuple(solved[i] for i in range(6)), scaled_held if instant == 0 else scaled_rows, 2, 0
         )
-        stacked = jnp.stack(fields).reshape(comps, strip, line_cells)
         if inverse_cols is None:
-            stacked = jnp.concatenate([stacked] + bf16_parts(inverse_rows), 0)
-        turned = turn_rows(stacked.astype(jnp.bfloat16), line_count)
+            stacked = jnp.stack(fields).reshape(comps, strip + 1, line_cells)
+            spare = jnp.zeros((eps_planes, 1, line_cells), jnp.float32)
+            eps_parts = [jnp.concatenate([p, spare], 1) for p in bf16_parts(inverse_rows)]
+            stacked = jnp.concatenate([stacked] + eps_parts, 0).astype(jnp.bfloat16)
+            slots = stacked.shape[0]
+            parts = stacked.reshape(slots, strip + 1, line_count, strip)
+            parts = jnp.transpose(parts, (2, 1, 0, 3)).reshape(line_count, strip + 1, slots * strip)
+            parts = lax.all_to_all(parts, "line", 0, 0, tiled=True)
+            held = parts[:, :strip].at[0, 0, : comps * strip].set(parts[line_count - 1, strip, : comps * strip])
+            turned = held.reshape(line_count * strip, slots * strip)
+        else:
+            stacked = jnp.stack(fields).reshape(comps, strip, line_cells)
+            turned = turn_rows(stacked.astype(jnp.bfloat16), line_count)
         if inverse_cols is None:
             width = eps_planes * strip
             pieces = [

time: 112 us -> 121 us (1.080)
  starting transfers between devices: 19.7 us -> 30.9 us
  waiting for transfers between devices: 45.4 us -> 35.2 us
  local copies, waits for them, and re-layouts: 12.7 us -> 17.3 us
  other arithmetic: 6.68 us -> 8.04 us
    all_to_all x0 -> x1, starting transfers between devices: none -> 19.5 us  [per_device(): parts = lax.all_to_all(parts, 'line', 0, 0, tiled=True)]
    all_to_all x0 -> x1, waiting for transfers between devices: none -> 18.5 us  [per_device(): parts = lax.all_to_all(parts, 'line', 0, 0, tiled=True)]
    all_to_all x2 -> x1, waiting for transfers between devices: 32.5 us -> 16.8 us  [turn_rows(): parts = lax.all_to_all(parts, 'line', 0, 0, tiled=True)]
    ppermute x1, waiting for transfers between devices: 12.9 us -> 0.01 us  [per_device(): message = lax.ppermute(message, 'line', up)]
    all_to_all x2 -> x1, starting transfers between devices: 12.8 us -> 4.61 us  [turn_rows(): parts = lax.all_to_all(parts, 'line', 0, 0, tiled=True)]
    another operation x0 -> x14, local copies, waits for them, and re-layouts: none -> 3.96 us  [the longest x12 2.27 us: per_device(): stacked = jnp.stack(fields).reshape(comps, strip + 1, line_cells)]
    another operation x11, other arithmetic: 0.69 us -> 3.07 us
    another operation x25 -> x13, local copies, waits for them, and re-layouts: 4.22 us -> 2.89 us  [per_device(): stacked = jnp.stack(fields).reshape(comps, strip, line_cells)]
  transfers between devices with their start and end apart: 3 -> 3, of which waited for: 3 -> 2; matrix products, arithmetic and copies ran while one was open for 0% -> 2% of each run, Pallas kernels for 0% -> 0%
where the time goes in v10:
time: 121 us; the launch traced here: 120 us
  waiting for transfers between devices  35.2 us (29%)
  starting transfers between devices  30.9 us (26%)
  blocking collectives  21.6 us (18%)
  local copies, waits for them, and re-layouts  17.3 us (14%)
  other arithmetic  8.04 us (7%)
  matrix products  4.44 us (4%)
  between operations  2.98 us (2%)
    all_to_all x1, blocking collectives, turn_rows(): parts = lax.all_to_all(parts, 'line', 0, 0, tiled=True)  21.6 us
    all_to_all x1, starting transfers between devices, per_device(): parts = lax.all_to_all(parts, 'line', 0, 0, tiled=True)  19.5 us
    all_to_all x1, waiting for transfers between devices, per_device(): parts = lax.all_to_all(parts, 'line', 0, 0, tiled=True)  18.5 us
    all_to_all x1, waiting for transfers between devices, turn_rows(): parts = lax.all_to_all(parts, 'line', 0, 0, tiled=True)  16.8 us
    ppermute x1, starting transfers between devices, per_device(): message = lax.ppermute(message, 'line', up)  6.83 us
    all_to_all x1, starting transfers between devices, turn_rows(): parts = lax.all_to_all(parts, 'line', 0, 0, tiled=True)  4.61 us
    dot_general x3, matrix products, solve_turned(): lax.dot_general(turned, inverse, (((0,), (1,)), ((), ())), preferred_elem...  3.66 us
    another operation x11, other arithmetic  3.07 us
  transfers between devices with their start and end apart: 3, of which 2 were waited for; matrix products, arithmetic and copies ran while one was open for 2% of the time, Pallas kernels for 0%

profile of v10, /device:TPU:8, one launch (start us, length us, event | category | flops | bytes accessed | tf_op | source)
XLA Modules:
  0.0 120.5 jit_solution(14852627561666700673)
XLA Ops:
  2.2 0.9 slice_bitcast_fusion.25
  3.1 0.9 slice_bitcast_fusion.23
  4.0 0.9 broadcast_multiply_fusion
  4.9 0.8 dynamic-slice_multiply_fusion
  5.6 0.9 bitcast_add_fusion
  6.7 6.8 %collective-permute-start = (f32[9,1,1,1024]{3,2,1,0:T(1,128)S(1)}, f32[9,1,1,1024]{3,2,1,0:T(1,128)S(1)}, u32[]{:S(2)}, u32[]{:S(2)}) collective-permute-start(f32[9,1,1,1024]{3,2,1,0:T(1,128)S(1)} %constant_dynamic-update-slice_fusion), channel_id=1, source_target_pairs={{0,1},{1,2},{2,3},{3,4},{4,5},{5,6},{6,7},{7,8},{8,9},{9,10},{10,1... | collective-permute-start | bytes 110600 | tf_op jit(solution)/shard_map/ppermute | solution.py:123
  13.5 0.8 fusion.71
  14.4 0.8 fusion.72
  15.3 1.1 fusion.87
  16.7 0.8 fusion.93
  21.4 1.1 copy.35
  22.4 19.5 %all-to-all-start = ((bf16[64,17,128]{2,1,0:T(8,128)(2,1)}), bf16[64,17,128]{2,1,0:T(8,128)(2,1)S(1)}, u32[]{:S(2)}, u32[]{:S(2)}) async-start(bf16[64,17,128]{2,1,0:T(8,128)(2,1)} %copy.35), calls=%async_computation | async-start | bytes 786432 | tf_op jit(solution)/shard_map/all_to_all | solution.py:173
  41.9 0.8 slice.386
  42.9 18.5 %all-to-all-done = bf16[64,17,128]{2,1,0:T(8,128)(2,1)S(1)} async-done(((bf16[64,17,128]{2,1,0:T(8,128)(2,1)}), bf16[64,17,128]{2,1,0:T(8,128)(2,1)S(1)}, u32[]{:S(2)}, u32[]{:S(2)}) %all-to-all-start) | async-done | bytes 278560 | tf_op jit(solution)/shard_map/all_to_all | solution.py:173
  61.8 2.1 %fusion = f32[96,1024]{1,0:T(8,128)S(1)} fusion(bf16[1024,1023]{1,0:T(8,128)(2,1)S(1)} %bitcast.353, bf16[1024,1]{1,0:T(8,128)(2,1)} %slice.386, bf16[1024,128]{1,0:T(8,128)(2,1)S(1)} %bitcast.355), kind=kOutput, calls=%fused_computation | convolution fusion | flops 205520896 | bytes 2752512 | tf_op jit(solution)/shard_map/dot_general | solution.py:26
  64.6 0.7 fusion.43
  67.1 1.0 stack.143
  68.7 21.6 %all_to_all.15 = bf16[64,16,96]{2,1,0:T(8,128)(2,1)S(1)} all-to-all(bf16[64,16,96]{2,1,0:T(8,128)(2,1)S(1)} %copy.45), channel_id=1, replica_groups=mesh['exc'=8,'line'=64] {'line'}, dimensions={0} | all-to-all | bytes 393216 | tf_op jit(solution)/shard_map/all_to_all | solution.py:21
  90.2 0.8 fusion.94
  93.9 1.0 stack.150
  95.2 0.9 copy.53
  96.1 4.6 %all-to-all-start.2 = ((bf16[64,16,96]{2,1,0:T(8,128)(2,1)}), bf16[64,16,96]{2,1,0:T(8,128)(2,1)S(1)}, u32[]{:S(2)}, u32[]{:S(2)}) async-start(bf16[64,16,96]{2,1,0:T(8,128)(2,1)} %copy.53), calls=%async_computation.2 | async-start | bytes 524288 | tf_op jit(solution)/shard_map/all_to_all | solution.py:21
  100.8 16.8 %all-to-all-done.2 = bf16[64,16,96]{2,1,0:T(8,128)(2,1)S(1)} async-done(((bf16[64,16,96]{2,1,0:T(8,128)(2,1)}), bf16[64,16,96]{2,1,0:T(8,128)(2,1)S(1)}, u32[]{:S(2)}, u32[]{:S(2)}) %all-to-all-start.2) | async-done | bytes 196640 | tf_op jit(solution)/shard_map/all_to_all | solution.py:21
  117.6 0.8 fusion.95
  (127 shorter events, 12.7 us)
Async XLA Ops:
  0.6 16.0 %copy-start = (bf16[1024,1024]{1,0:T(8,128)(2,1)S(1)}, bf16[1024,1024]{1,0:T(8,128)(2,1)}, u32[]{:S(2)}) copy-start(bf16[1024,1024]{1,0:T(8,128)(2,1)} %param.16) | copy-start | bytes 6291460
  6.7 8.5 %collective-permute-start = (f32[9,1,1,1024]{3,2,1,0:T(1,128)S(1)}, f32[9,1,1,1024]{3,2,1,0:T(1,128)S(1)}, u32[]{:S(2)}, u32[]{:S(2)}) collective-permute-start(f32[9,1,1,1024]{3,2,1,0:T(1,128)S(1)} %constant_dynamic-update-slice_fusion), channel_id=1, source_target_pairs={{0,1},{1,2},{2,3},{3,4},{4,5},{5,6},{6,7},{7,8},{8,9},{9,10},{10,1... | collective-permute-start | bytes 110600 | tf_op jit(solution)/shard_map/ppermute | solution.py:123
  22.4 38.9 %all-to-all-start = ((bf16[64,17,128]{2,1,0:T(8,128)(2,1)}), bf16[64,17,128]{2,1,0:T(8,128)(2,1)S(1)}, u32[]{:S(2)}, u32[]{:S(2)}) async-start(bf16[64,17,128]{2,1,0:T(8,128)(2,1)} %copy.35), calls=%async_computation | async-start | bytes 786432 | tf_op jit(solution)/shard_map/all_to_all | solution.py:173
  61.8 2.5 %copy-start.4 = (f32[1024]{0:T(1024)S(1)}, f32[1024]{0:T(1024)}, u32[]{:S(2)}) copy-start(f32[1024]{0:T(1024)} %param.18) | copy-start | bytes 12292
  68.4 22.7 %copy-start.1 = (f32[1,16,1024]{2,1,0:T(8,128)S(1)}, f32[1,16,1024]{2,1,0:T(8,128)}, u32[]{:S(2)}) copy-start(f32[1,16,1024]{2,1,0:T(8,128)} %param.14) | copy-start | bytes 196612
  95.0 5.7 %copy-start.2 = (bf16[2,3,1,16,1024]{4,3,2,1,0:T(8,128)(2,1)S(1)}, bf16[2,3,1,16,1024]{4,3,2,1,0:T(8,128)(2,1)}, u32[]{:S(2)}) copy-start(bf16[2,3,1,16,1024]{4,3,2,1,0:T(8,128)(2,1)} %param.13) | copy-start | bytes 589828
  96.1 21.4 %all-to-all-start.2 = ((bf16[64,16,96]{2,1,0:T(8,128)(2,1)}), bf16[64,16,96]{2,1,0:T(8,128)(2,1)S(1)}, u32[]{:S(2)}, u32[]{:S(2)}) async-start(bf16[64,16,96]{2,1,0:T(8,128)(2,1)} %copy.53), calls=%async_computation.2 | async-start | bytes 524288 | tf_op jit(solution)/shard_map/all_to_all | solution.py:21
  100.8 17.6 %copy-start.3 = (s32[1,16,1024]{2,1,0:T(8,128)S(1)}, s32[1,16,1024]{2,1,0:T(8,128)}, u32[]{:S(2)}) copy-start(s32[1,16,1024]{2,1,0:T(8,128)} %param.15) | copy-start | bytes 196612

commit v11 on v3

--- a/solution.py
+++ b/solution.py
@@ -117,12 +117,13 @@
     ez = ez + (amplitude * profile_rows[None, :, None]) * column[None, None, :]
     is_first = index == 0
     ring = [(i, (i + 1) % line_count) for i in range(line_count)]
-    scaled_planes = jnp.broadcast_to(scaled_rows, ex.shape)
+    eps_planes_b = jnp.broadcast_to(permittivity, ex.shape)
     message = jnp.stack(
-        [f[:, -1:] for f in (ex, ey, ez, hx, hy, hz, scaled_planes)] + [hx[:, -2:-1], hz[:, -2:-1]]
+        [f[:, -1:] for f in (ex, ey, ez, hx, hy, hz, eps_planes_b)] + [hx[:, -2:-1], hz[:, -2:-1]]
     )
     message = lax.ppermute(message, "line", ring)
-    p_ex, p_ey, p_ez, p_hx, p_hy, p_hz, p_r, p_hx2, p_hz2 = (message[i] for i in range(9))
+    p_ex, p_ey, p_ez, p_hx, p_hy, p_hz, p_eps, p_hx2, p_hz2 = (message[i] for i in range(9))
+    p_r = COURANT * (1.0 / p_eps)
     zero_row = jnp.zeros_like(p_hx)
     hx_prev = shift_down(hx, 1, jnp.where(is_first, zero_row, p_hx))
     hz_prev = shift_down(hz, 1, jnp.where(is_first, zero_row, p_hz))

time: 112 us -> 112 us (level)
  no operation moved by 1% of the time
where the time goes in v11:
time: 112 us; the launch traced here: 111 us
  waiting for transfers between devices  45.5 us (41%)
  blocking collectives  20.4 us (18%)
  starting transfers between devices  19.6 us (18%)
  local copies, waits for them, and re-layouts  13.4 us (12%)
  other arithmetic  5.83 us (5%)
  matrix products  3.48 us (3%)
  between operations  3.01 us (3%)
    all_to_all x2, waiting for transfers between devices, turn_rows(): parts = lax.all_to_all(parts, 'line', 0, 0, tiled=True)  32.5 us
    all_to_all x1, blocking collectives, turn_rows(): parts = lax.all_to_all(parts, 'line', 0, 0, tiled=True)  20.4 us
    ppermute x1, waiting for transfers between devices, per_device(): message = lax.ppermute(message, 'line', ring)  13 us
    all_to_all x2, starting transfers between devices, turn_rows(): parts = lax.all_to_all(parts, 'line', 0, 0, tiled=True)  12.8 us
    ppermute x1, starting transfers between devices, per_device(): message = lax.ppermute(message, 'line', ring)  6.83 us
    another operation x25, local copies, waits for them, and re-layouts, per_device(): stacked = jnp.stack(fields).reshape(comps, strip, line_cells)  4.22 us
    dot_general x3, matrix products, solve_turned(): lax.dot_general(turned, inverse, (((0,), (1,)), ((), ())), preferred_elem...  2.71 us
  transfers between devices with their start and end apart: 3, of which 3 were waited for; matrix products, arithmetic and copies ran while one was open for 0% of the time, Pallas kernels for 0%

profile of v11, /device:TPU:8, one launch (start us, length us, event | category | flops | bytes accessed | tf_op | source)
XLA Modules:
  0.0 111.3 jit_solution(7074228995739860995)
XLA Ops:
  2.2 0.9 slice_bitcast_fusion.24
  3.1 0.9 slice_bitcast_fusion.22
  4.0 0.8 dynamic-slice_multiply_fusion
  4.8 0.9 bitcast_add_fusion
  5.8 0.8 constant_dynamic-update-slice_fusion.2
  6.6 6.8 %collective-permute-start = (f32[9,1,1,1024]{3,2,1,0:T(1,128)S(1)}, f32[9,1,1,1024]{3,2,1,0:T(1,128)S(1)}, u32[]{:S(2)}, u32[]{:S(2)}) collective-permute-start(f32[9,1,1,1024]{3,2,1,0:T(1,128)S(1)} %constant_dynamic-update-slice_fusion), channel_id=1, source_target_pairs={{0,1},{1,2},{2,3},{3,4},{4,5},{5,6},{6,7},{7,8},{8,9},{9,10},{10,1... | collective-permute-start | bytes 110600 | tf_op jit(solution)/shard_map/ppermute | solution.py:124
  13.4 13.0 %collective-permute-done = f32[9,1,1,1024]{3,2,1,0:T(1,128)S(1)} collective-permute-done((f32[9,1,1,1024]{3,2,1,0:T(1,128)S(1)}, f32[9,1,1,1024]{3,2,1,0:T(1,128)S(1)}, u32[]{:S(2)}, u32[]{:S(2)}) %collective-permute-start) | collective-permute-done | bytes 36896 | tf_op jit(solution)/shard_map/ppermute | solution.py:124
  26.4 1.1 fusion.34
  27.8 0.8 fusion.85
  32.1 1.0 copy.35
  33.0 8.2 %all-to-all-start = ((bf16[64,16,128]{2,1,0:T(8,128)(2,1)}), bf16[64,16,128]{2,1,0:T(8,128)(2,1)S(1)}, u32[]{:S(2)}, u32[]{:S(2)}) async-start(bf16[64,16,128]{2,1,0:T(8,128)(2,1)} %copy.35), calls=%async_computation | async-start | bytes 524288 | tf_op jit(solution)/shard_map/all_to_all | solution.py:21
  41.5 16.7 %all-to-all-done = bf16[64,16,128]{2,1,0:T(8,128)(2,1)S(1)} async-done(((bf16[64,16,128]{2,1,0:T(8,128)(2,1)}), bf16[64,16,128]{2,1,0:T(8,128)(2,1)S(1)}, u32[]{:S(2)}, u32[]{:S(2)}) %all-to-all-start) | async-done | bytes 262176 | tf_op jit(solution)/shard_map/all_to_all | solution.py:21
  58.4 1.1 %fusion = f32[96,1024]{1,0:T(8,128)S(1)} fusion(bf16[1024,1023]{1,0:T(8,128)(2,1)S(1)} %bitcast.347, bf16[1024,1]{1,0:T(8,128)(2,1)S(1)} %slice.361, bf16[1024,128]{1,0:T(8,128)(2,1)S(1)} %bitcast.349), kind=kOutput, calls=%fused_computation | convolution fusion | flops 205520896 | bytes 2752512 | tf_op jit(solution)/shard_map/dot_general | solution.py:26
  60.4 0.2 stack.141
  62.7 0.3 copy.45
  63.0 20.4 %all_to_all.15 = bf16[64,16,96]{2,1,0:T(8,128)(2,1)S(1)} all-to-all(bf16[64,16,96]{2,1,0:T(8,128)(2,1)S(1)} %copy.45), channel_id=1, replica_groups=mesh['exc'=8,'line'=64] {'line'}, dimensions={0} | all-to-all | bytes 393216 | tf_op jit(solution)/shard_map/all_to_all | solution.py:21
  83.4 0.8 fusion.86
  86.9 0.9 copy.53
  87.9 4.6 %all-to-all-start.2 = ((bf16[64,16,96]{2,1,0:T(8,128)(2,1)}), bf16[64,16,96]{2,1,0:T(8,128)(2,1)S(1)}, u32[]{:S(2)}, u32[]{:S(2)}) async-start(bf16[64,16,96]{2,1,0:T(8,128)(2,1)} %copy.53), calls=%async_computation.2 | async-start | bytes 524288 | tf_op jit(solution)/shard_map/all_to_all | solution.py:21
  92.5 15.8 %all-to-all-done.2 = bf16[64,16,96]{2,1,0:T(8,128)(2,1)S(1)} async-done(((bf16[64,16,96]{2,1,0:T(8,128)(2,1)}), bf16[64,16,96]{2,1,0:T(8,128)(2,1)S(1)}, u32[]{:S(2)}, u32[]{:S(2)}) %all-to-all-start.2) | async-done | bytes 196640 | tf_op jit(solution)/shard_map/all_to_all | solution.py:21
  108.3 0.8 fusion.87
  109.2 0.7 fusion.11
  109.9 0.7 pad_maximum_fusion.1
  110.6 0.7 pad_maximum_fusion
  (125 shorter events, 9.5 us)
Async XLA Ops:
  0.6 27.2 %copy-start = (bf16[1024,1024]{1,0:T(8,128)(2,1)S(1)}, bf16[1024,1024]{1,0:T(8,128)(2,1)}, u32[]{:S(2)}) copy-start(bf16[1024,1024]{1,0:T(8,128)(2,1)} %param.14) | copy-start | bytes 6291460
  6.6 19.8 %collective-permute-start = (f32[9,1,1,1024]{3,2,1,0:T(1,128)S(1)}, f32[9,1,1,1024]{3,2,1,0:T(1,128)S(1)}, u32[]{:S(2)}, u32[]{:S(2)}) collective-permute-start(f32[9,1,1,1024]{3,2,1,0:T(1,128)S(1)} %constant_dynamic-update-slice_fusion), channel_id=1, source_target_pairs={{0,1},{1,2},{2,3},{3,4},{4,5},{5,6},{6,7},{7,8},{8,9},{9,10},{10,1... | collective-permute-start | bytes 110600 | tf_op jit(solution)/shard_map/ppermute | solution.py:124
  33.0 25.2 %all-to-all-start = ((bf16[64,16,128]{2,1,0:T(8,128)(2,1)}), bf16[64,16,128]{2,1,0:T(8,128)(2,1)S(1)}, u32[]{:S(2)}, u32[]{:S(2)}) async-start(bf16[64,16,128]{2,1,0:T(8,128)(2,1)} %copy.35), calls=%async_computation | async-start | bytes 524288 | tf_op jit(solution)/shard_map/all_to_all | solution.py:21
  58.4 1.6 %copy-start.4 = (f32[1024]{0:T(1024)S(1)}, f32[1024]{0:T(1024)}, u32[]{:S(2)}) copy-start(f32[1024]{0:T(1024)} %param.16) | copy-start | bytes 12292
  62.7 21.5 %copy-start.1 = (f32[1,16,1024]{2,1,0:T(8,128)S(1)}, f32[1,16,1024]{2,1,0:T(8,128)}, u32[]{:S(2)}) copy-start(f32[1,16,1024]{2,1,0:T(8,128)} %param.12) | copy-start | bytes 196612
  86.9 5.6 %copy-start.2 = (bf16[2,3,1,16,1024]{4,3,2,1,0:T(8,128)(2,1)S(1)}, bf16[2,3,1,16,1024]{4,3,2,1,0:T(8,128)(2,1)}, u32[]{:S(2)}) copy-start(bf16[2,3,1,16,1024]{4,3,2,1,0:T(8,128)(2,1)} %param.11) | copy-start | bytes 589828
  87.9 20.5 %all-to-all-start.2 = ((bf16[64,16,96]{2,1,0:T(8,128)(2,1)}), bf16[64,16,96]{2,1,0:T(8,128)(2,1)S(1)}, u32[]{:S(2)}, u32[]{:S(2)}) async-start(bf16[64,16,96]{2,1,0:T(8,128)(2,1)} %copy.53), calls=%async_computation.2 | async-start | bytes 524288 | tf_op jit(solution)/shard_map/all_to_all | solution.py:21
  92.5 16.7 %copy-start.3 = (s32[1,16,1024]{2,1,0:T(8,128)S(1)}, s32[1,16,1024]{2,1,0:T(8,128)}, u32[]{:S(2)}) copy-start(s32[1,16,1024]{2,1,0:T(8,128)} %param.13) | copy-start | bytes 196612

commit v12 on v4

--- a/solution.py
+++ b/solution.py
@@ -110,11 +110,6 @@
     comps = 6 * planes
 
     ring = [(i, (i + 1) % line_count) for i in range(line_count)]
-    eps_planes_b = jnp.broadcast_to(permittivity, adj_e[0].shape)
-    message = jnp.concatenate(
-        [adj_e[:, :, -1:], adj_h[:, :, -1:], eps_planes_b[None, :, -1:], adj_h[::2, :, -2:-1]], 0
-    )
-    message = lax.ppermute(message, "line", ring)
     is_first = index == 0
     column = (jnp.arange(line_cells, dtype=jnp.int32) == plane_at).astype(jnp.float32)
     profile_rows = lax.dynamic_slice_in_dim(port_mode, offset, strip)
@@ -122,6 +117,11 @@
     ex, ey, ez = adj_e[0], adj_e[1], adj_e[2]
     hx, hy, hz = adj_h[0], adj_h[1], adj_h[2]
     ez = ez + (amplitude * profile_rows[None, :, None]) * column[None, None, :]
+    scaled_planes = jnp.broadcast_to(scaled_rows, ex.shape)
+    message = jnp.stack(
+        [f[:, -1:] for f in (ex, ey, ez, hx, hy, hz, scaled_planes)] + [hx[:, -2:-1], hz[:, -2:-1]]
+    )
+    message = lax.ppermute(message, "line", ring)
     ex1 = ex[:, 1:] + scaled_rows[:, 1:] * (hz[:, 1:] - hz[:, :-1])
     ez1 = ez[:, 1:] - scaled_rows[:, 1:] * (hx[:, 1:] - hx[:, :-1])
     hx1 = hx[:, 1:-1] - COURANT * (ez1[:, 1:] - ez1[:, :-1])
@@ -129,12 +129,7 @@
     inner = (ex1[:, :-1], ey[:, 1:-1], ez1[:, :-1], hx1, hy[:, 1:-1], hz1)
     inner_solved = line_solve(jnp.stack(inner).astype(jnp.bfloat16), inverse)
     inner_fields = curl_xz(tuple(inner_solved[i] for i in range(6)), scaled_rows[:, 1:-1], 2, 0)
-    p_ex, p_ey, p_ez, p_hx, p_hy, p_hz = (message[i] for i in range(6))
-    p_eps, p_hx2, p_hz2 = message[6], message[7], message[8]
-    row_before = (offset + line_cells - 1) % line_cells
-    profile_before = lax.dynamic_slice_in_dim(port_mode, row_before, 1)
-    p_ez = p_ez + (amplitude * profile_before[None, :, None]) * column[None, None, :]
-    p_r = COURANT * (1.0 / p_eps)
+    p_ex, p_ey, p_ez, p_hx, p_hy, p_hz, p_r, p_hx2, p_hz2 = (message[i] for i in range(9))
     zero_row = jnp.zeros_like(p_hx)
     below_hx = jnp.where(is_first, zero_row, p_hx)
     below_hz = jnp.where(is_first, zero_row, p_hz)

time: 115 us -> 111 us (0.965)
  the two profiles are of different devices: /device:TPU:16 before, /device:TPU:8 now
where the time goes in v12:
time: 111 us
  waiting for transfers between devices  42.2 us (38%)
  blocking collectives  20.9 us (19%)
  starting transfers between devices  19.7 us (18%)
  local copies, waits for them, and re-layouts  14.7 us (13%)
  other arithmetic  6.05 us (5%)
  matrix products  4.11 us (4%)
  between operations  3.08 us (3%)
    all_to_all x2, waiting for transfers between devices, turn_rows(): parts = lax.all_to_all(parts, 'line', 0, 0, tiled=True)  33.4 us
    all_to_all x1, blocking collectives, turn_rows(): parts = lax.all_to_all(parts, 'line', 0, 0, tiled=True)  20.9 us
    all_to_all x2, starting transfers between devices, turn_rows(): parts = lax.all_to_all(parts, 'line', 0, 0, tiled=True)  12.8 us
    ppermute x1, waiting for transfers between devices, per_device(): message = lax.ppermute(message, 'line', ring)  8.76 us
    ppermute x1, starting transfers between devices, per_device(): message = lax.ppermute(message, 'line', ring)  6.83 us
    another operation x23, local copies, waits for them, and re-layouts, per_device(): stacked = jnp.stack(fields).reshape(comps, strip, line_cells)  3.85 us
    dot_general x3, matrix products, solve_turned(): lax.dot_general(turned, inverse, (((0,), (1,)), ((), ())), preferred_elem...  2.7 us
  transfers between devices with their start and end apart: 3, of which 3 were waited for; matrix products, arithmetic and copies ran while one was open for 4% of the time, Pallas kernels for 0%

profile of v12, /device:TPU:8, one launch (start us, length us, event | category | flops | bytes accessed | tf_op | source)
XLA Modules:
  0.0 110.7 jit_solution(8353207968549974898)
XLA Ops:
  2.2 0.9 slice_bitcast_fusion.24
  3.1 0.9 fusion.5
  4.0 0.9 slice_bitcast_fusion.26
  4.9 0.8 dynamic-slice_multiply_fusion
  5.6 0.9 bitcast_add_fusion
  6.7 6.8 %collective-permute-start = (f32[9,1,1,1024]{3,2,1,0:T(1,128)S(1)}, f32[9,1,1,1024]{3,2,1,0:T(1,128)S(1)}, u32[]{:S(2)}, u32[]{:S(2)}) collective-permute-start(f32[9,1,1,1024]{3,2,1,0:T(1,128)S(1)} %constant_dynamic-update-slice_fusion), channel_id=1, source_target_pairs={{0,1},{1,2},{2,3},{3,4},{4,5},{5,6},{6,7},{7,8},{8,9},{9,10},{10,1... | collective-permute-start | bytes 110600 | tf_op jit(solution)/shard_map/ppermute | solution.py:124
  13.6 0.8 fusion.87
  14.4 0.8 fusion.88
  15.4 0.8 fusion.109
  17.7 8.8 %collective-permute-done = f32[9,1,1,1024]{3,2,1,0:T(1,128)S(1)} collective-permute-done((f32[9,1,1,1024]{3,2,1,0:T(1,128)S(1)}, f32[9,1,1,1024]{3,2,1,0:T(1,128)S(1)}, u32[]{:S(2)}, u32[]{:S(2)}) %collective-permute-start) | collective-permute-done | bytes 36896 | tf_op jit(solution)/shard_map/ppermute | solution.py:124
  26.8 0.6 fusion.108
  30.1 1.0 copy.36
  31.1 8.2 %all-to-all-start = ((bf16[64,16,128]{2,1,0:T(8,128)(2,1)}), bf16[64,16,128]{2,1,0:T(8,128)(2,1)S(1)}, u32[]{:S(2)}, u32[]{:S(2)}) async-start(bf16[64,16,128]{2,1,0:T(8,128)(2,1)} %copy.36), calls=%async_computation | async-start | bytes 524288 | tf_op jit(solution)/shard_map/all_to_all | solution.py:21
  39.5 16.8 %all-to-all-done = bf16[64,16,128]{2,1,0:T(8,128)(2,1)S(1)} async-done(((bf16[64,16,128]{2,1,0:T(8,128)(2,1)}), bf16[64,16,128]{2,1,0:T(8,128)(2,1)S(1)}, u32[]{:S(2)}, u32[]{:S(2)}) %all-to-all-start) | async-done | bytes 262176 | tf_op jit(solution)/shard_map/all_to_all | solution.py:21
  56.5 1.1 %fusion = f32[96,1024]{1,0:T(8,128)S(1)} fusion(bf16[1024,1023]{1,0:T(8,128)(2,1)S(1)} %bitcast.419, bf16[1024,1]{1,0:T(8,128)(2,1)S(1)} %slice.468, bf16[1024,128]{1,0:T(8,128)(2,1)S(1)} %bitcast.421), kind=kOutput, calls=%fused_computation | convolution fusion | flops 205520896 | bytes 2752512 | tf_op jit(solution)/shard_map/dot_general | solution.py:26
  61.1 20.9 %all_to_all.15 = bf16[64,16,96]{2,1,0:T(8,128)(2,1)S(1)} all-to-all(bf16[64,16,96]{2,1,0:T(8,128)(2,1)S(1)} %copy.46), channel_id=1, replica_groups=mesh['exc'=8,'line'=64] {'line'}, dimensions={0} | all-to-all | bytes 393216 | tf_op jit(solution)/shard_map/all_to_all | solution.py:21
  82.0 0.8 fusion.110
  85.5 0.9 copy.54
  86.5 4.6 %all-to-all-start.2 = ((bf16[64,16,96]{2,1,0:T(8,128)(2,1)}), bf16[64,16,96]{2,1,0:T(8,128)(2,1)S(1)}, u32[]{:S(2)}, u32[]{:S(2)}) async-start(bf16[64,16,96]{2,1,0:T(8,128)(2,1)} %copy.54), calls=%async_computation.2 | async-start | bytes 524288 | tf_op jit(solution)/shard_map/all_to_all | solution.py:21
  91.1 16.6 %all-to-all-done.2 = bf16[64,16,96]{2,1,0:T(8,128)(2,1)S(1)} async-done(((bf16[64,16,96]{2,1,0:T(8,128)(2,1)}), bf16[64,16,96]{2,1,0:T(8,128)(2,1)S(1)}, u32[]{:S(2)}, u32[]{:S(2)}) %all-to-all-start.2) | async-done | bytes 196640 | tf_op jit(solution)/shard_map/all_to_all | solution.py:21
  107.8 0.8 fusion.111
  108.6 0.7 fusion.11
  109.3 0.7 pad_maximum_fusion.1
  110.0 0.7 pad_maximum_fusion
  (146 shorter events, 10.8 us)
Async XLA Ops:
  0.6 14.8 %copy-start = (bf16[1024,1024]{1,0:T(8,128)(2,1)S(1)}, bf16[1024,1024]{1,0:T(8,128)(2,1)}, u32[]{:S(2)}) copy-start(bf16[1024,1024]{1,0:T(8,128)(2,1)} %param.14) | copy-start | bytes 6291460
  6.7 19.8 %collective-permute-start = (f32[9,1,1,1024]{3,2,1,0:T(1,128)S(1)}, f32[9,1,1,1024]{3,2,1,0:T(1,128)S(1)}, u32[]{:S(2)}, u32[]{:S(2)}) collective-permute-start(f32[9,1,1,1024]{3,2,1,0:T(1,128)S(1)} %constant_dynamic-update-slice_fusion), channel_id=1, source_target_pairs={{0,1},{1,2},{2,3},{3,4},{4,5},{5,6},{6,7},{7,8},{8,9},{9,10},{10,1... | collective-permute-start | bytes 110600 | tf_op jit(solution)/shard_map/ppermute | solution.py:124
  31.1 25.2 %all-to-all-start = ((bf16[64,16,128]{2,1,0:T(8,128)(2,1)}), bf16[64,16,128]{2,1,0:T(8,128)(2,1)S(1)}, u32[]{:S(2)}, u32[]{:S(2)}) async-start(bf16[64,16,128]{2,1,0:T(8,128)(2,1)} %copy.36), calls=%async_computation | async-start | bytes 524288 | tf_op jit(solution)/shard_map/all_to_all | solution.py:21
  56.5 1.6 %copy-start.4 = (f32[1024]{0:T(1024)S(1)}, f32[1024]{0:T(1024)}, u32[]{:S(2)}) copy-start(f32[1024]{0:T(1024)} %param.16) | copy-start | bytes 12292
  60.8 22.0 %copy-start.1 = (f32[1,16,1024]{2,1,0:T(8,128)S(1)}, f32[1,16,1024]{2,1,0:T(8,128)}, u32[]{:S(2)}) copy-start(f32[1,16,1024]{2,1,0:T(8,128)} %param.12) | copy-start | bytes 196612
  85.5 5.6 %copy-start.2 = (bf16[2,3,1,16,1024]{4,3,2,1,0:T(8,128)(2,1)S(1)}, bf16[2,3,1,16,1024]{4,3,2,1,0:T(8,128)(2,1)}, u32[]{:S(2)}) copy-start(bf16[2,3,1,16,1024]{4,3,2,1,0:T(8,128)(2,1)} %param.11) | copy-start | bytes 589828
  86.5 21.3 %all-to-all-start.2 = ((bf16[64,16,96]{2,1,0:T(8,128)(2,1)}), bf16[64,16,96]{2,1,0:T(8,128)(2,1)S(1)}, u32[]{:S(2)}, u32[]{:S(2)}) async-start(bf16[64,16,96]{2,1,0:T(8,128)(2,1)} %copy.54), calls=%async_computation.2 | async-start | bytes 524288 | tf_op jit(solution)/shard_map/all_to_all | solution.py:21
  91.1 17.5 %copy-start.3 = (s32[1,16,1024]{2,1,0:T(8,128)S(1)}, s32[1,16,1024]{2,1,0:T(8,128)}, u32[]{:S(2)}) copy-start(s32[1,16,1024]{2,1,0:T(8,128)} %param.13) | copy-start | bytes 196612

commit v13 on v3

--- a/solution.py
+++ b/solution.py
@@ -145,7 +145,6 @@
         jnp.concatenate([hz_y, hz1], 1),
     )
     scaled_held = jnp.concatenate([p_r[:eps_planes], scaled_rows[:, :-1]], 1)
-    inverse_held = jnp.roll(inverse, 1, axis=1)
     inverse_cols = None
     for instant in range(step_count):
         if instant > 0:
@@ -177,7 +176,9 @@
             joined = pieces[0] + pieces[1]
             inverse_cols = joined.T.reshape(eps_planes, strip, line_cells)
             turned = turned[:, : comps * strip]
-        solved = solve_turned(turned, inverse_held if instant == 0 else inverse)
+        if instant == 0:
+            turned = jnp.roll(turned, -1, axis=0)
+        solved = solve_turned(turned, inverse)
         solved = solved.reshape(6, planes, strip, line_cells)
         fields = tuple(solved[i] for i in range(6))
         snapshot = fwd_e[instant].astype(jnp.float32)

time: 112 us -> 112 us (level)
  no operation moved by 1% of the time
where the time goes in v13:
time: 112 us; the launch traced here: 111 us
  waiting for transfers between devices  45.7 us (41%)
  blocking collectives  20.4 us (18%)
  starting transfers between devices  19.7 us (18%)
  local copies, waits for them, and re-layouts  12.6 us (11%)
  other arithmetic  6.67 us (6%)
  matrix products  3.12 us (3%)
  between operations  3.02 us (3%)
    all_to_all x2, waiting for transfers between devices, turn_rows(): parts = lax.all_to_all(parts, 'line', 0, 0, tiled=True)  32.7 us
    all_to_all x1, blocking collectives, turn_rows(): parts = lax.all_to_all(parts, 'line', 0, 0, tiled=True)  20.4 us
    ppermute x1, waiting for transfers between devices, per_device(): message = lax.ppermute(message, 'line', ring)  12.9 us
    all_to_all x2, starting transfers between devices, turn_rows(): parts = lax.all_to_all(parts, 'line', 0, 0, tiled=True)  12.8 us
    ppermute x1, starting transfers between devices, per_device(): message = lax.ppermute(message, 'line', ring)  6.83 us
    another operation x25, local copies, waits for them, and re-layouts, per_device(): stacked = jnp.stack(fields).reshape(comps, strip, line_cells)  4.22 us
    dot_general x3, matrix products, solve_turned(): lax.dot_general(turned, inverse, (((0,), (1,)), ((), ())), preferred_elem...  2.35 us
  transfers between devices with their start and end apart: 3, of which 3 were waited for; matrix products, arithmetic and copies ran while one was open for 0% of the time, Pallas kernels for 0%

profile of v13, /device:TPU:8, one launch (start us, length us, event | category | flops | bytes accessed | tf_op | source)
XLA Modules:
  0.0 111.2 jit_solution(11970992524679155885)
XLA Ops:
  2.2 0.9 slice_bitcast_fusion.24
  3.1 0.9 slice_bitcast_fusion.22
  4.0 0.9 broadcast_multiply_fusion
  4.9 0.8 dynamic-slice_multiply_fusion
  5.6 0.9 bitcast_add_fusion
  6.7 6.8 %collective-permute-start = (f32[9,1,1,1024]{3,2,1,0:T(1,128)S(1)}, f32[9,1,1,1024]{3,2,1,0:T(1,128)S(1)}, u32[]{:S(2)}, u32[]{:S(2)}) collective-permute-start(f32[9,1,1,1024]{3,2,1,0:T(1,128)S(1)} %constant_dynamic-update-slice_fusion), channel_id=1, source_target_pairs={{0,1},{1,2},{2,3},{3,4},{4,5},{5,6},{6,7},{7,8},{8,9},{9,10},{10,1... | collective-permute-start | bytes 110600 | tf_op jit(solution)/shard_map/ppermute | solution.py:124
  13.6 12.9 %collective-permute-done = f32[9,1,1,1024]{3,2,1,0:T(1,128)S(1)} collective-permute-done((f32[9,1,1,1024]{3,2,1,0:T(1,128)S(1)}, f32[9,1,1,1024]{3,2,1,0:T(1,128)S(1)}, u32[]{:S(2)}, u32[]{:S(2)}) %collective-permute-start) | collective-permute-done | bytes 36896 | tf_op jit(solution)/shard_map/ppermute | solution.py:124
  26.5 1.1 fusion.33
  27.9 0.8 fusion.82
  32.1 1.0 copy.35
  33.1 8.2 %all-to-all-start = ((bf16[64,16,128]{2,1,0:T(8,128)(2,1)}), bf16[64,16,128]{2,1,0:T(8,128)(2,1)S(1)}, u32[]{:S(2)}, u32[]{:S(2)}) async-start(bf16[64,16,128]{2,1,0:T(8,128)(2,1)} %copy.35), calls=%async_computation | async-start | bytes 524288 | tf_op jit(solution)/shard_map/all_to_all | solution.py:21
  41.4 16.9 %all-to-all-done = bf16[64,16,128]{2,1,0:T(8,128)(2,1)S(1)} async-done(((bf16[64,16,128]{2,1,0:T(8,128)(2,1)}), bf16[64,16,128]{2,1,0:T(8,128)(2,1)S(1)}, u32[]{:S(2)}, u32[]{:S(2)}) %all-to-all-start) | async-done | bytes 262176 | tf_op jit(solution)/shard_map/all_to_all | solution.py:21
  58.6 0.8 fusion
  60.2 0.2 stack.141
  62.5 0.3 copy.45
  62.8 20.4 %all_to_all.15 = bf16[64,16,96]{2,1,0:T(8,128)(2,1)S(1)} all-to-all(bf16[64,16,96]{2,1,0:T(8,128)(2,1)S(1)} %copy.45), channel_id=1, replica_groups=mesh['exc'=8,'line'=64] {'line'}, dimensions={0} | all-to-all | bytes 393216 | tf_op jit(solution)/shard_map/all_to_all | solution.py:21
  83.2 0.8 fusion.83
  86.8 0.9 copy.53
  87.7 4.6 %all-to-all-start.2 = ((bf16[64,16,96]{2,1,0:T(8,128)(2,1)}), bf16[64,16,96]{2,1,0:T(8,128)(2,1)S(1)}, u32[]{:S(2)}, u32[]{:S(2)}) async-start(bf16[64,16,96]{2,1,0:T(8,128)(2,1)} %copy.53), calls=%async_computation.2 | async-start | bytes 524288 | tf_op jit(solution)/shard_map/all_to_all | solution.py:21
  92.4 15.9 %all-to-all-done.2 = bf16[64,16,96]{2,1,0:T(8,128)(2,1)S(1)} async-done(((bf16[64,16,96]{2,1,0:T(8,128)(2,1)}), bf16[64,16,96]{2,1,0:T(8,128)(2,1)S(1)}, u32[]{:S(2)}, u32[]{:S(2)}) %all-to-all-start.2) | async-done | bytes 196640 | tf_op jit(solution)/shard_map/all_to_all | solution.py:21
  108.2 0.8 fusion.84
  109.1 0.7 fusion.10
  109.8 0.7 pad_maximum_fusion.1
  110.5 0.7 pad_maximum_fusion
  (126 shorter events, 9.4 us)
Async XLA Ops:
  0.6 27.3 %copy-start = (bf16[1024,1024]{1,0:T(8,128)(2,1)S(1)}, bf16[1024,1024]{1,0:T(8,128)(2,1)}, u32[]{:S(2)}) copy-start(bf16[1024,1024]{1,0:T(8,128)(2,1)} %param.14) | copy-start | bytes 6291460
  6.7 19.8 %collective-permute-start = (f32[9,1,1,1024]{3,2,1,0:T(1,128)S(1)}, f32[9,1,1,1024]{3,2,1,0:T(1,128)S(1)}, u32[]{:S(2)}, u32[]{:S(2)}) collective-permute-start(f32[9,1,1,1024]{3,2,1,0:T(1,128)S(1)} %constant_dynamic-update-slice_fusion), channel_id=1, source_target_pairs={{0,1},{1,2},{2,3},{3,4},{4,5},{5,6},{6,7},{7,8},{8,9},{9,10},{10,1... | collective-permute-start | bytes 110600 | tf_op jit(solution)/shard_map/ppermute | solution.py:124
  33.1 25.2 %all-to-all-start = ((bf16[64,16,128]{2,1,0:T(8,128)(2,1)}), bf16[64,16,128]{2,1,0:T(8,128)(2,1)S(1)}, u32[]{:S(2)}, u32[]{:S(2)}) async-start(bf16[64,16,128]{2,1,0:T(8,128)(2,1)} %copy.35), calls=%async_computation | async-start | bytes 524288 | tf_op jit(solution)/shard_map/all_to_all | solution.py:21
  58.6 1.2 %copy-start.4 = (f32[1024]{0:T(1024)S(1)}, f32[1024]{0:T(1024)}, u32[]{:S(2)}) copy-start(f32[1024]{0:T(1024)} %param.16) | copy-start | bytes 12292
  62.5 21.5 %copy-start.1 = (f32[1,16,1024]{2,1,0:T(8,128)S(1)}, f32[1,16,1024]{2,1,0:T(8,128)}, u32[]{:S(2)}) copy-start(f32[1,16,1024]{2,1,0:T(8,128)} %param.12) | copy-start | bytes 196612
  86.7 5.6 %copy-start.2 = (bf16[2,3,1,16,1024]{4,3,2,1,0:T(8,128)(2,1)S(1)}, bf16[2,3,1,16,1024]{4,3,2,1,0:T(8,128)(2,1)}, u32[]{:S(2)}) copy-start(bf16[2,3,1,16,1024]{4,3,2,1,0:T(8,128)(2,1)} %param.11) | copy-start | bytes 589828
  87.7 20.5 %all-to-all-start.2 = ((bf16[64,16,96]{2,1,0:T(8,128)(2,1)}), bf16[64,16,96]{2,1,0:T(8,128)(2,1)S(1)}, u32[]{:S(2)}, u32[]{:S(2)}) async-start(bf16[64,16,96]{2,1,0:T(8,128)(2,1)} %copy.53), calls=%async_computation.2 | async-start | bytes 524288 | tf_op jit(solution)/shard_map/all_to_all | solution.py:21
  92.4 16.7 %copy-start.3 = (s32[1,16,1024]{2,1,0:T(8,128)S(1)}, s32[1,16,1024]{2,1,0:T(8,128)}, u32[]{:S(2)}) copy-start(s32[1,16,1024]{2,1,0:T(8,128)} %param.13) | copy-start | bytes 196612

commit v14 on v3

--- a/solution.py
+++ b/solution.py
@@ -177,14 +177,15 @@
             joined = pieces[0] + pieces[1]
             inverse_cols = joined.T.reshape(eps_planes, strip, line_cells)
             turned = turned[:, : comps * strip]
-        solved = solve_turned(turned, inverse_held if instant == 0 else inverse)
-        solved = solved.reshape(6, planes, strip, line_cells)
-        fields = tuple(solved[i] for i in range(6))
+        held = inverse_held if instant == 0 else inverse
+        half = 3 * planes * strip
+        solved_e = solve_turned(turned[:, :half], held).reshape(3, planes, strip, line_cells)
+        solved_h = solve_turned(turned[:, half:], held).reshape(3, planes, strip, line_cells)
+        fields = tuple(solved_e[i] for i in range(3)) + tuple(solved_h[i] for i in range(3))
         snapshot = fwd_e[instant].astype(jnp.float32)
         intersection = fields[0] * snapshot[0] + fields[1] * snapshot[1] + fields[2] * snapshot[2]
         gradient = gradient + mask_weight * intersection * (inverse_cols * inverse_cols)
-    out = jnp.stack(fields)
-    return (out[:3], out[3:], gradient)
+    return (solved_e, solved_h, gradient)
 
 
 def solution(mesh):

time: 112 us -> 114 us (1.018)
  matrix products: 3.48 us -> 6.12 us
    dot_general x3 -> x5, matrix products: 2.71 us -> 5.35 us  [solve_turned(): lax.dot_general(turned, inverse, (((0,), (1,)), ((), ())), preferred_elem...]
where the time goes in v14:
time: 114 us; the launch traced here: 113 us
  waiting for transfers between devices  45.4 us (40%)
  blocking collectives  20.4 us (18%)
  starting transfers between devices  19.7 us (17%)
  local copies, waits for them, and re-layouts  12.7 us (11%)
  matrix products  6.12 us (5%)
  other arithmetic  5.84 us (5%)
  between operations  3.03 us (3%)
    all_to_all x2, waiting for transfers between devices, turn_rows(): parts = lax.all_to_all(parts, 'line', 0, 0, tiled=True)  32.5 us
    all_to_all x1, blocking collectives, turn_rows(): parts = lax.all_to_all(parts, 'line', 0, 0, tiled=True)  20.4 us
    ppermute x1, waiting for transfers between devices, per_device(): message = lax.ppermute(message, 'line', ring)  12.9 us
    all_to_all x2, starting transfers between devices, turn_rows(): parts = lax.all_to_all(parts, 'line', 0, 0, tiled=True)  12.8 us
    ppermute x1, starting transfers between devices, per_device(): message = lax.ppermute(message, 'line', ring)  6.83 us
    dot_general x5, matrix products, solve_turned(): lax.dot_general(turned, inverse, (((0,), (1,)), ((), ())), preferred_elem...  5.35 us
    another operation x25, local copies, waits for them, and re-layouts, per_device(): stacked = jnp.stack(fields).reshape(comps, strip, line_cells)  4.22 us
  transfers between devices with their start and end apart: 3, of which 3 were waited for; matrix products, arithmetic and copies ran while one was open for 0% of the time, Pallas kernels for 0%

profile of v14, /device:TPU:8, one launch (start us, length us, event | category | flops | bytes accessed | tf_op | source)
XLA Modules:
  0.0 113.2 jit_solution(10461520574874924736)
XLA Ops:
  2.2 0.9 slice_bitcast_fusion.21
  3.1 0.9 slice_bitcast_fusion.19
  4.0 0.9 broadcast_multiply_fusion
  4.9 0.8 dynamic-slice_multiply_fusion
  5.6 0.9 bitcast_add_fusion
  6.7 6.8 %collective-permute-start = (f32[9,1,1,1024]{3,2,1,0:T(1,128)S(1)}, f32[9,1,1,1024]{3,2,1,0:T(1,128)S(1)}, u32[]{:S(2)}, u32[]{:S(2)}) collective-permute-start(f32[9,1,1,1024]{3,2,1,0:T(1,128)S(1)} %constant_dynamic-update-slice_fusion), channel_id=1, source_target_pairs={{0,1},{1,2},{2,3},{3,4},{4,5},{5,6},{6,7},{7,8},{8,9},{9,10},{10,1... | collective-permute-start | bytes 110600 | tf_op jit(solution)/shard_map/ppermute | solution.py:124
  13.6 12.9 %collective-permute-done = f32[9,1,1,1024]{3,2,1,0:T(1,128)S(1)} collective-permute-done((f32[9,1,1,1024]{3,2,1,0:T(1,128)S(1)}, f32[9,1,1,1024]{3,2,1,0:T(1,128)S(1)}, u32[]{:S(2)}, u32[]{:S(2)}) %collective-permute-start) | collective-permute-done | bytes 36896 | tf_op jit(solution)/shard_map/ppermute | solution.py:124
  26.5 1.1 fusion.37
  27.9 0.8 fusion.86
  32.1 1.0 copy.41
  33.1 8.2 %all-to-all-start = ((bf16[64,16,128]{2,1,0:T(8,128)(2,1)}), bf16[64,16,128]{2,1,0:T(8,128)(2,1)S(1)}, u32[]{:S(2)}, u32[]{:S(2)}) async-start(bf16[64,16,128]{2,1,0:T(8,128)(2,1)} %copy.41), calls=%async_computation | async-start | bytes 524288 | tf_op jit(solution)/shard_map/all_to_all | solution.py:21
  41.6 16.7 %all-to-all-done = bf16[64,16,128]{2,1,0:T(8,128)(2,1)S(1)} async-done(((bf16[64,16,128]{2,1,0:T(8,128)(2,1)}), bf16[64,16,128]{2,1,0:T(8,128)(2,1)S(1)}, u32[]{:S(2)}, u32[]{:S(2)}) %all-to-all-start) | async-done | bytes 262176 | tf_op jit(solution)/shard_map/all_to_all | solution.py:21
  58.5 1.1 fusion.1
  59.6 1.2 %fusion = f32[48,1024]{1,0:T(8,128)S(1)} fusion(bf16[1024,1023]{1,0:T(8,128)(2,1)S(1)} %bitcast.348, bf16[1024,1]{1,0:T(8,128)(2,1)S(1)} %slice.345, bf16[1024,128]{1,0:T(8,128)(2,1)S(1)} %bitcast.353), kind=kOutput, calls=%fused_computation.1 | convolution fusion | flops 104857600 | bytes 2555904 | tf_op jit(solution)/shard_map/dot_general | solution.py:26
  63.9 0.3 copy.51
  64.2 20.4 %all_to_all.15 = bf16[64,16,96]{2,1,0:T(8,128)(2,1)S(1)} all-to-all(bf16[64,16,96]{2,1,0:T(8,128)(2,1)S(1)} %copy.51), channel_id=1, replica_groups=mesh['exc'=8,'line'=64] {'line'}, dimensions={0} | all-to-all | bytes 393216 | tf_op jit(solution)/shard_map/all_to_all | solution.py:21
  84.6 0.8 fusion.87
  85.6 0.7 add_convert_fusion.1
  88.7 0.9 copy.59
  89.6 4.6 %all-to-all-start.2 = ((bf16[64,16,96]{2,1,0:T(8,128)(2,1)}), bf16[64,16,96]{2,1,0:T(8,128)(2,1)S(1)}, u32[]{:S(2)}, u32[]{:S(2)}) async-start(bf16[64,16,96]{2,1,0:T(8,128)(2,1)} %copy.59), calls=%async_computation.2 | async-start | bytes 524288 | tf_op jit(solution)/shard_map/all_to_all | solution.py:21
  94.3 15.8 %all-to-all-done.2 = bf16[64,16,96]{2,1,0:T(8,128)(2,1)S(1)} async-done(((bf16[64,16,96]{2,1,0:T(8,128)(2,1)}), bf16[64,16,96]{2,1,0:T(8,128)(2,1)S(1)}, u32[]{:S(2)}, u32[]{:S(2)}) %all-to-all-start.2) | async-done | bytes 196640 | tf_op jit(solution)/shard_map/all_to_all | solution.py:21
  110.1 0.7 fusion.4
  110.9 1.6 %fusion.2 = f32[48,1024]{1,0:T(8,128)} fusion(bf16[1024,1024]{1,0:T(8,128)(2,1)S(1)} %copy-done, bf16[1024,96]{1,0:T(8,128)(2,1)S(1)} %bitcast.350), kind=kOutput, calls=%fused_computation.3 | convolution fusion | flops 100663296 | bytes 2490368 | tf_op jit(solution)/shard_map/dot_general | solution.py:26
  112.5 0.7 fusion.14
  (129 shorter events, 9.6 us)
Async XLA Ops:
  0.6 27.2 %copy-start = (bf16[1024,1024]{1,0:T(8,128)(2,1)S(1)}, bf16[1024,1024]{1,0:T(8,128)(2,1)}, u32[]{:S(2)}) copy-start(bf16[1024,1024]{1,0:T(8,128)(2,1)} %param.14) | copy-start | bytes 6291460
  6.7 19.8 %collective-permute-start = (f32[9,1,1,1024]{3,2,1,0:T(1,128)S(1)}, f32[9,1,1,1024]{3,2,1,0:T(1,128)S(1)}, u32[]{:S(2)}, u32[]{:S(2)}) collective-permute-start(f32[9,1,1,1024]{3,2,1,0:T(1,128)S(1)} %constant_dynamic-update-slice_fusion), channel_id=1, source_target_pairs={{0,1},{1,2},{2,3},{3,4},{4,5},{5,6},{6,7},{7,8},{8,9},{9,10},{10,1... | collective-permute-start | bytes 110600 | tf_op jit(solution)/shard_map/ppermute | solution.py:124
  33.1 25.2 %all-to-all-start = ((bf16[64,16,128]{2,1,0:T(8,128)(2,1)}), bf16[64,16,128]{2,1,0:T(8,128)(2,1)S(1)}, u32[]{:S(2)}, u32[]{:S(2)}) async-start(bf16[64,16,128]{2,1,0:T(8,128)(2,1)} %copy.41), calls=%async_computation | async-start | bytes 524288 | tf_op jit(solution)/shard_map/all_to_all | solution.py:21
  59.6 1.6 %copy-start.6 = (f32[1024]{0:T(1024)S(1)}, f32[1024]{0:T(1024)}, u32[]{:S(2)}) copy-start(f32[1024]{0:T(1024)} %param.16) | copy-start | bytes 12292
  63.9 21.5 %copy-start.1 = (f32[1,16,1024]{2,1,0:T(8,128)S(1)}, f32[1,16,1024]{2,1,0:T(8,128)}, u32[]{:S(2)}) copy-start(f32[1,16,1024]{2,1,0:T(8,128)} %param.12) | copy-start | bytes 196612
  86.2 1.6 %copy-start.4 = (bf16[1,16,1024]{2,1,0:T(8,128)(2,1)S(1)}, bf16[1,16,1024]{2,1,0:T(8,128)(2,1)}, u32[]{:S(2)}) copy-start(bf16[1,16,1024]{2,1,0:T(8,128)(2,1)} %get-tuple-element.35) | copy-start | bytes 98308
  87.7 6.6 %copy-start.3 = (bf16[2,3,1,16,1024]{4,3,2,1,0:T(8,128)(2,1)S(1)}, bf16[2,3,1,16,1024]{4,3,2,1,0:T(8,128)(2,1)}, u32[]{:S(2)}) copy-start(bf16[2,3,1,16,1024]{4,3,2,1,0:T(8,128)(2,1)} %param.11) | copy-start | bytes 589828
  89.6 20.5 %all-to-all-start.2 = ((bf16[64,16,96]{2,1,0:T(8,128)(2,1)}), bf16[64,16,96]{2,1,0:T(8,128)(2,1)S(1)}, u32[]{:S(2)}, u32[]{:S(2)}) async-start(bf16[64,16,96]{2,1,0:T(8,128)(2,1)} %copy.59), calls=%async_computation.2 | async-start | bytes 524288 | tf_op jit(solution)/shard_map/all_to_all | solution.py:21
  110.1 2.4 %copy-start.5 = (s32[1,16,1024]{2,1,0:T(8,128)S(1)}, s32[1,16,1024]{2,1,0:T(8,128)}, u32[]{:S(2)}) copy-start(s32[1,16,1024]{2,1,0:T(8,128)} %param.13) | copy-start | bytes 196612
  110.9 2.3 %copy-start.2 = (f32[48,1024]{1,0:T(8,128)}, f32[48,1024]{1,0:T(8,128)S(1)}, u32[]{:S(2)}) copy-start(f32[48,1024]{1,0:T(8,128)S(1)} %fusion.4) | copy-start | bytes 589828
